TPU v7x, 32 devices: a whole 2x2x4 slice. The times are simulated.
32 devices in a mesh: ep: 16 (over z, x, core), dp: 2 (over y).
Axes of the slice: x: 2, y: 2, z: 4, core: 2. Of those that a mesh axis runs over, the one named last changes fastest.
Arguments:
- tokens: bfloat16 [1024, 4096], P('ep', 'dp'), may hold values from -6 to 6
- expert_ids: int32 [1024, 8], P('ep'), may hold values from 0 to 15, all different within a row
- gate_logits: float32 [1024, 8], P('ep'), may hold values from -6 to 6
- placement: int32 [8], replicated, may hold values from 0 to 15, as said below
- split_rows: int32 [8], replicated, may hold values from 0 to 32
- gate_up_weight: bfloat16 [16, 4096, 2, 1024], P('ep', None, None, 'dp'), may hold values from -0.09375 to 0.09375
- down_weight: bfloat16 [16, 1024, 4096], P('ep', None, 'dp'), may hold values from -0.1875 to 0.1875
- spare_gate_up: bfloat16 [16, 4096, 2, 512], P('ep', None, None, 'dp'), may hold values from -0.09375 to 0.09375
- spare_down: bfloat16 [16, 512, 4096], P('ep', None, 'dp'), may hold values from -0.1875 to 0.1875
Outputs:
- mixed: bfloat16 [1024, 4096], P('ep', 'dp')
Inputs may be any that keep to these rules, and one draw needn't show every extreme that they name: `expert_ids`: each token names 8 different experts. `placement`: 8 different experts.
All inputs are finite; a program needn't handle non-finite values.
Results may differ from a plain program's by a relative error of at most 0.0058.
Values may be sent and summed in bfloat16 or wider, within the bound.
No kernel may reach another device: no remote copies, remote signals or barrier semaphores. Data moves between devices by JAX's collectives and lax.ppermute only.
A program may use at most 64 MiB of HBM per device.

v0:
```python
import jax
import jax.numpy as jnp
from jax import lax
from jax.sharding import PartitionSpec as P


def rank_pairs(chosen_ids, experts):
    per_group = chosen_ids.shape[0]
    which = (chosen_ids[:, None] == jnp.arange(experts, dtype=jnp.int32)[None, :]).astype(
        jnp.float32
    )
    ordinal = jnp.arange(per_group, dtype=jnp.int32)
    earlier = (ordinal[None, :] < ordinal[:, None]).astype(jnp.float32)
    before = jnp.dot(
        earlier, which, preferred_element_type=jnp.float32, precision=lax.Precision.HIGHEST
    )
    return jnp.sum(before * which, axis=1).astype(jnp.int32)


def gate_up(row_block, weight):
    gate_both = jnp.einsum("...d,djf->...jf", row_block, weight, preferred_element_type=jnp.float32)
    return (jax.nn.silu(gate_both[..., 0, :]) * gate_both[..., 1, :]).astype(jnp.bfloat16)


def per_device(
    tokens,
    expert_ids,
    gate_logits,
    placement,
    split_rows,
    gate_up_weight,
    down_weight,
    spare_gate_up,
    spare_down,
):
    ep_count = lax.axis_size("ep")
    dp_count = lax.axis_size("dp")
    whole_rows = lax.all_gather(tokens, "dp", axis=1, tiled=True)
    group_tokens, d_model = whole_rows.shape
    top_count = expert_ids.shape[1]
    spares = placement.shape[0]
    capacity = group_tokens * top_count // ep_count
    per_group = group_tokens * top_count
    chosen_ids = expert_ids.reshape(per_group)
    pair_rank = rank_pairs(chosen_ids, ep_count)
    is_match = chosen_ids[:, None] == placement[None, :]
    is_hot = jnp.any(is_match, axis=1)
    copy_index = jnp.sum(
        jnp.where(is_match, jnp.arange(spares, dtype=jnp.int32)[None, :], 0), axis=1
    )
    split_here = jnp.sum(jnp.where(is_match, split_rows[None, :], 0), axis=1)
    to_copy = is_hot & (pair_rank >= split_here)
    slot_of = jnp.where(to_copy, ep_count + copy_index, chosen_ids)
    position = jnp.where(to_copy, pair_rank - split_here, pair_rank)
    kept_mask = position < capacity
    flat_slot = slot_of * capacity + position
    slot_total = (ep_count + spares) * capacity
    row_table = jnp.full((slot_total,), group_tokens, jnp.int32)
    row_table = row_table.at[jnp.where(kept_mask, flat_slot, slot_total)].set(
        jnp.arange(per_group, dtype=jnp.int32) // top_count, mode="drop"
    )
    padded = jnp.concatenate([whole_rows, jnp.zeros((1, d_model), whole_rows.dtype)], axis=0)
    send_all = jnp.take(padded, row_table, axis=0)
    home_send = send_all[: ep_count * capacity].reshape(ep_count, capacity, d_model)
    spare_table = send_all[ep_count * capacity :].reshape(spares, capacity, d_model)
    own_gu = gate_up_weight[0]
    own_dn = down_weight[0]
    extra_gu = spare_gate_up[0]
    extra_dn = spare_down[0]
    home_rows, spare_rows = (
        lax.all_to_all(home_send, "ep", split_axis=0, concat_axis=0, tiled=True),
        lax.all_to_all(
            jnp.repeat(spare_table, 2, axis=0), "ep", split_axis=0, concat_axis=0, tiled=True
        ),
    )
    home_hidden = gate_up(home_rows, own_gu)
    spare_hidden = gate_up(spare_rows, extra_gu)
    unit_piece = spare_hidden.shape[2]
    stacked = jnp.concatenate(
        [home_hidden.reshape(ep_count, capacity, 2, unit_piece), spare_hidden[:, :, None, :]],
        axis=2,
    )
    columns = own_dn.shape[1]
    home_view = jnp.transpose(
        own_dn.reshape(dp_count, 2, unit_piece, columns), (1, 0, 2, 3)
    ).reshape(2, dp_count * unit_piece, columns)
    piece = lax.all_gather(stacked, "dp", axis=3, tiled=True)
    home_term = jnp.einsum(
        "gchf,hfe->gce", piece[:, :, 0:2], home_view, preferred_element_type=jnp.float32
    )
    spare_term = jnp.einsum(
        "gcf,fe->gce", piece[:, :, 2], extra_dn, preferred_element_type=jnp.float32
    )
    home_out = home_term.astype(jnp.bfloat16)
    home_back = lax.all_to_all(home_out, "ep", split_axis=0, concat_axis=0, tiled=True)
    halves_back = lax.all_to_all(spare_term, "ep", split_axis=0, concat_axis=0, tiled=True)
    spare_back = jnp.sum(halves_back.reshape(spares, 2, capacity, columns), axis=1).astype(
        jnp.bfloat16
    )
    table = jnp.concatenate(
        [
            home_back.reshape(ep_count * capacity, columns),
            spare_back.reshape(spares * capacity, columns),
        ],
        axis=0,
    )
    chosen = jnp.take(table, jnp.where(kept_mask, flat_slot, 0), axis=0).reshape(
        group_tokens, top_count, columns
    )
    gate_score = jax.nn.sigmoid(gate_logits)
    gate_weight = 2.5 * gate_score / jnp.sum(gate_score, axis=1, keepdims=True)
    kept_weight = jnp.where(kept_mask.reshape(group_tokens, top_count), gate_weight, 0.0)
    mixed = jnp.sum(kept_weight[:, :, None] * chosen.astype(jnp.float32), axis=1)
    return mixed.astype(jnp.bfloat16)


def solution(mesh):
    return jax.shard_map(
        per_device,
        mesh=mesh,
        in_specs=(
            P("ep", "dp"),
            P("ep", None),
            P("ep", None),
            P(),
            P(),
            P("ep", None, None, "dp"),
            P("ep", None, "dp"),
            P("ep", None, None, "dp"),
            P("ep", None, "dp"),
        ),
        out_specs=P("ep", "dp"),
        check_vma=False,
    )
```

profile of v0, /device:TPU:0, one launch (start us, length us, event | category | flops | bytes accessed | tf_op | source)
XLA Modules:
  0.0 441.4 jit_solution(16183501435783012586)
XLA Ops:
  6.5 0.0 copy-start
  6.5 0.9 copy.28
  7.5 0.1 eq.28
  7.5 0.1 reshape.164
  7.6 0.3 fusion.10
  7.9 0.7 compare_reduce_fusion
  8.7 0.8 fusion.14
  9.5 2.4 scatter_custom_fusion
  12.0 10.2 %all_gather.6 = bf16[64,4096]{1,0:T(8,128)(2,1)S(1)} all-gather(bf16[64,2048]{1,0:T(8,128)(2,1)} %param.9), channel_id=1, replica_groups=mesh['ep'=16,'dp'=2] {'dp'}, dimensions={1}, use_global_device_ids=true | all-gather | bytes 786432 | tf_op jit(solution)/shard_map/all_gather | solution.py:38
  22.2 5.7 %gather_fusion = bf16[768,4096]{1,0:T(8,128)(2,1)} fusion(bf16[65,4096]{1,0:T(8,128)(2,1)S(1)} %concatenate.9, s32[1024]{0:T(1024)S(1)} %pad_clamp_fusion.1), kind=kCustom, calls=%fused_computation | custom fusion | bytes 12585984 | tf_op jit(solution)/shard_map/jit(_take)/gather | solution.py:63
  28.0 3.4 broadcast_select_fusion
  31.4 0.0 copy-start.1
  31.4 2.4 slice.36
  33.8 1.6 copy-done.1
  35.4 6.1 %all-to-all-start = ((bf16[16,32,4096]{2,1,0:T(8,128)(2,1)}), bf16[16,32,4096]{2,1,0:T(8,128)(2,1)}, u32[]{:S(2)}, u32[]{:S(2)}) async-start(bf16[16,32,4096]{2,1,0:T(8,128)(2,1)} %bitcast.61), calls=%async_computation | async-start | bytes 8388608 | tf_op jit(solution)/shard_map/all_to_all | solution.py:71
  41.5 3.2 slice.39
  44.7 74.5 %all-to-all-done = bf16[16,32,4096]{2,1,0:T(8,128)(2,1)} async-done(((bf16[16,32,4096]{2,1,0:T(8,128)(2,1)}), bf16[16,32,4096]{2,1,0:T(8,128)(2,1)}, u32[]{:S(2)}, u32[]{:S(2)}) %all-to-all-start) | async-done | bytes 4194336 | tf_op jit(solution)/shard_map/all_to_all | solution.py:71
  119.2 4.0 broadcast_in_dim.82
  123.2 19.7 %all-to-all-start.1 = ((bf16[16,32,4096]{2,1,0:T(8,128)(2,1)}), bf16[16,32,4096]{2,1,0:T(8,128)(2,1)}, u32[]{:S(2)}, u32[]{:S(2)}) async-start(bf16[16,32,4096]{2,1,0:T(8,128)(2,1)} %bitcast.60), calls=%async_computation.1 | async-start | bytes 8388608 | tf_op jit(solution)/shard_map/all_to_all | solution.py:72
  142.9 0.0 all-gather.2.cloned.1.call-start
  143.0 8.3 %fusion = f32[16,32,2,512]{3,1,2,0:T(8,128)S(1)} fusion(bf16[4096,2,512]{2,1,0:T(2,128)(2,1)} %bitcast.73, bf16[16,32,4096]{2,1,0:T(8,128)(2,1)} %all-to-all-done), kind=kOutput, calls=%fused_computation.3 | convolution fusion | flops 4294967296 | bytes 14680064 | tf_op jit(solution)/shard_map/...d,djf->...jf/dot_general | solution.py:21
  151.2 1.6 fusion.23
  152.8 1.9 squeeze.21
  154.7 2.9 squeeze.22
  157.6 63.0 %all-to-all-done.1 = bf16[16,32,4096]{2,1,0:T(8,128)(2,1)} async-done(((bf16[16,32,4096]{2,1,0:T(8,128)(2,1)}), bf16[16,32,4096]{2,1,0:T(8,128)(2,1)}, u32[]{:S(2)}, u32[]{:S(2)}) %all-to-all-start.1) | async-done | bytes 4194336 | tf_op jit(solution)/shard_map/all_to_all | solution.py:72
  220.6 0.0 copy-start.2
  220.6 5.9 %fusion.3 = f32[16,32,2,256]{3,1,2,0:T(8,128)S(1)} fusion(bf16[16,32,4096]{2,1,0:T(8,128)(2,1)} %all-to-all-done.1, bf16[4096,2,256]{2,1,0:T(2,128)(2,1)} %bitcast.74), kind=kOutput, calls=%fused_computation.7 | convolution fusion | flops 2147483648 | bytes 9437184 | tf_op jit(solution)/shard_map/...d,djf->...jf/dot_general | solution.py:21
  226.5 0.2 fusion.12
  226.6 0.0 copy-done.2
  226.6 0.3 fusion.11
  226.9 1.0 pad_maximum_fusion.1
  227.9 0.0 all-gather.2.cloned.1.call-update
  227.9 42.3 %all-gather.2.cloned.1.call-done = bf16[16,32,3,512]{3,1,2,0:T(8,128)(2,1)} async-done(((bf16[16,32,3,256]{3,1,2,0:T(8,128)(2,1)}), bf16[16,32,3,512]{3,1,2,0:T(8,128)(2,1)}) %all-gather.2.cloned.1.call-update) | async-done | bytes 1572880 | tf_op jit(solution)/shard_map/all_gather | solution.py:87
  270.2 0.0 copy-done
  270.2 4.3 fusion.8
  274.5 5.7 %all-to-all-start.3 = ((f32[16,32,2048]{2,1,0:T(8,128)}), f32[16,32,2048]{2,1,0:T(8,128)}, u32[]{:S(2)}, u32[]{:S(2)}) async-start(f32[16,32,2048]{2,1,0:T(8,128)} %fusion.8), calls=%async_computation.3 | async-start | bytes 8388608 | tf_op jit(solution)/shard_map/all_to_all | solution.py:96
  280.2 0.0 copy-start.4
  280.2 2.6 copy.37
  282.8 0.0 copy-done.4
  282.9 3.7 bitcast_convert_fusion
  286.6 0.0 copy-start.3
  286.6 71.3 %all-to-all-done.3 = f32[16,32,2048]{2,1,0:T(8,128)} async-done(((f32[16,32,2048]{2,1,0:T(8,128)}), f32[16,32,2048]{2,1,0:T(8,128)}, u32[]{:S(2)}, u32[]{:S(2)}) %all-to-all-start.3) | async-done | bytes 4194336 | tf_op jit(solution)/shard_map/all_to_all | solution.py:96
  357.9 19.7 %all-to-all-start.2 = ((bf16[16,32,2048]{2,1,0:T(8,128)(2,1)}), bf16[16,32,2048]{2,1,0:T(8,128)(2,1)}, u32[]{:S(2)}, u32[]{:S(2)}) async-start(bf16[16,32,2048]{2,1,0:T(8,128)(2,1)} %bitcast_convert_fusion), calls=%async_computation.2 | async-start | bytes 4194304 | tf_op jit(solution)/shard_map/all_to_all | solution.py:95
  377.6 0.1 reduce_sum.60
  377.6 0.1 reduce_or.14
  377.7 0.1 add.105
  377.8 0.1 convert_element_type.51
  377.9 0.0 copy-done.3
  377.9 0.1 copy.29
  378.0 0.1 fusion.17
  378.1 0.1 divide_select_fusion
  378.3 2.7 bitcast_reduce_fusion
  381.0 37.7 %all-to-all-done.2 = bf16[16,32,2048]{2,1,0:T(8,128)(2,1)} async-done(((bf16[16,32,2048]{2,1,0:T(8,128)(2,1)}), bf16[16,32,2048]{2,1,0:T(8,128)(2,1)}, u32[]{:S(2)}, u32[]{:S(2)}) %all-to-all-start.2) | async-done | bytes 2097184 | tf_op jit(solution)/shard_map/all_to_all | solution.py:95
  418.7 3.6 pad_maximum_fusion
  422.4 7.5 %gather_fusion.1 = bf16[512,2048]{1,0:T(8,128)(2,1)} fusion(bf16[768,2048]{1,0:T(8,128)(2,1)} %pad_maximum_fusion, s32[1024]{0:T(1024)S(1)} %pad_clamp_fusion), kind=kCustom, calls=%fused_computation.1 | custom fusion | bytes 4196352 | tf_op jit(solution)/shard_map/jit(_take)/gather | solution.py:107
  429.9 4.7 %multiply_reduce_fusion = bf16[64,2048]{1,0:T(8,128)(2,1)} fusion(bf16[512,2048]{1,0:T(8,128)(2,1)} %gather_fusion.1, f32[64,8]{1,0:T(8,128)S(1)} %divide_select_fusion, pred[64,8]{1,0:T(8,128)(4,1)S(1)} %compare_and_fusion), kind=kLoop, calls=%fused_computation.14 | loop fusion | flops 4063232 | bytes 2361856 | tf_op jit(solution)/shard_map/reduce_sum | solution.py:113
  (11 shorter events, 0.1 us)
Async XLA Ops:
  6.5 263.7 %copy-start = (bf16[1,512,2048]{2,1,0:T(8,128)(2,1)S(1)}, bf16[1,512,2048]{2,1,0:T(8,128)(2,1)}, u32[]{:S(2)}) copy-start(bf16[1,512,2048]{2,1,0:T(8,128)(2,1)} %param.17) | copy-start | bytes 6291460
  31.4 4.0 copy-start.1
  35.4 83.8 %all-to-all-start = ((bf16[16,32,4096]{2,1,0:T(8,128)(2,1)}), bf16[16,32,4096]{2,1,0:T(8,128)(2,1)}, u32[]{:S(2)}, u32[]{:S(2)}) async-start(bf16[16,32,4096]{2,1,0:T(8,128)(2,1)} %bitcast.61), calls=%async_computation | async-start | bytes 8388608 | tf_op jit(solution)/shard_map/all_to_all | solution.py:71
  123.2 97.4 %all-to-all-start.1 = ((bf16[16,32,4096]{2,1,0:T(8,128)(2,1)}), bf16[16,32,4096]{2,1,0:T(8,128)(2,1)}, u32[]{:S(2)}, u32[]{:S(2)}) async-start(bf16[16,32,4096]{2,1,0:T(8,128)(2,1)} %bitcast.60), calls=%async_computation.1 | async-start | bytes 8388608 | tf_op jit(solution)/shard_map/all_to_all | solution.py:72
  142.9 127.3 %all-gather.2.cloned.1.call-start = ((), (), s32[]{:S(2)}) async-start(), calls=%async_computation.4 | async-start | bytes 2359296 | tf_op jit(solution)/shard_map/all_gather | solution.py:87
  220.6 6.0 %copy-start.2 = (f32[16,32,2,256]{3,2,1,0:T(2,128)S(1)}, f32[16,32,2,256]{3,2,1,0:T(2,128)}, u32[]{:S(2)}) copy-start(f32[16,32,2,256]{3,2,1,0:T(2,128)} %squeeze.22) | copy-start | bytes 3145732
  274.5 83.3 %all-to-all-start.3 = ((f32[16,32,2048]{2,1,0:T(8,128)}), f32[16,32,2048]{2,1,0:T(8,128)}, u32[]{:S(2)}, u32[]{:S(2)}) async-start(f32[16,32,2048]{2,1,0:T(8,128)} %fusion.8), calls=%async_computation.3 | async-start | bytes 8388608 | tf_op jit(solution)/shard_map/all_to_all | solution.py:96
  280.2 2.7 copy-start.4
  286.6 91.3 %copy-start.3 = (f32[64,8]{0,1:T(8,128)S(1)}, f32[64,8]{0,1:T(8,128)}, u32[]{:S(2)}) copy-start(f32[64,8]{0,1:T(8,128)} %param.11) | copy-start | bytes 6148
  357.9 60.9 %all-to-all-start.2 = ((bf16[16,32,2048]{2,1,0:T(8,128)(2,1)}), bf16[16,32,2048]{2,1,0:T(8,128)(2,1)}, u32[]{:S(2)}, u32[]{:S(2)}) async-start(bf16[16,32,2048]{2,1,0:T(8,128)(2,1)} %bitcast_convert_fusion), calls=%async_computation.2 | async-start | bytes 4194304 | tf_op jit(solution)/shard_map/all_to_all | solution.py:95
Sparse Core Ops, SparseCore 0:
  228.0 42.1 all-gather.1
where the time goes:
time: 448 us; the launch traced here: 441 us
  waiting for transfers between devices  289 us (65%)
  starting transfers between devices  51.2 us (11%)
  local copies, waits for them, and re-layouts  37.5 us (8%)
  matrix products  22.4 us (5%)
  other arithmetic  17.7 us (4%)
  between operations  13.6 us (3%)
  blocking collectives  10.2 us (2%)
    all_to_all x1, waiting for transfers between devices, per_device(): lax.all_to_all(home_send, 'ep', split_axis=0, concat_axis=0, tiled=True)  74.5 us
    all_to_all x1, waiting for transfers between devices, per_device(): lax.all_to_all(spare_term, 'ep', split_axis=0, concat_axis=0, tiled=True)  71.3 us
    all_to_all x1, waiting for transfers between devices, per_device(): lax.all_to_all(jnp.repeat(spare_table, 2, axis=0), 'ep', split_axis=0, co...  63 us
    all_gather x1, waiting for transfers between devices, per_device(): piece = lax.all_gather(stacked, 'dp', axis=3, tiled=True)  42.3 us
    all_to_all x1, waiting for transfers between devices, per_device(): lax.all_to_all(home_out, 'ep', split_axis=0, concat_axis=0, tiled=True)  37.7 us
    all_to_all x1, starting transfers between devices, per_device(): lax.all_to_all(home_out, 'ep', split_axis=0, concat_axis=0, tiled=True)  19.7 us
    all_to_all x1, starting transfers between devices, per_device(): lax.all_to_all(jnp.repeat(spare_table, 2, axis=0), 'ep', split_axis=0, co...  19.7 us
    dot_general x2, matrix products, gate_up(): jnp.einsum('...d,djf->...jf', row_block, weight, preferred_element_type=j...  14.1 us
  transfers between devices with their start and end apart: 5, of which 5 were waited for; matrix products, arithmetic and copies ran while one was open for 6% of the time, Pallas kernels for 0%

commit v1 on v0

v1 whole, which is shorter than its diff:
```python
import jax
import jax.numpy as jnp
from jax import lax
from jax.sharding import PartitionSpec as P


def gate_up(row_block, weight):
    gate_both = jnp.einsum("rd,djf->rjf", row_block, weight, preferred_element_type=jnp.float32)
    return (jax.nn.silu(gate_both[:, 0, :]) * gate_both[:, 1, :]).astype(jnp.bfloat16)


def slot_tables(ids, target, low, limit, capacity, top_count):
    groups, per_group = ids.shape
    hit = ids == target
    ordinal = jnp.arange(per_group, dtype=jnp.int32)
    earlier = (ordinal[None, :] < ordinal[:, None]).astype(jnp.bfloat16)
    rank = jnp.einsum(
        "pq,gq->gp", earlier, hit.astype(jnp.bfloat16), preferred_element_type=jnp.float32
    ).astype(jnp.int32)
    position = rank - low
    kept = hit & (position >= 0) & (position < limit)
    group_tokens = per_group // top_count
    token = jnp.arange(groups, dtype=jnp.int32)[:, None] * group_tokens + ordinal[None, :] // top_count
    slots = jnp.arange(capacity, dtype=jnp.int32)
    sel = kept[:, :, None] & (position[:, :, None] == slots[None, None, :])
    row_of_slot = jnp.sum(jnp.where(sel, token[:, :, None], 0), axis=1)
    flat = jnp.arange(groups, dtype=jnp.int32)[:, None] * capacity + position
    return row_of_slot.reshape(-1), kept, flat


def per_token(kept, flat, weight, group_tokens, top_count):
    groups = kept.shape[0]
    kept = kept.reshape(groups * group_tokens, top_count)
    flat = flat.reshape(groups * group_tokens, top_count)
    index = jnp.sum(jnp.where(kept, flat, 0), axis=1)
    scale = jnp.sum(jnp.where(kept, weight, 0.0), axis=1)
    return index, scale


def per_device(
    tokens,
    expert_ids,
    gate_logits,
    placement,
    split_rows,
    gate_up_weight,
    down_weight,
    spare_gate_up,
    spare_down,
):
    ep_count = lax.axis_size("ep")
    me = lax.axis_index("ep")
    group_tokens = tokens.shape[0]
    top_count = expert_ids.shape[1]
    spares = placement.shape[0]
    halves = spare_gate_up.shape[0] * ep_count // spares
    capacity = group_tokens * top_count // ep_count
    per_group = group_tokens * top_count

    whole_rows = lax.all_gather(tokens, "dp", axis=1, tiled=True)
    every_row = lax.all_gather(whole_rows, "ep", axis=0, tiled=True)
    every_id = lax.all_gather(expert_ids, "ep", axis=0, tiled=True)
    every_logit = lax.all_gather(gate_logits, "ep", axis=0, tiled=True)
    ids = every_id.reshape(ep_count, per_group)

    gate_score = jax.nn.sigmoid(every_logit)
    gate_weight = 2.5 * gate_score / jnp.sum(gate_score, axis=1, keepdims=True)

    is_match = placement == me
    home_limit = jnp.where(
        jnp.any(is_match), jnp.minimum(jnp.sum(jnp.where(is_match, split_rows, 0)), capacity), capacity
    )
    home_rows_of, home_kept, home_flat = slot_tables(
        ids, me, 0, home_limit, capacity, top_count
    )
    spare_index = me // halves
    spare_rows_of, spare_kept, spare_flat = slot_tables(
        ids, placement[spare_index], split_rows[spare_index], capacity, capacity, top_count
    )

    home_rows = jnp.take(every_row, home_rows_of, axis=0)
    spare_rows = jnp.take(every_row, spare_rows_of, axis=0)
    home_hidden = gate_up(home_rows, gate_up_weight[0])
    spare_hidden = gate_up(spare_rows, spare_gate_up[0])
    home_hidden = lax.all_gather(home_hidden, "dp", axis=1, tiled=True)
    spare_hidden = lax.all_gather(spare_hidden, "dp", axis=1, tiled=True)
    home_out = jnp.dot(home_hidden, down_weight[0], preferred_element_type=jnp.float32)
    home_out = home_out.astype(jnp.bfloat16).astype(jnp.float32)
    spare_out = jnp.dot(spare_hidden, spare_down[0], preferred_element_type=jnp.float32)

    home_at, home_scale = per_token(home_kept, home_flat, gate_weight, group_tokens, top_count)
    spare_at, spare_scale = per_token(spare_kept, spare_flat, gate_weight, group_tokens, top_count)
    partial = home_scale[:, None] * jnp.take(home_out, home_at, axis=0) + spare_scale[
        :, None
    ] * jnp.take(spare_out, spare_at, axis=0)
    mixed = lax.psum_scatter(partial, "ep", scatter_dimension=0, tiled=True)
    return mixed.astype(jnp.bfloat16)


def solution(mesh):
    return jax.shard_map(
        per_device,
        mesh=mesh,
        in_specs=(
            P("ep", "dp"),
            P("ep", None),
            P("ep", None),
            P(),
            P(),
            P("ep", None, None, "dp"),
            P("ep", None, "dp"),
            P("ep", None, None, "dp"),
            P("ep", None, "dp"),
        ),
        out_specs=P("ep", "dp"),
        check_vma=False,
    )
```

time: 448 us -> 300 us (0.67); the launches traced: 441 us -> 300 us
  waiting for transfers between devices: 289 us -> 124 us
  blocking collectives: 10.2 us -> 62.2 us
  starting transfers between devices: 51.2 us -> 0.27 us
  local copies, waits for them, and re-layouts: 37.5 us -> 54.2 us
    all_to_all x4 -> x0, waiting for transfers between devices: 246 us -> none  [the longest x1 74.5 us: per_device(): lax.all_to_all(home_send, 'ep', split_axis=0, concat_axis=0, tiled=True)]
    reduce_scatter x0 -> x1, waiting for transfers between devices: none -> 103 us  [per_device(): mixed = lax.psum_scatter(partial, 'ep', scatter_dimension=0, tiled=True)]
    all_to_all x4 -> x0, starting transfers between devices: 51.2 us -> none  [the longest x1 19.7 us: per_device(): lax.all_to_all(home_out, 'ep', split_axis=0, concat_axis=0, tiled=True)]
    all_gather x0 -> x3, blocking collectives: none -> 50.2 us  [the longest x1 22.4 us: per_device(): every_id = lax.all_gather(expert_ids, 'ep', axis=0, tiled=True)]
    gather x2 -> x4, local copies, waits for them, and re-layouts: 13.2 us -> 48.5 us  [the longest x1 13 us: per_device(): spare_rows = jnp.take(every_row, spare_rows_of, axis=0)]
    all_gather x1 -> x2, waiting for transfers between devices: 42.3 us -> 20.5 us  [the longest x1 20.5 us: per_device(): every_row = lax.all_gather(whole_rows, 'ep', axis=0, tiled=True)]
    add x1 -> x3, other arithmetic: 0.01 us -> 10.1 us  [the longest x1 9.91 us: per_device(): home_scale[:, None] * jnp.take(home_out, home_at, axis=0)]
    slice x3 -> x0, local copies, waits for them, and re-layouts: 7.14 us -> none  [the longest x1 3.16 us: per_device(): send_all[ep_count * capacity:].reshape(spares, capacity, d_model)]
  transfers between devices with their start and end apart: 5 -> 3, of which waited for: 5 -> 2; matrix products, arithmetic and copies ran while one was open for 6% -> 16% of each run, Pallas kernels for 0% -> 0%
where the time goes in v1:
time: 300 us
  waiting for transfers between devices  124 us (41%)
  blocking collectives  62.2 us (21%)
  local copies, waits for them, and re-layouts  54.2 us (18%)
  matrix products  25.4 us (8%)
  other arithmetic  19.1 us (6%)
  between operations  14.6 us (5%)
    reduce_scatter x1, waiting for transfers between devices, per_device(): mixed = lax.psum_scatter(partial, 'ep', scatter_dimension=0, tiled=True)  103 us
    all_gather x1, blocking collectives, per_device(): every_id = lax.all_gather(expert_ids, 'ep', axis=0, tiled=True)  22.4 us
    all_gather x1, waiting for transfers between devices, per_device(): every_row = lax.all_gather(whole_rows, 'ep', axis=0, tiled=True)  20.5 us
    all_gather x1, blocking collectives, per_device(): every_logit = lax.all_gather(gate_logits, 'ep', axis=0, tiled=True)  18.5 us
    dot_general x2, matrix products, gate_up(): jnp.einsum('rd,djf->rjf', row_block, weight, preferred_element_type=jnp.f...  14.2 us
    gather x1, local copies, waits for them, and re-layouts, per_device(): spare_rows = jnp.take(every_row, spare_rows_of, axis=0)  13 us
    gather x1, local copies, waits for them, and re-layouts, per_device(): home_rows = jnp.take(every_row, home_rows_of, axis=0)  13 us
    all_gather x1, blocking collectives, per_device(): whole_rows = lax.all_gather(tokens, 'dp', axis=1, tiled=True)  12 us
  transfers between devices with their start and end apart: 3, of which 2 were waited for; matrix products, arithmetic and copies ran while one was open for 16% of the time, Pallas kernels for 0%

profile of v1, /device:TPU:0, one launch (start us, length us, event | category | flops | bytes accessed | tf_op | source)
XLA Modules:
  0.0 299.5 jit_solution(7959396471671987635)
XLA Ops:
  6.5 0.0 copy-start
  6.5 0.0 all-gather.5.cloned.1.call-start
  6.5 12.0 %all_gather.20 = bf16[64,4096]{1,0:T(8,128)(2,1)} all-gather(bf16[64,2048]{1,0:T(8,128)(2,1)} %param.13), channel_id=1, replica_groups=mesh['ep'=16,'dp'=2] {'dp'}, dimensions={1}, use_global_device_ids=true | all-gather | bytes 786432 | tf_op jit(solution)/shard_map/all_gather | solution.py:60
  18.6 0.0 all-gather.5.cloned.1.call-update
  18.6 0.0 all-gather.7.cloned.1.call-start
  18.6 1.2 dynamic_slice.6
  19.9 1.3 dynamic_slice.7
  21.2 22.4 %all-gather = s32[16,64,8]{1,2,0:T(8,128)S(1)} all-gather(s32[1,64,8]{1,2,0:T(8,128)} %bitcast.64), channel_id=1, replica_groups=mesh['ep'=16,'dp'=2] {'ep'}, dimensions={0}, use_global_device_ids=true | all-gather | bytes 34816 | tf_op jit(solution)/shard_map/all_gather | solution.py:62
  43.5 0.7 broadcast_compare_fusion
  44.2 0.2 copy.35
  44.4 0.1 copy.36
  44.5 0.2 copy.30
  44.7 0.1 copy.31
  44.8 0.9 compare_and_fusion
  45.7 0.4 reshape.117
  46.1 1.3 fusion.37
  48.1 1.3 compare_reduce_fusion
  50.0 0.3 compare_and_fusion.1
  50.3 0.4 reshape.114
  50.7 0.1 broadcast_add_fusion.2
  50.8 0.6 select_reduce_fusion.1
  51.4 0.1 reshape.115
  51.5 0.1 reshape.118
  51.6 18.5 %all-gather.1 = f32[16,64,8]{1,2,0:T(8,128)S(1)} all-gather(f32[1,64,8]{1,2,0:T(8,128)} %bitcast.65), channel_id=1, replica_groups=mesh['ep'=16,'dp'=2] {'ep'}, dimensions={0}, use_global_device_ids=true | all-gather | bytes 34816 | tf_op jit(solution)/shard_map/all_gather | solution.py:63
  70.1 0.1 reshape.171
  70.2 1.1 copy.33
  71.3 0.1 broadcast_add_fusion.1
  71.4 0.3 reshape.116
  71.7 0.3 reshape.119
  72.1 0.2 select_reduce_fusion.4
  72.3 0.2 select_reduce_fusion.2
  72.5 1.5 select_reduce_fusion.5
  74.1 20.5 %all-gather.5.cloned.1.call-done = bf16[1024,4096]{1,0:T(8,128)(2,1)} async-done(((bf16[64,4096]{1,0:T(8,128)(2,1)}), bf16[1024,4096]{1,0:T(8,128)(2,1)}) %all-gather.5.cloned.1.call-update) | async-done | bytes 8388624 | tf_op jit(solution)/shard_map/all_gather | solution.py:61
  94.6 13.0 %gather_fusion = bf16[512,4096]{1,0:T(8,128)(2,1)} fusion(bf16[1024,4096]{1,0:T(8,128)(2,1)} %all-gather.5.cloned.1.call-done, s32[1024]{0:T(1024)S(1)} %pad_clamp_fusion.1), kind=kCustom, calls=%fused_computation.clone | custom fusion | bytes 8390656 | tf_op jit(solution)/shard_map/jit(_take)/gather | solution.py:81
  107.7 8.3 %fusion = f32[512,2,512]{2,0,1:T(8,128)S(1)} fusion(bf16[4096,2,512]{2,1,0:T(2,128)(2,1)} %bitcast.66, bf16[512,4096]{1,0:T(8,128)(2,1)} %gather_fusion, pred[512]{0:T(512)(128)(4,1)S(1)} %compare_and_fusion.5), kind=kOutput, calls=%fused_computation.4 | convolution fusion | flops 4297064448 | bytes 14680576 | tf_op jit(solution)/shard_map/rd,djf->rjf/dot_general | solution.py:8
  116.0 1.1 fusion.25
  117.1 0.0 all-gather.7.cloned.1.call-update
  117.1 0.2 reduce-scatter.2.cloned.1.call-start
  117.3 13.0 %gather_fusion.2 = bf16[512,4096]{1,0:T(8,128)(2,1)} fusion(bf16[1024,4096]{1,0:T(8,128)(2,1)} %all-gather.5.cloned.1.call-done, s32[1024]{0:T(1024)S(1)} %pad_clamp_fusion), kind=kCustom, calls=%fused_computation.2.clone | custom fusion | bytes 8390656 | tf_op jit(solution)/shard_map/jit(_take)/gather | solution.py:82
  130.4 5.8 %fusion.3 = f32[512,2,256]{2,0,1:T(8,128)S(1)} fusion(bf16[4096,2,256]{2,1,0:T(2,128)(2,1)} %bitcast.67, bf16[512,4096]{1,0:T(8,128)(2,1)} %gather_fusion.2, pred[512]{0:T(512)(128)(4,1)S(1)} %compare_and_fusion.4), kind=kOutput, calls=%fused_computation.9 | convolution fusion | flops 2149580800 | bytes 9437696 | tf_op jit(solution)/shard_map/rd,djf->rjf/dot_general | solution.py:8
  136.2 0.2 fusion.29
  136.4 9.4 %all_gather.23 = bf16[512,512]{1,0:T(8,128)(2,1)S(1)} all-gather(bf16[512,256]{1,0:T(8,128)(2,1)S(1)} %fusion.29), channel_id=1, replica_groups=mesh['ep'=16,'dp'=2] {'dp'}, dimensions={1}, use_global_device_ids=true | all-gather | bytes 786432 | tf_op jit(solution)/shard_map/all_gather | solution.py:86
  145.7 0.0 copy-done
  145.7 3.3 %fusion.19 = f32[512,2048]{1,0:T(8,128)} fusion(bf16[512,512]{1,0:T(8,128)(2,1)S(1)} %all_gather.23, bf16[1,512,2048]{2,1,0:T(8,128)(2,1)S(1)} %copy-done), kind=kOutput, calls=%fused_computation.21 | convolution fusion | flops 1073741824 | bytes 6815744 | tf_op jit(solution)/shard_map/dot_general | solution.py:89
  149.0 11.2 %gather_fusion.3 = f32[1024,2048]{1,0:T(8,128)} fusion(f32[512,2048]{1,0:T(8,128)} %fusion.19, s32[1024]{0:T(1024)S(1)} %fusion.33), kind=kCustom, calls=%fused_computation.3.clone | custom fusion | bytes 16781312 | tf_op jit(solution)/shard_map/jit(_take)/gather | solution.py:95
  160.2 0.0 all-gather.7.cloned.1.call-done
  160.2 6.8 %fusion.16 = f32[512,2048]{1,0:T(8,128)} fusion(bf16[512,1024]{1,0:T(8,128)(2,1)} %all-gather.7.cloned.1.call-done, bf16[1,1024,2048]{2,1,0:T(8,128)(2,1)} %param.19), kind=kOutput, calls=%fused_computation.20 | convolution fusion | flops 2149580800 | bytes 9437184 | tf_op jit(solution)/shard_map/dot_general | solution.py:87
  167.0 11.3 %gather_fusion.1 = f32[1024,2048]{1,0:T(8,128)} fusion(f32[512,2048]{1,0:T(8,128)} %fusion.16, s32[1024]{0:T(1024)S(1)} %fusion.32), kind=kCustom, calls=%fused_computation.1.clone | custom fusion | bytes 16781312 | tf_op jit(solution)/shard_map/jit(_take)/gather | solution.py:93
  178.2 9.9 %fusion.2 = f32[1024,2048]{1,0:T(8,128)} fusion(f32[1024,2048]{1,0:T(8,128)} %gather_fusion.3, f32[1024,2048]{1,0:T(8,128)} %gather_fusion.1, f32[1024]{0:T(1024)S(1)} %get-tuple-element.8, f32[1024]{0:T(1024)S(1)} %get-tuple-element.6, pred[1024]{0:T(1024)(128)(4,1)S(1)} %get-tuple-element.19, pred[1024]{0:T(1024)(128)(4,1)S(1)} %get-tuple-element.20), kind=kLoop, calls=%fused_computation.7 | loop fusion | flops 10485760 | bytes 25176064 | tf_op jit(solution)/shard_map/add | solution.py:93
  188.1 0.0 copy-start.1
  188.1 0.0 reduce-scatter.2.cloned.1.call-update
  188.2 103.1 %reduce-scatter.2.cloned.1.call-done = f32[64,2048]{1,0:T(8,128)} async-done(((f32[1024,2048]{1,0:T(8,128)}), f32[64,2048]{1,0:T(8,128)}) %reduce-scatter.2.cloned.1.call-update) | async-done | bytes 524304 | tf_op jit(solution)/shard_map/reduce_scatter | solution.py:96
  291.2 1.8 convert_element_type.31
  293.0 0.0 copy-done.1
  (15 shorter events, 0.1 us)
Async XLA Ops:
  6.5 139.2 %copy-start = (bf16[1,512,2048]{2,1,0:T(8,128)(2,1)S(1)}, bf16[1,512,2048]{2,1,0:T(8,128)(2,1)}, u32[]{:S(2)}) copy-start(bf16[1,512,2048]{2,1,0:T(8,128)(2,1)} %param.21) | copy-start | bytes 6291460
  6.5 88.1 %all-gather.5.cloned.1.call-start = ((), (), s32[]{:S(2)}) async-start(), calls=%async_computation.1 | async-start | bytes 8912896 | tf_op jit(solution)/shard_map/all_gather | solution.py:61
  18.6 141.6 %all-gather.7.cloned.1.call-start = ((), (), s32[]{:S(2)}) async-start(), calls=%async_computation.2 | async-start | bytes 1572864 | tf_op jit(solution)/shard_map/all_gather | solution.py:85
  117.1 174.1 %reduce-scatter.2.cloned.1.call-start = ((), (), s32[]{:S(2)}) async-start(), calls=%async_computation.3 | async-start | bytes 8912896 | tf_op jit(solution)/shard_map/reduce_scatter | solution.py:96
  188.1 104.9 %copy-start.1 = (bf16[1,512,2048]{2,1,0:T(8,128)(2,1)S(1)}, bf16[1,512,2048]{2,1,0:T(8,128)(2,1)}, u32[]{:S(2)}) copy-start(bf16[1,512,2048]{2,1,0:T(8,128)(2,1)} %param.21) | copy-start | bytes 6291460
Sparse Core Ops, SparseCore 0:
  18.7 75.8 all-gather.4
  117.2 19.5 all-gather.6
  188.3 102.8 reduce-scatter.1

commit v2 on v1

--- a/solution.py
+++ b/solution.py
@@ -37,6 +37,20 @@
     return index, scale
 
 
+def one_hot(index, size):
+    return (index[:, None] == jnp.arange(size, dtype=jnp.int32)[None, :]).astype(jnp.bfloat16)
+
+
+def side_columns(expert_ids, gate_logits):
+    high = gate_logits.astype(jnp.bfloat16)
+    rest = gate_logits - high.astype(jnp.float32)
+    middle = rest.astype(jnp.bfloat16)
+    low = (rest - middle.astype(jnp.float32)).astype(jnp.bfloat16)
+    columns = jnp.concatenate([expert_ids.astype(jnp.bfloat16), high, middle, low], axis=1)
+    width = -columns.shape[1] % 128
+    return jnp.pad(columns, ((0, 0), (0, width)))
+
+
 def per_device(
     tokens,
     expert_ids,
@@ -57,11 +71,17 @@
     capacity = group_tokens * top_count // ep_count
     per_group = group_tokens * top_count
 
+    d_model = tokens.shape[1] * lax.axis_size("dp")
     whole_rows = lax.all_gather(tokens, "dp", axis=1, tiled=True)
-    every_row = lax.all_gather(whole_rows, "ep", axis=0, tiled=True)
-    every_id = lax.all_gather(expert_ids, "ep", axis=0, tiled=True)
-    every_logit = lax.all_gather(gate_logits, "ep", axis=0, tiled=True)
-    ids = every_id.reshape(ep_count, per_group)
+    packed = jnp.concatenate([whole_rows, side_columns(expert_ids, gate_logits)], axis=1)
+    every_row = lax.all_gather(packed, "ep", axis=0, tiled=True)
+    all_tokens = every_row.shape[0]
+    ids = every_row[:, d_model : d_model + top_count].astype(jnp.int32)
+    parts = every_row[:, d_model + top_count : d_model + 4 * top_count].astype(jnp.float32)
+    every_logit = (
+        parts[:, :top_count] + parts[:, top_count : 2 * top_count]
+    ) + parts[:, 2 * top_count :]
+    ids = ids.reshape(ep_count, per_group)
 
     gate_score = jax.nn.sigmoid(every_logit)
     gate_weight = 2.5 * gate_score / jnp.sum(gate_score, axis=1, keepdims=True)
@@ -78,21 +98,30 @@
         ids, placement[spare_index], split_rows[spare_index], capacity, capacity, top_count
     )
 
-    home_rows = jnp.take(every_row, home_rows_of, axis=0)
-    spare_rows = jnp.take(every_row, spare_rows_of, axis=0)
-    home_hidden = gate_up(home_rows, gate_up_weight[0])
-    spare_hidden = gate_up(spare_rows, spare_gate_up[0])
+    slot_rows = home_rows_of.shape[0]
+    pick = one_hot(jnp.concatenate([home_rows_of, spare_rows_of]), all_tokens)
+    rows = jnp.dot(pick, every_row, preferred_element_type=jnp.float32).astype(jnp.bfloat16)
+    home_hidden = gate_up(rows[:slot_rows, :d_model], gate_up_weight[0])
+    spare_hidden = gate_up(rows[slot_rows:, :d_model], spare_gate_up[0])
     home_hidden = lax.all_gather(home_hidden, "dp", axis=1, tiled=True)
     spare_hidden = lax.all_gather(spare_hidden, "dp", axis=1, tiled=True)
     home_out = jnp.dot(home_hidden, down_weight[0], preferred_element_type=jnp.float32)
-    home_out = home_out.astype(jnp.bfloat16).astype(jnp.float32)
+    home_out = home_out.astype(jnp.bfloat16)
     spare_out = jnp.dot(spare_hidden, spare_down[0], preferred_element_type=jnp.float32)
+    spare_high = spare_out.astype(jnp.bfloat16)
+    spare_low = (spare_out - spare_high.astype(jnp.float32)).astype(jnp.bfloat16)
 
     home_at, home_scale = per_token(home_kept, home_flat, gate_weight, group_tokens, top_count)
     spare_at, spare_scale = per_token(spare_kept, spare_flat, gate_weight, group_tokens, top_count)
-    partial = home_scale[:, None] * jnp.take(home_out, home_at, axis=0) + spare_scale[
-        :, None
-    ] * jnp.take(spare_out, spare_at, axis=0)
+    home_pick = one_hot(home_at, slot_rows)
+    spare_pick = one_hot(spare_at, slot_rows)
+    home_term = jnp.dot(home_pick, home_out, preferred_element_type=jnp.float32)
+    spare_term = jnp.dot(
+        jnp.concatenate([spare_pick, spare_pick], axis=1),
+        jnp.concatenate([spare_high, spare_low], axis=0),
+        preferred_element_type=jnp.float32,
+    )
+    partial = home_scale[:, None] * home_term + spare_scale[:, None] * spare_term
     mixed = lax.psum_scatter(partial, "ep", scatter_dimension=0, tiled=True)
     return mixed.astype(jnp.bfloat16)
 

time: 300 us -> 278 us (0.927)
  waiting for transfers between devices: 124 us -> 176 us
  local copies, waits for them, and re-layouts: 54.2 us -> 4.81 us
  blocking collectives: 62.2 us -> 21.6 us
  matrix products: 25.4 us -> 44 us
    all_gather x1, waiting for transfers between devices: 20.5 us -> 71.3 us  [per_device(): every_row = lax.all_gather(packed, 'ep', axis=0, tiled=True)]
    gather x4 -> x0, local copies, waits for them, and re-layouts: 48.5 us -> none  [the longest x1 13 us: per_device(): spare_rows = jnp.take(every_row, spare_rows_of, axis=0)]
    all_gather x2 -> x0, blocking collectives: 40.9 us -> none  [the longest x1 22.4 us: per_device(): every_id = lax.all_gather(expert_ids, 'ep', axis=0, tiled=True)]
    dot_general x1 -> x3, matrix products: 6.77 us -> 33.8 us  [the longest x1 14.1 us: per_device(): jnp.dot(pick, every_row, preferred_element_type=jnp.float32)]
    add x1 -> x0, other arithmetic: 9.91 us -> none  [per_device(): home_scale[:, None] * jnp.take(home_out, home_at, axis=0)]
    dot_general x2, matrix products: 14.2 us -> 7.81 us  [gate_up(): jnp.einsum('rd,djf->rjf', row_block, weight, preferred_element_type=jnp.f...]
  transfers between devices with their start and end apart: 3 -> 3, of which waited for: 2 -> 3; matrix products, arithmetic and copies ran while one was open for 16% -> 5% of each run, Pallas kernels for 0% -> 0%
where the time goes in v2:
time: 278 us; the launch traced here: 277 us
  waiting for transfers between devices  176 us (63%)
  matrix products  44 us (16%)
  blocking collectives  21.6 us (8%)
  other arithmetic  16.5 us (6%)
  between operations  14.7 us (5%)
  local copies, waits for them, and re-layouts  4.81 us (2%)
    reduce_scatter x1, waiting for transfers between devices, per_device(): mixed = lax.psum_scatter(partial, 'ep', scatter_dimension=0, tiled=True)  104 us
    all_gather x1, waiting for transfers between devices, per_device(): every_row = lax.all_gather(packed, 'ep', axis=0, tiled=True)  71.3 us
    dot_general x1, matrix products, per_device(): jnp.dot(pick, every_row, preferred_element_type=jnp.float32)  14.1 us
    dot_general x1, matrix products, per_device(): home_term = jnp.dot(home_pick, home_out, preferred_element_type=jnp.float32)  12.8 us
    all_gather x1, blocking collectives, per_device(): spare_hidden = lax.all_gather(spare_hidden, 'dp', axis=1, tiled=True)  11.4 us
    all_gather x1, blocking collectives, per_device(): whole_rows = lax.all_gather(tokens, 'dp', axis=1, tiled=True)  10.2 us
    dot_general x2, matrix products, gate_up(): jnp.einsum('rd,djf->rjf', row_block, weight, preferred_element_type=jnp.f...  7.81 us
    dot_general x1, matrix products, per_device(): jnp.dot(jnp.concatenate([spare_pick, spare_pick], axis=1), jnp.concatenat...  6.9 us
  transfers between devices with their start and end apart: 3, of which 3 were waited for; matrix products, arithmetic and copies ran while one was open for 5% of the time, Pallas kernels for 0%

profile of v2, /device:TPU:0, one launch (start us, length us, event | category | flops | bytes accessed | tf_op | source)
XLA Modules:
  0.0 277.2 jit_solution(11659869268425289471)
XLA Ops:
  6.5 0.0 copy-start
  6.5 0.0 all-gather.3.cloned.1.call-start
  6.5 0.8 convert_element_type.63
  7.4 0.8 fusion.44
  8.2 0.1 copy.26
  8.3 10.2 %all_gather.12 = bf16[64,4096]{1,0:T(8,128)(2,1)S(1)} all-gather(bf16[64,2048]{1,0:T(8,128)(2,1)} %param.9), channel_id=1, replica_groups=mesh['ep'=16,'dp'=2] {'dp'}, dimensions={1}, use_global_device_ids=true | all-gather | bytes 786432 | tf_op jit(solution)/shard_map/all_gather | solution.py:75
  18.4 0.9 fusion.28
  19.3 0.0 all-gather.3.cloned.1.call-update
  19.3 0.0 all-gather.5.cloned.1.call-start
  19.4 1.2 dynamic_slice.6
  20.7 1.3 dynamic_slice.7
  21.9 1.4 fusion.39
  24.0 1.4 compare_reduce_fusion
  26.1 0.1 broadcast_add_fusion
  26.2 71.3 %all-gather.3.cloned.1.call-done = bf16[1024,4224]{1,0:T(8,128)(2,1)} async-done(((bf16[64,4224]{1,0:T(8,128)(2,1)}), bf16[1024,4224]{1,0:T(8,128)(2,1)}) %all-gather.3.cloned.1.call-update) | async-done | bytes 8650768 | tf_op jit(solution)/shard_map/all_gather | solution.py:77
  97.5 1.8 convert_compare_fusion
  99.3 0.3 eq.102
  99.7 0.3 eq.91
  100.0 0.9 compare_and_fusion
  100.9 0.4 reshape.111
  101.2 0.3 compare_and_fusion.1
  101.5 0.4 reshape.107
  101.9 0.6 select_reduce_fusion.1
  102.5 0.1 broadcast_add_fusion.2
  102.6 0.1 reshape.109
  102.7 0.1 reshape.110
  102.8 0.3 reshape.108
  103.1 0.3 reshape.112
  103.4 0.2 select_reduce_fusion.2
  103.6 1.2 iota_compare_fusion.2
  104.8 1.1 slice_convert_fusion
  105.9 0.0 slice-start
  105.9 0.5 fusion.42
  106.4 0.0 copy-start.2
  106.4 0.0 slice-start.1
  106.4 14.1 %convolution_convert_fusion = bf16[1024,4224]{1,0:T(8,128)(2,1)S(1)} fusion(bf16[1024,4224]{1,0:T(8,128)(2,1)} %all-gather.3.cloned.1.call-done, s32[1024]{0:T(1024)S(1)} %pad_add_fusion), kind=kOutput, calls=%fused_computation | convolution fusion | flops 8863744000 | bytes 17305600 | tf_op jit(solution)/shard_map/dot_general | solution.py:103
  120.6 0.0 copy-done.2
  120.6 3.3 %fusion.2 = f32[512,2,256]{2,0,1:T(8,128)} fusion(bf16[1024,4224]{1,0:T(8,128)(2,1)S(1)} %convolution_convert_fusion, bf16[4096,2,256]{2,1,0:T(2,128)(2,1)S(1)} %bitcast.50), kind=kOutput, calls=%fused_computation.5 | convolution fusion | flops 2147483648 | bytes 9437184 | tf_op jit(solution)/shard_map/rd,djf->rjf/dot_general | solution.py:8
  123.9 0.0 slice-done
  123.9 0.0 slice-done.1
  123.9 4.5 %fusion = f32[512,2,512]{2,0,1:T(8,128)S(1)} fusion(bf16[4096,2,512]{2,1,0:T(2,128)(2,1)S(1)} %bitcast.49, bf16[1024,4224]{1,0:T(8,128)(2,1)S(1)} %convolution_convert_fusion), kind=kOutput, calls=%fused_computation.1 | convolution fusion | flops 4294967296 | bytes 14680064 | tf_op jit(solution)/shard_map/rd,djf->rjf/dot_general | solution.py:8
  128.4 1.1 fusion.22
  129.5 2.1 fusion.30
  131.6 0.0 all-gather.5.cloned.1.call-update
  131.6 0.0 reduce-scatter.2.cloned.1.call-start
  131.6 11.4 %all_gather.15 = bf16[512,512]{1,0:T(8,128)(2,1)S(1)} all-gather(bf16[512,256]{1,0:T(8,128)(2,1)} %fusion.30), channel_id=1, replica_groups=mesh['ep'=16,'dp'=2] {'dp'}, dimensions={1}, use_global_device_ids=true | all-gather | bytes 786432 | tf_op jit(solution)/shard_map/all_gather | solution.py:107
  143.0 0.2 select_reduce_fusion.4
  143.2 0.5 select_reduce_fusion.5
  143.8 0.0 copy-done
  143.8 0.0 copy-start.1
  143.8 1.3 subtract_convert_fusion
  145.1 0.0 copy-done.1
  145.1 6.9 %fusion.3 = f32[1024,2048]{1,0:T(8,128)} fusion(bf16[512,2048]{1,0:T(8,128)(2,1)S(1)} %get-tuple-element.11, bf16[512,2048]{1,0:T(8,128)(2,1)S(1)} %get-tuple-element.12, pred[1024,512]{1,0:T(32,128)(4,1)S(1)} %copy-done.1), kind=kOutput, calls=%fused_computation.7 | convolution fusion | flops 4304404480 | bytes 13107200 | tf_op jit(solution)/shard_map/dot_general | solution.py:119
  152.0 0.5 all-gather.5.cloned.1.call-done
  152.5 12.8 %multiply_add_fusion = f32[1024,2048]{1,0:T(8,128)} fusion(f32[1024,2048]{1,0:T(8,128)} %fusion.3, f32[1024]{0:T(1024)S(1)} %get-tuple-element.6, f32[1024]{0:T(1024)S(1)} %get-tuple-element.5, s32[1024]{0:T(1024)S(1)} %select_reduce_fusion.4, bf16[512,1024]{1,0:T(8,128)(2,1)} %all-gather.5.cloned.1.call-done, bf16[1,1024,2048]{2,1,0:T(8,128)(2,1)} %param.15), kind=kOutput, calls=%fused_computation.3 | convolution fusion | flops 4302831616 | bytes 22032384 | tf_op jit(solution)/shard_map/dot_general | solution.py:118
  165.3 0.0 reduce-scatter.2.cloned.1.call-update
  165.3 103.6 %reduce-scatter.2.cloned.1.call-done = f32[64,2048]{1,0:T(8,128)} async-done(((f32[1024,2048]{1,0:T(8,128)}), f32[64,2048]{1,0:T(8,128)}) %reduce-scatter.2.cloned.1.call-update) | async-done | bytes 524304 | tf_op jit(solution)/shard_map/reduce_scatter | solution.py:125
  268.9 1.8 convert_element_type.80
  (6 shorter events, 0.0 us)
Async XLA Ops:
  6.5 137.2 %copy-start = (bf16[1,512,2048]{2,1,0:T(8,128)(2,1)S(1)}, bf16[1,512,2048]{2,1,0:T(8,128)(2,1)}, u32[]{:S(2)}) copy-start(bf16[1,512,2048]{2,1,0:T(8,128)(2,1)} %param.17) | copy-start | bytes 6291460
  6.5 91.0 %all-gather.3.cloned.1.call-start = ((), (), s32[]{:S(2)}) async-start(), calls=%async_computation.1 | async-start | bytes 9191424 | tf_op jit(solution)/shard_map/all_gather | solution.py:77
  19.3 133.1 %all-gather.5.cloned.1.call-start = ((), (), s32[]{:S(2)}) async-start(), calls=%async_computation.2 | async-start | bytes 1572864 | tf_op jit(solution)/shard_map/all_gather | solution.py:106
  105.9 18.0 %slice-start = ((s8[8388608]{0:T(1024)(128)(4,1)}), s8[4194304]{0:T(1024)(128)(4,1)S(1)}, s32[]{:S(2)}) async-start(s8[8388608]{0:T(1024)(128)(4,1)} %bitcast.47), calls=%async_computation.4 | async-start | bytes 8388608
  106.4 14.2 %copy-start.2 = (bf16[1,4096,2,256]{3,2,1,0:T(2,128)(2,1)S(1)}, bf16[1,4096,2,256]{3,2,1,0:T(2,128)(2,1)}, u32[]{:S(2)}) copy-start(bf16[1,4096,2,256]{3,2,1,0:T(2,128)(2,1)} %param.16) | copy-start | bytes 12582916
  106.4 17.5 %slice-start.1 = ((s8[8388608]{0:T(1024)(128)(4,1)}), s8[4194304]{0:T(1024)(128)(4,1)S(1)}, s32[]{:S(2)}) async-start(s8[8388608]{0:T(1024)(128)(4,1)} %bitcast.47), calls=%async_computation.5 | async-start | bytes 8388608
  131.6 137.3 %reduce-scatter.2.cloned.1.call-start = ((), (), s32[]{:S(2)}) async-start(), calls=%async_computation.3 | async-start | bytes 8912896 | tf_op jit(solution)/shard_map/reduce_scatter | solution.py:125
  143.8 1.3 copy-start.1
Sparse Core Ops, SparseCore 0:
  19.5 78.0 all-gather.2
  131.7 20.7 all-gather.4
  165.4 103.4 reduce-scatter.1

commit v3 on v2

--- a/solution.py
+++ b/solution.py
@@ -122,7 +122,7 @@
         preferred_element_type=jnp.float32,
     )
     partial = home_scale[:, None] * home_term + spare_scale[:, None] * spare_term
-    mixed = lax.psum_scatter(partial, "ep", scatter_dimension=0, tiled=True)
+    mixed = lax.psum_scatter(partial.astype(jnp.bfloat16), "ep", scatter_dimension=0, tiled=True)
     return mixed.astype(jnp.bfloat16)
 
 

time: 278 us -> 240 us (0.86)
  waiting for transfers between devices: 176 us -> 144 us
  matrix products: 44 us -> 40.5 us
    reduce_scatter x1, waiting for transfers between devices: 104 us -> 71.7 us  [per_device(): lax.psum_scatter(partial.astype(jnp.bfloat16), 'ep', scatter_dimension=0,...]
    dot_general x1, matrix products: 12.8 us -> 9.31 us  [per_device(): home_term = jnp.dot(home_pick, home_out, preferred_element_type=jnp.float32)]
  transfers between devices with their start and end apart: 3 -> 3, of which waited for: 3 -> 3; matrix products, arithmetic and copies ran while one was open for 5% -> 6% of each run, Pallas kernels for 0% -> 0%
where the time goes in v3:
time: 240 us
  waiting for transfers between devices  144 us (60%)
  matrix products  40.5 us (17%)
  blocking collectives  21.6 us (9%)
  other arithmetic  14.8 us (6%)
  between operations  14.7 us (6%)
  local copies, waits for them, and re-layouts  4.81 us (2%)
    reduce_scatter x1, waiting for transfers between devices, per_device(): lax.psum_scatter(partial.astype(jnp.bfloat16), 'ep', scatter_dimension=0,...  71.7 us
    all_gather x1, waiting for transfers between devices, per_device(): every_row = lax.all_gather(packed, 'ep', axis=0, tiled=True)  71.3 us
    dot_general x1, matrix products, per_device(): jnp.dot(pick, every_row, preferred_element_type=jnp.float32)  14.1 us
    all_gather x1, blocking collectives, per_device(): spare_hidden = lax.all_gather(spare_hidden, 'dp', axis=1, tiled=True)  11.4 us
    all_gather x1, blocking collectives, per_device(): whole_rows = lax.all_gather(tokens, 'dp', axis=1, tiled=True)  10.2 us
    dot_general x1, matrix products, per_device(): home_term = jnp.dot(home_pick, home_out, preferred_element_type=jnp.float32)  9.31 us
    dot_general x2, matrix products, gate_up(): jnp.einsum('rd,djf->rjf', row_block, weight, preferred_element_type=jnp.f...  7.81 us
    dot_general x1, matrix products, per_device(): jnp.dot(jnp.concatenate([spare_pick, spare_pick], axis=1), jnp.concatenat...  6.9 us
  transfers between devices with their start and end apart: 3, of which 3 were waited for; matrix products, arithmetic and copies ran while one was open for 6% of the time, Pallas kernels for 0%

profile of v3, /device:TPU:0, one launch (start us, length us, event | category | flops | bytes accessed | tf_op | source)
XLA Modules:
  0.0 240.1 jit_solution(3717927794578679420)
XLA Ops:
  6.5 0.0 copy-start
  6.5 0.0 all-gather.3.cloned.1.call-start
  6.5 0.8 convert_element_type.63
  7.4 0.8 fusion.44
  8.2 0.1 copy.26
  8.3 10.2 %all_gather.12 = bf16[64,4096]{1,0:T(8,128)(2,1)S(1)} all-gather(bf16[64,2048]{1,0:T(8,128)(2,1)} %param.9), channel_id=1, replica_groups=mesh['ep'=16,'dp'=2] {'dp'}, dimensions={1}, use_global_device_ids=true | all-gather | bytes 786432 | tf_op jit(solution)/shard_map/all_gather | solution.py:75
  18.4 0.9 fusion.28
  19.3 0.0 all-gather.3.cloned.1.call-update
  19.3 0.0 all-gather.5.cloned.1.call-start
  19.4 1.2 dynamic_slice.6
  20.7 1.3 dynamic_slice.7
  21.9 1.4 fusion.39
  24.0 1.4 compare_reduce_fusion
  26.1 0.1 broadcast_add_fusion
  26.2 71.3 %all-gather.3.cloned.1.call-done = bf16[1024,4224]{1,0:T(8,128)(2,1)} async-done(((bf16[64,4224]{1,0:T(8,128)(2,1)}), bf16[1024,4224]{1,0:T(8,128)(2,1)}) %all-gather.3.cloned.1.call-update) | async-done | bytes 8650768 | tf_op jit(solution)/shard_map/all_gather | solution.py:77
  97.5 1.8 convert_compare_fusion
  99.3 0.3 eq.102
  99.7 0.3 eq.91
  100.0 0.9 compare_and_fusion
  100.9 0.4 reshape.111
  101.2 0.3 compare_and_fusion.1
  101.5 0.4 reshape.107
  101.9 0.6 select_reduce_fusion.1
  102.5 0.1 broadcast_add_fusion.2
  102.6 0.1 reshape.109
  102.7 0.1 reshape.110
  102.8 0.3 reshape.108
  103.1 0.3 reshape.112
  103.4 0.2 select_reduce_fusion.2
  103.6 1.2 iota_compare_fusion.2
  104.8 1.1 slice_convert_fusion
  105.9 0.0 slice-start
  105.9 0.5 fusion.42
  106.4 0.0 copy-start.2
  106.4 0.0 slice-start.1
  106.5 14.1 %convolution_convert_fusion = bf16[1024,4224]{1,0:T(8,128)(2,1)S(1)} fusion(bf16[1024,4224]{1,0:T(8,128)(2,1)} %all-gather.3.cloned.1.call-done, s32[1024]{0:T(1024)S(1)} %pad_add_fusion), kind=kOutput, calls=%fused_computation | convolution fusion | flops 8863744000 | bytes 17305600 | tf_op jit(solution)/shard_map/dot_general | solution.py:103
  120.6 0.0 copy-done.2
  120.6 3.3 %fusion.2 = f32[512,2,256]{2,0,1:T(8,128)} fusion(bf16[1024,4224]{1,0:T(8,128)(2,1)S(1)} %convolution_convert_fusion, bf16[4096,2,256]{2,1,0:T(2,128)(2,1)S(1)} %bitcast.50), kind=kOutput, calls=%fused_computation.5 | convolution fusion | flops 2147483648 | bytes 9437184 | tf_op jit(solution)/shard_map/rd,djf->rjf/dot_general | solution.py:8
  123.9 0.0 slice-done
  123.9 0.0 slice-done.1
  124.0 4.5 %fusion = f32[512,2,512]{2,0,1:T(8,128)S(1)} fusion(bf16[4096,2,512]{2,1,0:T(2,128)(2,1)S(1)} %bitcast.49, bf16[1024,4224]{1,0:T(8,128)(2,1)S(1)} %convolution_convert_fusion), kind=kOutput, calls=%fused_computation.1 | convolution fusion | flops 4294967296 | bytes 14680064 | tf_op jit(solution)/shard_map/rd,djf->rjf/dot_general | solution.py:8
  128.4 1.1 fusion.22
  129.6 2.1 fusion.30
  131.6 0.0 all-gather.5.cloned.1.call-update
  131.7 0.0 reduce-scatter.2.cloned.1.call-start
  131.7 11.4 %all_gather.15 = bf16[512,512]{1,0:T(8,128)(2,1)S(1)} all-gather(bf16[512,256]{1,0:T(8,128)(2,1)} %fusion.30), channel_id=1, replica_groups=mesh['ep'=16,'dp'=2] {'dp'}, dimensions={1}, use_global_device_ids=true | all-gather | bytes 786432 | tf_op jit(solution)/shard_map/all_gather | solution.py:107
  143.1 0.2 select_reduce_fusion.4
  143.3 0.5 select_reduce_fusion.5
  143.8 0.0 copy-done
  143.8 0.0 copy-start.1
  143.9 1.3 subtract_convert_fusion
  145.1 0.0 copy-done.1
  145.1 6.9 %fusion.3 = f32[1024,2048]{1,0:T(8,128)} fusion(bf16[512,2048]{1,0:T(8,128)(2,1)S(1)} %get-tuple-element.11, bf16[512,2048]{1,0:T(8,128)(2,1)S(1)} %get-tuple-element.12, pred[1024,512]{1,0:T(32,128)(4,1)S(1)} %copy-done.1), kind=kOutput, calls=%fused_computation.7 | convolution fusion | flops 4304404480 | bytes 13107200 | tf_op jit(solution)/shard_map/dot_general | solution.py:119
  152.0 0.5 all-gather.5.cloned.1.call-done
  152.5 9.3 %add_convert_fusion = bf16[1024,2048]{1,0:T(8,128)(2,1)} fusion(f32[1024,2048]{1,0:T(8,128)} %fusion.3, f32[1024]{0:T(1024)S(1)} %get-tuple-element.6, f32[1024]{0:T(1024)S(1)} %get-tuple-element.5, s32[1024]{0:T(1024)S(1)} %select_reduce_fusion.4, bf16[512,1024]{1,0:T(8,128)(2,1)} %all-gather.5.cloned.1.call-done, bf16[1,1024,2048]{2,1,0:T(8,128)(2,1)} %param.15), kind=kOutput, calls=%fused_computation.3 | convolution fusion | flops 4304928768 | bytes 17838080 | tf_op jit(solution)/shard_map/dot_general | solution.py:118
  161.9 0.0 reduce-scatter.2.cloned.1.call-update
  161.9 71.7 %reduce-scatter.2.cloned.1.call-done = bf16[64,2048]{1,0:T(8,128)(2,1)} async-done(((bf16[1024,2048]{1,0:T(8,128)(2,1)}), bf16[64,2048]{1,0:T(8,128)(2,1)}) %reduce-scatter.2.cloned.1.call-update) | async-done | bytes 262160 | tf_op jit(solution)/shard_map/reduce_scatter | solution.py:125
  (6 shorter events, 0.0 us)
Async XLA Ops:
  6.5 137.3 %copy-start = (bf16[1,512,2048]{2,1,0:T(8,128)(2,1)S(1)}, bf16[1,512,2048]{2,1,0:T(8,128)(2,1)}, u32[]{:S(2)}) copy-start(bf16[1,512,2048]{2,1,0:T(8,128)(2,1)} %param.17) | copy-start | bytes 6291460
  6.5 91.0 %all-gather.3.cloned.1.call-start = ((), (), s32[]{:S(2)}) async-start(), calls=%async_computation.1 | async-start | bytes 9191424 | tf_op jit(solution)/shard_map/all_gather | solution.py:77
  19.3 133.2 %all-gather.5.cloned.1.call-start = ((), (), s32[]{:S(2)}) async-start(), calls=%async_computation.2 | async-start | bytes 1572864 | tf_op jit(solution)/shard_map/all_gather | solution.py:106
  105.9 18.0 %slice-start = ((s8[8388608]{0:T(1024)(128)(4,1)}), s8[4194304]{0:T(1024)(128)(4,1)S(1)}, s32[]{:S(2)}) async-start(s8[8388608]{0:T(1024)(128)(4,1)} %bitcast.47), calls=%async_computation.4 | async-start | bytes 8388608
  106.4 14.2 %copy-start.2 = (bf16[1,4096,2,256]{3,2,1,0:T(2,128)(2,1)S(1)}, bf16[1,4096,2,256]{3,2,1,0:T(2,128)(2,1)}, u32[]{:S(2)}) copy-start(bf16[1,4096,2,256]{3,2,1,0:T(2,128)(2,1)} %param.16) | copy-start | bytes 12582916
  106.4 17.5 %slice-start.1 = ((s8[8388608]{0:T(1024)(128)(4,1)}), s8[4194304]{0:T(1024)(128)(4,1)S(1)}, s32[]{:S(2)}) async-start(s8[8388608]{0:T(1024)(128)(4,1)} %bitcast.47), calls=%async_computation.5 | async-start | bytes 8388608
  131.7 101.9 %reduce-scatter.2.cloned.1.call-start = ((), (), s32[]{:S(2)}) async-start(), calls=%async_computation.3 | async-start | bytes 4456448 | tf_op jit(solution)/shard_map/reduce_scatter | solution.py:125
  143.8 1.3 copy-start.1
Sparse Core Ops, SparseCore 0:
  19.5 78.0 all-gather.2
  131.8 20.7 all-gather.4
  162.0 71.5 reduce-scatter.1

commit v4 on v3

--- a/solution.py
+++ b/solution.py
@@ -4,8 +4,16 @@
 from jax.sharding import PartitionSpec as P
 
 
-def gate_up(row_block, weight):
-    gate_both = jnp.einsum("rd,djf->rjf", row_block, weight, preferred_element_type=jnp.float32)
+def gate_up(rows_own, rows_other, weight, dp_me, order):
+    dp_count = order.shape[0] + 1
+    blocks = weight.reshape(dp_count, -1, weight.shape[1], weight.shape[2])
+    own = jnp.einsum(
+        "rd,djf->rjf", rows_own, blocks[dp_me], preferred_element_type=jnp.float32
+    )
+    rest = jnp.einsum(
+        "rbd,bdjf->rjf", rows_other, jnp.take(blocks, order, axis=0), preferred_element_type=jnp.float32
+    )
+    gate_both = own + rest
     return (jax.nn.silu(gate_both[:, 0, :]) * gate_both[:, 1, :]).astype(jnp.bfloat16)
 
 
@@ -71,13 +79,18 @@
     capacity = group_tokens * top_count // ep_count
     per_group = group_tokens * top_count
 
-    d_model = tokens.shape[1] * lax.axis_size("dp")
-    whole_rows = lax.all_gather(tokens, "dp", axis=1, tiled=True)
-    packed = jnp.concatenate([whole_rows, side_columns(expert_ids, gate_logits)], axis=1)
-    every_row = lax.all_gather(packed, "ep", axis=0, tiled=True)
-    all_tokens = every_row.shape[0]
-    ids = every_row[:, d_model : d_model + top_count].astype(jnp.int32)
-    parts = every_row[:, d_model + top_count : d_model + 4 * top_count].astype(jnp.float32)
+    dp_count = lax.axis_size("dp")
+    dp_me = lax.axis_index("dp")
+    block = tokens.shape[1]
+    own_columns = jnp.concatenate([tokens, side_columns(expert_ids, gate_logits)], axis=1)
+    first = lax.all_gather(own_columns, "ep", axis=0, tiled=True)
+    blocks = lax.all_gather(tokens, "dp", axis=0)
+    order = (dp_me + 1 + jnp.arange(dp_count - 1, dtype=jnp.int32)) % dp_count
+    others = jnp.transpose(jnp.take(blocks, order, axis=0), (1, 0, 2)).reshape(group_tokens, -1)
+    second = lax.all_gather(others, "ep", axis=0, tiled=True)
+    all_tokens = first.shape[0]
+    ids = first[:, block : block + top_count].astype(jnp.int32)
+    parts = first[:, block + top_count : block + 4 * top_count].astype(jnp.float32)
     every_logit = (
         parts[:, :top_count] + parts[:, top_count : 2 * top_count]
     ) + parts[:, 2 * top_count :]
@@ -100,14 +113,32 @@
 
     slot_rows = home_rows_of.shape[0]
     pick = one_hot(jnp.concatenate([home_rows_of, spare_rows_of]), all_tokens)
-    rows = jnp.dot(pick, every_row, preferred_element_type=jnp.float32).astype(jnp.bfloat16)
-    home_hidden = gate_up(rows[:slot_rows, :d_model], gate_up_weight[0])
-    spare_hidden = gate_up(rows[slot_rows:, :d_model], spare_gate_up[0])
-    home_hidden = lax.all_gather(home_hidden, "dp", axis=1, tiled=True)
-    spare_hidden = lax.all_gather(spare_hidden, "dp", axis=1, tiled=True)
-    home_out = jnp.dot(home_hidden, down_weight[0], preferred_element_type=jnp.float32)
+    rows_own = jnp.dot(pick, first, preferred_element_type=jnp.float32).astype(jnp.bfloat16)
+    rows_other = jnp.dot(pick, second, preferred_element_type=jnp.float32).astype(jnp.bfloat16)
+    rows_other = rows_other.reshape(2 * slot_rows, dp_count - 1, block)
+    home_hidden = gate_up(
+        rows_own[:slot_rows, :block], rows_other[:slot_rows], gate_up_weight[0], dp_me, order
+    )
+    spare_hidden = gate_up(
+        rows_own[slot_rows:, :block], rows_other[slot_rows:], spare_gate_up[0], dp_me, order
+    )
+    home_units = home_hidden.shape[1]
+    hidden = lax.all_gather(
+        jnp.concatenate([home_hidden, spare_hidden], axis=1), "dp", axis=1, tiled=True
+    ).reshape(slot_rows, dp_count, -1)
+    home_out = jnp.einsum(
+        "rdf,dfe->re",
+        hidden[:, :, :home_units],
+        down_weight[0].reshape(dp_count, home_units, -1),
+        preferred_element_type=jnp.float32,
+    )
     home_out = home_out.astype(jnp.bfloat16)
-    spare_out = jnp.dot(spare_hidden, spare_down[0], preferred_element_type=jnp.float32)
+    spare_out = jnp.einsum(
+        "rdf,dfe->re",
+        hidden[:, :, home_units:],
+        spare_down[0].reshape(dp_count, -1, spare_down.shape[2]),
+        preferred_element_type=jnp.float32,
+    )
     spare_high = spare_out.astype(jnp.bfloat16)
     spare_low = (spare_out - spare_high.astype(jnp.float32)).astype(jnp.bfloat16)
 

time: 240 us -> 254 us (1.058)
  local copies, waits for them, and re-layouts: 4.81 us -> 35.1 us
  blocking collectives: 21.6 us -> 10.2 us
  waiting for transfers between devices: 144 us -> 136 us
  matrix products: 40.5 us -> 45.9 us
  other arithmetic: 14.8 us -> 12.1 us
    unnamed x11 -> x21, local copies, waits for them, and re-layouts: 0.13 us -> 24.5 us
    all_gather x2 -> x1, blocking collectives: 21.6 us -> 10.2 us  [per_device(): blocks = lax.all_gather(tokens, 'dp', axis=0)]
    all_gather x2 -> x3, waiting for transfers between devices: 71.9 us -> 62.8 us  [the longest x1 31.6 us: per_device(): second = lax.all_gather(others, 'ep', axis=0, tiled=True)]
    gather x0 -> x2, local copies, waits for them, and re-layouts: none -> 5.91 us  [gate_up(): jnp.take(blocks, order, axis=0)]
    dot_general x4 -> x7, matrix products: 23.2 us -> 28.5 us  [the longest x1 7.96 us: per_device(): jnp.dot(pick, first, preferred_element_type=jnp.float32)]
    convert_element_type x2, other arithmetic: 3.19 us -> 0.48 us  [gate_up(): (jax.nn.silu(gate_both[:, 0, :]) * gate_both[:, 1, :]).astype(jnp.bfloat16)]
  transfers between devices with their start and end apart: 3 -> 4, of which waited for: 3 -> 4; matrix products, arithmetic and copies ran while one was open for 6% -> 22% of each run, Pallas kernels for 0% -> 0%
where the time goes in v4:
time: 254 us
  waiting for transfers between devices  136 us (54%)
  matrix products  45.9 us (18%)
  local copies, waits for them, and re-layouts  35.1 us (14%)
  between operations  14.5 us (6%)
  other arithmetic  12.1 us (5%)
  blocking collectives  10.2 us (4%)
    reduce_scatter x1, waiting for transfers between devices, per_device(): lax.psum_scatter(partial.astype(jnp.bfloat16), 'ep', scatter_dimension=0,...  72.9 us
    all_gather x1, waiting for transfers between devices, per_device(): second = lax.all_gather(others, 'ep', axis=0, tiled=True)  31.6 us
    unnamed x21, local copies, waits for them, and re-layouts  24.5 us
    all_gather x1, waiting for transfers between devices, per_device(): lax.all_gather(jnp.concatenate([home_hidden, spare_hidden], axis=1), 'dp'...  21.4 us
    all_gather x1, blocking collectives, per_device(): blocks = lax.all_gather(tokens, 'dp', axis=0)  10.2 us
    all_gather x1, waiting for transfers between devices, per_device(): first = lax.all_gather(own_columns, 'ep', axis=0, tiled=True)  9.68 us
    dot_general x1, matrix products, per_device(): home_term = jnp.dot(home_pick, home_out, preferred_element_type=jnp.float32)  9.35 us
    dot_general x1, matrix products, per_device(): jnp.dot(pick, first, preferred_element_type=jnp.float32)  7.96 us
  transfers between devices with their start and end apart: 4, of which 4 were waited for; matrix products, arithmetic and copies ran while one was open for 22% of the time, Pallas kernels for 0%

profile of v4, /device:TPU:0, one launch (start us, length us, event | category | flops | bytes accessed | tf_op | source)
XLA Modules:
  0.0 253.7 jit_solution(15969460563746020169)
XLA Ops:
  6.5 0.0 copy-start
  6.5 0.0 all-gather.6.cloned.1.call-start
  6.5 0.8 convert_element_type.66
  7.4 0.8 fusion.69
  8.2 0.1 copy.46
  8.3 1.7 fusion.55
  10.0 0.0 all-gather.6.cloned.1.call-update
  10.0 0.0 all-gather.10.cloned.1.call-start
  10.1 10.2 %all-gather = bf16[128,2048]{1,0:T(8,128)(2,1)S(1)} all-gather(bf16[64,2048]{1,0:T(8,128)(2,1)} %param.9), channel_id=2, replica_groups=mesh['ep'=16,'dp'=2] {'dp'}, dimensions={0}, use_global_device_ids=true | all-gather | bytes 786432 | tf_op jit(solution)/shard_map/all_gather | solution.py:87
  20.3 0.7 dynamic-slice_select_fusion
  21.0 0.0 all-gather.10.cloned.1.call-update
  21.0 0.0 all-gather.8.cloned.1.call-start
  21.1 1.2 dynamic_slice.12
  22.3 1.3 dynamic_slice.13
  23.6 2.7 %copy.37 = bf16[1,4096,2,256]{3,1,2,0:T(8,128)(2,1)S(1)} copy(bf16[1,4096,2,256]{3,2,1,0:T(2,128)(2,1)} %param.16) | data formatting | bytes 8388608 | tf_op args[7]
  26.3 1.9 copy-done.1
  28.3 1.5 constant_dynamic-slice_fusion
  29.8 4.0 %copy.43 = bf16[1,2048,2,256]{1,3,2,0:T(8,128)(2,1)} copy(bf16[1,2048,2,256]{3,1,0,2:T(8,128)(2,1)} %constant_dynamic-slice_fusion) | data formatting | bytes 4194304
  33.8 8.1 %copy.34 = bf16[1,4096,2,512]{3,1,2,0:T(8,128)(2,1)} copy(bf16[1,4096,2,512]{3,2,1,0:T(2,128)(2,1)} %param.14) | data formatting | bytes 16777216 | tf_op args[5]
  41.8 4.4 %constant_dynamic-slice_fusion.1 = bf16[1,2048,2,512]{3,1,0,2:T(8,128)(2,1)} fusion(bf16[2,2048,2,512]{3,1,0,2:T(8,128)(2,1)} %bitcast.86, s32[]{:T(128)} %bitcast.8), kind=kLoop, calls=%fused_computation.102 | loop fusion | bytes 8388612 | tf_op jit(solution)/shard_map/jit(_take)/gather | solution.py:14
  46.2 6.4 %copy.42 = bf16[1,2048,2,512]{1,3,2,0:T(8,128)(2,1)} copy(bf16[1,2048,2,512]{3,1,0,2:T(8,128)(2,1)} %constant_dynamic-slice_fusion.1) | data formatting | bytes 8388608
  52.6 0.6 fusion.62
  53.8 0.6 compare_reduce_fusion
  55.0 0.1 broadcast_add_fusion
  55.1 9.7 %all-gather.6.cloned.1.call-done = bf16[1024,2176]{1,0:T(8,128)(2,1)} async-done(((bf16[64,2176]{1,0:T(8,128)(2,1)}), bf16[1024,2176]{1,0:T(8,128)(2,1)}) %all-gather.6.cloned.1.call-update) | async-done | bytes 4456464 | tf_op jit(solution)/shard_map/all_gather | solution.py:86
  64.8 1.7 convert_compare_fusion
  66.5 0.3 eq.104
  66.8 0.3 eq.93
  67.2 0.3 compare_and_fusion.1
  67.5 0.9 compare_and_fusion
  68.4 0.6 select_reduce_fusion.1
  69.0 0.1 reshape.156
  69.1 0.1 reshape.157
  69.2 8.0 %convolution_convert_fusion = bf16[1024,2176]{1,0:T(8,128)(2,1)S(1)} fusion(bf16[1024,2176]{1,0:T(8,128)(2,1)} %all-gather.6.cloned.1.call-done, s32[1024]{0:T(1024)S(1)} %pad_add_fusion), kind=kOutput, calls=%fused_computation.1 | convolution fusion | flops 4566679552 | bytes 8916992 | tf_op jit(solution)/shard_map/dot_general | solution.py:116
  77.2 1.3 fusion.21
  78.5 6.0 %fusion.4 = f32[512,2,512]{0,2,1:T(8,128)} fusion(bf16[2,2048,2,512]{3,1,0,2:T(8,128)(2,1)} %bitcast.87, s32[]{:T(128)S(6)} %select_n.117, bf16[1024,2176]{1,0:T(8,128)(2,1)S(1)} %convolution_convert_fusion), kind=kOutput, calls=%fused_computation.6 | convolution fusion | flops 2147483648 | bytes 8388612 | tf_op jit(solution)/shard_map/rd,djf->rjf/dot_general | solution.py:10
  84.4 31.6 %all-gather.10.cloned.1.call-done = bf16[1,1024,2048]{2,1,0:T(8,128)(2,1)} async-done(((bf16[1,64,2048]{2,1,0:T(8,128)(2,1)}), bf16[1,1024,2048]{2,1,0:T(8,128)(2,1)}) %all-gather.10.cloned.1.call-update) | async-done | bytes 4194320 | tf_op jit(solution)/shard_map/all_gather | solution.py:90
  116.1 7.2 %fusion.17 = bf16[1024,2048]{1,0:T(8,128)(2,1)S(1)} fusion(bf16[1,1024,2048]{2,1,0:T(8,128)(2,1)} %all-gather.10.cloned.1.call-done, s32[1024]{0:T(1024)S(1)} %pad_add_fusion), kind=kOutput, calls=%fused_computation.23 | convolution fusion | flops 4298113024 | bytes 8392704 | tf_op jit(solution)/shard_map/dot_general | solution.py:117
  123.3 1.4 fusion.33
  124.7 0.2 fusion.50
  124.9 0.6 copy-done.3
  125.5 0.7 copy-done.7
  126.2 2.4 fusion.30
  128.6 0.3 fusion.39
  128.9 0.9 pad_maximum_fusion
  129.8 0.0 all-gather.8.cloned.1.call-update
  129.8 0.0 reduce-scatter.2.cloned.1.call-start
  129.9 0.4 reshape.159
  130.3 0.4 reshape.154
  130.6 0.1 broadcast_add_fusion.2
  130.7 0.3 reshape.155
  131.0 0.3 reshape.160
  131.3 0.2 select_reduce_fusion.4
  131.6 0.2 select_reduce_fusion.2
  131.8 1.1 slice_convert_fusion
  132.9 0.5 fusion.67
  133.4 0.5 select_reduce_fusion.5
  133.9 0.4 iota_compare_fusion.5
  134.3 21.4 %all-gather.8.cloned.1.call-done = bf16[512,1536]{0,1:T(8,128)(2,1)} async-done(((bf16[512,768]{0,1:T(8,128)(2,1)}), bf16[512,1536]{0,1:T(8,128)(2,1)}) %all-gather.8.cloned.1.call-update) | async-done | bytes 1572880 | tf_op jit(solution)/shard_map/all_gather | solution.py:126
  155.7 2.3 fusion.6
  158.1 6.9 %fusion = f32[1024,2048]{1,0:T(8,128)} fusion(bf16[512,2048]{1,0:T(8,128)(2,1)S(1)} %get-tuple-element.44, bf16[512,2048]{1,0:T(8,128)(2,1)S(1)} %get-tuple-element.45, pred[1024,512]{1,0:T(32,128)(4,1)S(1)} %iota_compare_fusion.5), kind=kOutput, calls=%fused_computation.2 | convolution fusion | flops 4304404480 | bytes 13107200 | tf_op jit(solution)/shard_map/dot_general | solution.py:150
  165.0 9.3 %add_convert_fusion = bf16[1024,2048]{1,0:T(8,128)(2,1)} fusion(f32[1024,2048]{1,0:T(8,128)} %fusion, f32[1024]{0:T(1024)S(1)} %get-tuple-element.39, f32[1024]{0:T(1024)S(1)} %get-tuple-element.38, s32[1024]{0:T(1024)S(1)} %select_reduce_fusion.4, bf16[2,512,2048]{2,1,0:T(8,128)(2,1)} %bitcast.91, bf16[512,2,768]{0,2,1:T(8,128)(2,1)} %bitcast.93), kind=kOutput, calls=%fused_computation | convolution fusion | flops 4304928768 | bytes 17838080 | tf_op jit(solution)/shard_map/dot_general | solution.py:149
  174.3 0.0 reduce-scatter.2.cloned.1.call-update
  174.3 72.9 %reduce-scatter.2.cloned.1.call-done = bf16[64,2048]{1,0:T(8,128)(2,1)} async-done(((bf16[1024,2048]{1,0:T(8,128)(2,1)}), bf16[64,2048]{1,0:T(8,128)(2,1)}) %reduce-scatter.2.cloned.1.call-update) | async-done | bytes 262160 | tf_op jit(solution)/shard_map/reduce_scatter | solution.py:156
  (17 shorter events, 0.1 us)
Async XLA Ops:
  6.5 149.2 %copy-start = (bf16[1,512,2048]{2,1,0:T(8,128)(2,1)S(1)}, bf16[1,512,2048]{2,1,0:T(8,128)(2,1)}, u32[]{:S(2)}) copy-start(bf16[1,512,2048]{2,1,0:T(8,128)(2,1)} %param.17) | copy-start | bytes 6291460
  6.5 58.3 %all-gather.6.cloned.1.call-start = ((), (), s32[]{:S(2)}) async-start(), calls=%async_computation.1 | async-start | bytes 4734976 | tf_op jit(solution)/shard_map/all_gather | solution.py:86
  10.0 106.1 %all-gather.10.cloned.1.call-start = ((), (), s32[]{:S(2)}) async-start(), calls=%async_computation.4 | async-start | bytes 4456448 | tf_op jit(solution)/shard_map/all_gather | solution.py:90
  21.0 134.7 %all-gather.8.cloned.1.call-start = ((), (), s32[]{:S(2)}) async-start(), calls=%async_computation.2 | async-start | bytes 2359296 | tf_op jit(solution)/shard_map/all_gather | solution.py:126
  26.3 1.9 copy-start.1
  46.2 6.4 %copy-start.5 = (s32[8]{0:T(128)S(1)}, s32[8]{0:T(128)}, u32[]{:S(2)}) copy-start(s32[8]{0:T(128)} %param.13) | copy-start | bytes 100
  46.2 6.4 %copy-start.6 = (s32[8]{0:T(128)S(1)}, s32[8]{0:T(128)}, u32[]{:S(2)}) copy-start(s32[8]{0:T(128)} %param.12) | copy-start | bytes 100
  69.2 8.0 %copy-start.2 = (bf16[1,4096,2,256]{3,1,2,0:T(8,128)(2,1)S(1)}, bf16[1,4096,2,256]{3,1,2,0:T(8,128)(2,1)}, u32[]{:S(2)}) copy-start(bf16[1,4096,2,256]{3,1,2,0:T(8,128)(2,1)} %copy-done.1) | copy-start | bytes 12582916
  116.1 7.2 %copy-start.4 = (bf16[1,2048,2,256]{1,3,2,0:T(8,128)(2,1)S(1)}, bf16[1,2048,2,256]{1,3,2,0:T(8,128)(2,1)}, u32[]{:S(2)}) copy-start(bf16[1,2048,2,256]{1,3,2,0:T(8,128)(2,1)} %copy.43) | copy-start | bytes 6291460
  123.3 2.2 copy-start.3
  123.3 2.9 %copy-start.7 = (f32[512,2,512]{0,2,1:T(8,128)S(1)}, f32[512,2,512]{0,2,1:T(8,128)}, u32[]{:S(2)}) copy-start(f32[512,2,512]{0,2,1:T(8,128)} %fusion.4) | copy-start | bytes 6291460
  129.8 117.4 %reduce-scatter.2.cloned.1.call-start = ((), (), s32[]{:S(2)}) async-start(), calls=%async_computation.3 | async-start | bytes 4456448 | tf_op jit(solution)/shard_map/reduce_scatter | solution.py:156
Sparse Core Ops, SparseCore 0:
  10.1 54.6 all-gather.5
  67.0 49.0 all-gather.9
  130.0 25.7 all-gather.7
  174.5 72.7 reduce-scatter.1

commit v5 on v3

--- a/solution.py
+++ b/solution.py
@@ -51,6 +51,16 @@
     return jnp.pad(columns, ((0, 0), (0, width)))
 
 
+def gather_dp(block, axis):
+    if lax.axis_size("dp") != 2:
+        return lax.all_gather(block, "dp", axis=axis, tiled=True)
+    partner = lax.ppermute(block, "dp", perm=[(0, 1), (1, 0)])
+    first = lax.axis_index("dp") == 0
+    low = jnp.where(first, block, partner)
+    high = jnp.where(first, partner, block)
+    return jnp.concatenate([low, high], axis=axis)
+
+
 def per_device(
     tokens,
     expert_ids,
@@ -72,7 +82,7 @@
     per_group = group_tokens * top_count
 
     d_model = tokens.shape[1] * lax.axis_size("dp")
-    whole_rows = lax.all_gather(tokens, "dp", axis=1, tiled=True)
+    whole_rows = gather_dp(tokens, 1)
     packed = jnp.concatenate([whole_rows, side_columns(expert_ids, gate_logits)], axis=1)
     every_row = lax.all_gather(packed, "ep", axis=0, tiled=True)
     all_tokens = every_row.shape[0]
@@ -104,7 +114,7 @@
     home_hidden = gate_up(rows[:slot_rows, :d_model], gate_up_weight[0])
     spare_hidden = gate_up(rows[slot_rows:, :d_model], spare_gate_up[0])
     home_hidden = lax.all_gather(home_hidden, "dp", axis=1, tiled=True)
-    spare_hidden = lax.all_gather(spare_hidden, "dp", axis=1, tiled=True)
+    spare_hidden = gather_dp(spare_hidden, 1)
     home_out = jnp.dot(home_hidden, down_weight[0], preferred_element_type=jnp.float32)
     home_out = home_out.astype(jnp.bfloat16)
     spare_out = jnp.dot(spare_hidden, spare_down[0], preferred_element_type=jnp.float32)

time: 240 us -> 242 us (level)
  blocking collectives: 21.6 us -> 0 us
  waiting for transfers between devices: 144 us -> 158 us
  starting transfers between devices: 0.09 us -> 4.75 us
  other arithmetic: 14.8 us -> 18.5 us
    all_gather x2 -> x0, blocking collectives: 21.6 us -> none  [the longest x1 11.4 us: per_device(): spare_hidden = lax.all_gather(spare_hidden, 'dp', axis=1, tiled=True)]
    ppermute x0 -> x2, waiting for transfers between devices: none -> 7.54 us  [gather_dp(): partner = lax.ppermute(block, 'dp', perm=[(0, 1), (1, 0)])]
    all_gather x1, waiting for transfers between devices: 0.52 us -> 6.43 us  [per_device(): home_hidden = lax.all_gather(home_hidden, 'dp', axis=1, tiled=True)]
    ppermute x0 -> x2, starting transfers between devices: none -> 4.44 us  [gather_dp(): partner = lax.ppermute(block, 'dp', perm=[(0, 1), (1, 0)])]
  transfers between devices with their start and end apart: 3 -> 5, of which waited for: 3 -> 5; matrix products, arithmetic and copies ran while one was open for 6% -> 8% of each run, Pallas kernels for 0% -> 0%
where the time goes in v5:
time: 242 us
  waiting for transfers between devices  158 us (65%)
  matrix products  39.4 us (16%)
  other arithmetic  18.5 us (8%)
  between operations  14.7 us (6%)
  local copies, waits for them, and re-layouts  6.48 us (3%)
  starting transfers between devices  4.75 us (2%)
    reduce_scatter x1, waiting for transfers between devices, per_device(): lax.psum_scatter(partial.astype(jnp.bfloat16), 'ep', scatter_dimension=0,...  72.5 us
    all_gather x1, waiting for transfers between devices, per_device(): every_row = lax.all_gather(packed, 'ep', axis=0, tiled=True)  71.4 us
    dot_general x1, matrix products, per_device(): jnp.dot(pick, every_row, preferred_element_type=jnp.float32)  14.2 us
    dot_general x1, matrix products, per_device(): home_term = jnp.dot(home_pick, home_out, preferred_element_type=jnp.float32)  9.31 us
    ppermute x2, waiting for transfers between devices, gather_dp(): partner = lax.ppermute(block, 'dp', perm=[(0, 1), (1, 0)])  7.54 us
    dot_general x2, matrix products, gate_up(): jnp.einsum('rd,djf->rjf', row_block, weight, preferred_element_type=jnp.f...  6.85 us
    dot_general x1, matrix products, per_device(): jnp.dot(jnp.concatenate([spare_pick, spare_pick], axis=1), jnp.concatenat...  6.68 us
    all_gather x1, waiting for transfers between devices, per_device(): home_hidden = lax.all_gather(home_hidden, 'dp', axis=1, tiled=True)  6.43 us
  transfers between devices with their start and end apart: 5, of which 5 were waited for; matrix products, arithmetic and copies ran while one was open for 8% of the time, Pallas kernels for 0%

profile of v5, /device:TPU:0, one launch (start us, length us, event | category | flops | bytes accessed | tf_op | source)
XLA Modules:
  0.0 241.8 jit_solution(6790626181531272970)
XLA Ops:
  6.5 0.0 copy-start
  6.5 0.0 all-gather.3.cloned.1.call-start
  6.5 3.0 %collective-permute-start = (bf16[64,2048]{1,0:T(8,128)(2,1)}, bf16[64,2048]{1,0:T(8,128)(2,1)S(1)}, u32[]{:S(2)}, u32[]{:S(2)}) collective-permute-start(bf16[64,2048]{1,0:T(8,128)(2,1)} %param.9), channel_id=1, source_target_pairs={{0,1},{1,0},{2,3},{3,2},{4,5},{5,4},{6,7},{7,6},{8,9},{9,8},{10,11... | collective-permute-start | bytes 786440 | tf_op jit(solution)/shard_map/ppermute | solution.py:57
  9.5 0.7 convert_element_type.63
  10.2 0.8 fusion.48
  11.0 0.1 copy.26
  11.1 4.9 %collective-permute-done = bf16[64,2048]{1,0:T(8,128)(2,1)S(1)} collective-permute-done((bf16[64,2048]{1,0:T(8,128)(2,1)}, bf16[64,2048]{1,0:T(8,128)(2,1)S(1)}, u32[]{:S(2)}, u32[]{:S(2)}) %collective-permute-start) | collective-permute-done | bytes 262176 | tf_op jit(solution)/shard_map/ppermute | solution.py:57
  16.0 1.0 broadcast_select_fusion.3
  17.0 0.9 fusion.28
  17.9 0.0 all-gather.3.cloned.1.call-update
  17.9 0.0 all-gather.5.cloned.1.call-start
  18.0 1.2 dynamic_slice.6
  19.2 1.3 dynamic_slice.7
  20.5 1.4 fusion.42
  22.6 1.4 compare_reduce_fusion
  24.7 0.1 broadcast_add_fusion
  24.8 71.4 %all-gather.3.cloned.1.call-done = bf16[1024,4224]{1,0:T(8,128)(2,1)} async-done(((bf16[64,4224]{1,0:T(8,128)(2,1)}), bf16[1024,4224]{1,0:T(8,128)(2,1)}) %all-gather.3.cloned.1.call-update) | async-done | bytes 8650768 | tf_op jit(solution)/shard_map/all_gather | solution.py:87
  96.1 1.8 convert_compare_fusion
  97.9 0.3 eq.107
  98.3 0.3 eq.96
  98.6 0.9 compare_and_fusion
  99.5 0.4 reshape.111
  99.9 0.3 compare_and_fusion.1
  100.1 0.4 reshape.107
  100.5 0.6 select_reduce_fusion.1
  101.1 0.1 broadcast_add_fusion.2
  101.2 0.1 reshape.109
  101.3 0.1 reshape.110
  101.4 1.1 reshape.108
  102.5 1.2 reshape.112
  103.7 1.1 slice_convert_fusion
  104.7 0.0 slice-start
  104.8 1.1 fusion.46
  105.9 0.0 copy-start.1
  105.9 0.0 slice-start.1
  105.9 14.2 %convolution_convert_fusion = bf16[1024,4224]{1,0:T(8,128)(2,1)S(1)} fusion(bf16[1024,4224]{1,0:T(8,128)(2,1)} %all-gather.3.cloned.1.call-done, s32[1024]{0:T(1024)S(1)} %pad_add_fusion), kind=kOutput, calls=%fused_computation | convolution fusion | flops 8863744000 | bytes 17305600 | tf_op jit(solution)/shard_map/dot_general | solution.py:113
  120.1 0.0 copy-done.1
  120.1 2.4 fusion.2
  122.5 0.0 slice-done
  122.5 0.0 slice-done.1
  122.5 4.5 %fusion = f32[512,2,512]{2,0,1:T(8,128)S(1)} fusion(bf16[4096,2,512]{2,1,0:T(2,128)(2,1)S(1)} %bitcast.52, bf16[1024,4224]{1,0:T(8,128)(2,1)S(1)} %convolution_convert_fusion), kind=kOutput, calls=%fused_computation.1 | convolution fusion | flops 4294967296 | bytes 14680064 | tf_op jit(solution)/shard_map/rd,djf->rjf/dot_general | solution.py:8
  127.0 1.2 fusion.22
  128.2 0.9 fusion.30
  129.0 1.5 collective-permute-start.1
  130.5 1.2 select_reduce_fusion.4
  131.8 1.5 select_reduce_fusion.5
  133.3 1.3 select_reduce_fusion.2
  134.6 0.0 all-gather.5.cloned.1.call-update
  134.6 0.3 reduce-scatter.2.cloned.1.call-start
  134.9 0.4 iota_compare_fusion.2
  135.2 2.6 %collective-permute-done.1 = bf16[512,256]{0,1:T(8,128)(2,1)} collective-permute-done((bf16[512,256]{0,1:T(8,128)(2,1)}, bf16[512,256]{0,1:T(8,128)(2,1)}, u32[]{:S(2)}, u32[]{:S(2)}) %collective-permute-start.1) | collective-permute-done | bytes 262176 | tf_op jit(solution)/shard_map/ppermute | solution.py:57
  137.8 1.2 broadcast_select_fusion.1
  139.0 0.0 copy-done
  139.0 1.3 subtract_convert_fusion
  140.3 6.7 %fusion.3 = f32[1024,2048]{1,0:T(8,128)} fusion(bf16[512,2048]{1,0:T(8,128)(2,1)S(1)} %get-tuple-element.11, bf16[512,2048]{1,0:T(8,128)(2,1)S(1)} %get-tuple-element.12, pred[1024,512]{1,0:T(32,128)(4,1)S(1)} %iota_compare_fusion.2), kind=kOutput, calls=%fused_computation.7 | convolution fusion | flops 4304404480 | bytes 13107200 | tf_op jit(solution)/shard_map/dot_general | solution.py:129
  147.0 6.4 %all-gather.5.cloned.1.call-done = bf16[512,1024]{1,0:T(8,128)(2,1)} async-done(((bf16[512,512]{1,0:T(8,128)(2,1)}), bf16[512,1024]{1,0:T(8,128)(2,1)}) %all-gather.5.cloned.1.call-update) | async-done | bytes 1048592 | tf_op jit(solution)/shard_map/all_gather | solution.py:116
  153.4 9.3 %add_convert_fusion = bf16[1024,2048]{1,0:T(8,128)(2,1)} fusion(f32[1024,2048]{1,0:T(8,128)} %fusion.3, f32[1024]{0:T(1024)S(1)} %get-tuple-element.6, f32[1024]{0:T(1024)S(1)} %get-tuple-element.5, s32[1024]{0:T(1024)S(1)} %select_reduce_fusion.4, bf16[512,1024]{1,0:T(8,128)(2,1)} %all-gather.5.cloned.1.call-done, bf16[1,1024,2048]{2,1,0:T(8,128)(2,1)} %param.15), kind=kOutput, calls=%fused_computation.3 | convolution fusion | flops 4304928768 | bytes 17838080 | tf_op jit(solution)/shard_map/dot_general | solution.py:128
  162.7 0.0 reduce-scatter.2.cloned.1.call-update
  162.7 72.5 %reduce-scatter.2.cloned.1.call-done = bf16[64,2048]{1,0:T(8,128)(2,1)} async-done(((bf16[1024,2048]{1,0:T(8,128)(2,1)}), bf16[64,2048]{1,0:T(8,128)(2,1)}) %reduce-scatter.2.cloned.1.call-update) | async-done | bytes 262160 | tf_op jit(solution)/shard_map/reduce_scatter | solution.py:135
  (6 shorter events, 0.0 us)
Async XLA Ops:
  6.5 132.5 %copy-start = (bf16[1,512,2048]{2,1,0:T(8,128)(2,1)S(1)}, bf16[1,512,2048]{2,1,0:T(8,128)(2,1)}, u32[]{:S(2)}) copy-start(bf16[1,512,2048]{2,1,0:T(8,128)(2,1)} %param.17) | copy-start | bytes 6291460
  6.5 89.6 %all-gather.3.cloned.1.call-start = ((), (), s32[]{:S(2)}) async-start(), calls=%async_computation.1 | async-start | bytes 9191424 | tf_op jit(solution)/shard_map/all_gather | solution.py:87
  6.5 9.5 %collective-permute-start = (bf16[64,2048]{1,0:T(8,128)(2,1)}, bf16[64,2048]{1,0:T(8,128)(2,1)S(1)}, u32[]{:S(2)}, u32[]{:S(2)}) collective-permute-start(bf16[64,2048]{1,0:T(8,128)(2,1)} %param.9), channel_id=1, source_target_pairs={{0,1},{1,0},{2,3},{3,2},{4,5},{5,4},{6,7},{7,6},{8,9},{9,8},{10,11... | collective-permute-start | bytes 786440 | tf_op jit(solution)/shard_map/ppermute | solution.py:57
  17.9 135.5 %all-gather.5.cloned.1.call-start = ((), (), s32[]{:S(2)}) async-start(), calls=%async_computation.2 | async-start | bytes 1572864 | tf_op jit(solution)/shard_map/all_gather | solution.py:116
  104.7 17.7 %slice-start = ((s8[8388608]{0:T(1024)(128)(4,1)}), s8[4194304]{0:T(1024)(128)(4,1)S(1)}, s32[]{:S(2)}) async-start(s8[8388608]{0:T(1024)(128)(4,1)} %bitcast.50), calls=%async_computation.4 | async-start | bytes 8388608
  105.9 14.2 %copy-start.1 = (bf16[1,4096,2,256]{3,2,1,0:T(2,128)(2,1)S(1)}, bf16[1,4096,2,256]{3,2,1,0:T(2,128)(2,1)}, u32[]{:S(2)}) copy-start(bf16[1,4096,2,256]{3,2,1,0:T(2,128)(2,1)} %param.16) | copy-start | bytes 12582916
  105.9 16.6 %slice-start.1 = ((s8[8388608]{0:T(1024)(128)(4,1)}), s8[4194304]{0:T(1024)(128)(4,1)S(1)}, s32[]{:S(2)}) async-start(s8[8388608]{0:T(1024)(128)(4,1)} %bitcast.50), calls=%async_computation.5 | async-start | bytes 8388608
  129.0 8.8 %collective-permute-start.1 = (bf16[512,256]{0,1:T(8,128)(2,1)}, bf16[512,256]{0,1:T(8,128)(2,1)}, u32[]{:S(2)}, u32[]{:S(2)}) collective-permute-start(bf16[512,256]{0,1:T(8,128)(2,1)} %fusion.30), channel_id=1, source_target_pairs={{0,1},{1,0},{2,3},{3,2},{4,5},{5,4},{6,7},{7,6},{8,9},{9,8},{10,11... | collective-permute-start | bytes 786440 | tf_op jit(solution)/shard_map/ppermute | solution.py:57
  134.6 100.7 %reduce-scatter.2.cloned.1.call-start = ((), (), s32[]{:S(2)}) async-start(), calls=%async_computation.3 | async-start | bytes 4456448 | tf_op jit(solution)/shard_map/reduce_scatter | solution.py:135
Sparse Core Ops, SparseCore 0:
  18.0 78.0 all-gather.2
  134.7 18.6 all-gather.4
  162.9 72.3 reduce-scatter.1

commit v6 on v5

--- a/solution.py
+++ b/solution.py
@@ -9,8 +9,9 @@
     return (jax.nn.silu(gate_both[:, 0, :]) * gate_both[:, 1, :]).astype(jnp.bfloat16)
 
 
-def slot_tables(ids, target, low, limit, capacity, top_count):
+def slot_tables(ids, target, low, limit, capacity, top_count, gate_weight):
     groups, per_group = ids.shape
+    group_tokens = per_group // top_count
     hit = ids == target
     ordinal = jnp.arange(per_group, dtype=jnp.int32)
     earlier = (ordinal[None, :] < ordinal[:, None]).astype(jnp.bfloat16)
@@ -19,26 +20,14 @@
     ).astype(jnp.int32)
     position = rank - low
     kept = hit & (position >= 0) & (position < limit)
-    group_tokens = per_group // top_count
-    token = jnp.arange(groups, dtype=jnp.int32)[:, None] * group_tokens + ordinal[None, :] // top_count
     slots = jnp.arange(capacity, dtype=jnp.int32)
     sel = kept[:, :, None] & (position[:, :, None] == slots[None, None, :])
-    row_of_slot = jnp.sum(jnp.where(sel, token[:, :, None], 0), axis=1)
-    flat = jnp.arange(groups, dtype=jnp.int32)[:, None] * capacity + position
-    return row_of_slot.reshape(-1), kept, flat
-
-
-def per_token(kept, flat, weight, group_tokens, top_count):
-    groups = kept.shape[0]
-    kept = kept.reshape(groups * group_tokens, top_count)
-    flat = flat.reshape(groups * group_tokens, top_count)
-    index = jnp.sum(jnp.where(kept, flat, 0), axis=1)
-    scale = jnp.sum(jnp.where(kept, weight, 0.0), axis=1)
-    return index, scale
-
-
-def one_hot(index, size):
-    return (index[:, None] == jnp.arange(size, dtype=jnp.int32)[None, :]).astype(jnp.bfloat16)
+    holds = jnp.any(sel.reshape(groups, group_tokens, top_count, capacity), axis=2)
+    pick = jnp.transpose(holds, (0, 2, 1)).astype(jnp.bfloat16)
+    scale = jnp.sum(
+        jnp.where(kept.reshape(groups * group_tokens, top_count), gate_weight, 0.0), axis=1
+    )
+    return pick, holds.astype(jnp.bfloat16), scale
 
 
 def side_columns(expert_ids, gate_logits):
@@ -100,37 +89,49 @@
     home_limit = jnp.where(
         jnp.any(is_match), jnp.minimum(jnp.sum(jnp.where(is_match, split_rows, 0)), capacity), capacity
     )
-    home_rows_of, home_kept, home_flat = slot_tables(
-        ids, me, 0, home_limit, capacity, top_count
+    home_pick, home_take, home_scale = slot_tables(
+        ids, me, 0, home_limit, capacity, top_count, gate_weight
     )
     spare_index = me // halves
-    spare_rows_of, spare_kept, spare_flat = slot_tables(
-        ids, placement[spare_index], split_rows[spare_index], capacity, capacity, top_count
+    spare_pick, spare_take, spare_scale = slot_tables(
+        ids,
+        placement[spare_index],
+        split_rows[spare_index],
+        capacity,
+        capacity,
+        top_count,
+        gate_weight,
     )
 
-    slot_rows = home_rows_of.shape[0]
-    pick = one_hot(jnp.concatenate([home_rows_of, spare_rows_of]), all_tokens)
-    rows = jnp.dot(pick, every_row, preferred_element_type=jnp.float32).astype(jnp.bfloat16)
-    home_hidden = gate_up(rows[:slot_rows, :d_model], gate_up_weight[0])
-    spare_hidden = gate_up(rows[slot_rows:, :d_model], spare_gate_up[0])
+    grouped = every_row.reshape(ep_count, group_tokens, -1)
+    slot_rows = ep_count * capacity
+    home_rows = jnp.einsum(
+        "gpi,gic->gpc", home_pick, grouped, preferred_element_type=jnp.float32
+    ).astype(jnp.bfloat16).reshape(slot_rows, -1)
+    spare_rows = jnp.einsum(
+        "gpi,gic->gpc", spare_pick, grouped, preferred_element_type=jnp.float32
+    ).astype(jnp.bfloat16).reshape(slot_rows, -1)
+    home_hidden = gate_up(home_rows[:, :d_model], gate_up_weight[0])
+    spare_hidden = gate_up(spare_rows[:, :d_model], spare_gate_up[0])
     home_hidden = lax.all_gather(home_hidden, "dp", axis=1, tiled=True)
     spare_hidden = gather_dp(spare_hidden, 1)
     home_out = jnp.dot(home_hidden, down_weight[0], preferred_element_type=jnp.float32)
-    home_out = home_out.astype(jnp.bfloat16)
+    home_out = home_out.astype(jnp.bfloat16).reshape(ep_count, capacity, -1)
     spare_out = jnp.dot(spare_hidden, spare_down[0], preferred_element_type=jnp.float32)
     spare_high = spare_out.astype(jnp.bfloat16)
     spare_low = (spare_out - spare_high.astype(jnp.float32)).astype(jnp.bfloat16)
+    spare_high = spare_high.reshape(ep_count, capacity, -1)
+    spare_low = spare_low.reshape(ep_count, capacity, -1)
 
-    home_at, home_scale = per_token(home_kept, home_flat, gate_weight, group_tokens, top_count)
-    spare_at, spare_scale = per_token(spare_kept, spare_flat, gate_weight, group_tokens, top_count)
-    home_pick = one_hot(home_at, slot_rows)
-    spare_pick = one_hot(spare_at, slot_rows)
-    home_term = jnp.dot(home_pick, home_out, preferred_element_type=jnp.float32)
-    spare_term = jnp.dot(
-        jnp.concatenate([spare_pick, spare_pick], axis=1),
-        jnp.concatenate([spare_high, spare_low], axis=0),
+    home_term = jnp.einsum(
+        "gip,gpc->gic", home_take, home_out, preferred_element_type=jnp.float32
+    ).reshape(all_tokens, -1)
+    spare_term = jnp.einsum(
+        "gip,gpc->gic",
+        jnp.concatenate([spare_take, spare_take], axis=2),
+        jnp.concatenate([spare_high, spare_low], axis=1),
         preferred_element_type=jnp.float32,
-    )
+    ).reshape(all_tokens, -1)
     partial = home_scale[:, None] * home_term + spare_scale[:, None] * spare_term
     mixed = lax.psum_scatter(partial.astype(jnp.bfloat16), "ep", scatter_dimension=0, tiled=True)
     return mixed.astype(jnp.bfloat16)

time: 242 us -> 239 us (0.988)
  matrix products: 39.4 us -> 31.2 us
    dot_general x3 -> x5, matrix products: 30.2 us -> 18.5 us  [the longest x1 7.08 us: per_device(): jnp.einsum('gpi,gic->gpc', spare_pick, grouped, preferred_element_type=jn...]
    convert_element_type x0 -> x1, other arithmetic: none -> 3.66 us  [per_device(): partial.astype(jnp.bfloat16)]
    dot_general x2, matrix products: 6.85 us -> 10.3 us  [gate_up(): jnp.einsum('rd,djf->rjf', row_block, weight, preferred_element_type=jnp.f...]
    reduce_sum x4 -> x1, other arithmetic: 4.68 us -> 1.54 us  [slot_tables(): jnp.sum(jnp.where(kept.reshape(groups * group_tokens, top_count), gate_we...]
    unnamed x9 -> x15, local copies, waits for them, and re-layouts: 0.12 us -> 3.07 us
    reshape x6 -> x2, local copies, waits for them, and re-layouts: 3.16 us -> 0.7 us  [slot_tables(): kept.reshape(groups * group_tokens, top_count)]
where the time goes in v6:
time: 239 us; the launch traced here: 238 us
  waiting for transfers between devices  160 us (67%)
  matrix products  31.2 us (13%)
  other arithmetic  19.7 us (8%)
  between operations  14.8 us (6%)
  local copies, waits for them, and re-layouts  8.35 us (3%)
  starting transfers between devices  4.53 us (2%)
    reduce_scatter x1, waiting for transfers between devices, per_device(): lax.psum_scatter(partial.astype(jnp.bfloat16), 'ep', scatter_dimension=0,...  72.8 us
    all_gather x1, waiting for transfers between devices, per_device(): every_row = lax.all_gather(packed, 'ep', axis=0, tiled=True)  71.5 us
    dot_general x2, matrix products, gate_up(): jnp.einsum('rd,djf->rjf', row_block, weight, preferred_element_type=jnp.f...  10.3 us
    all_gather x1, waiting for transfers between devices, per_device(): home_hidden = lax.all_gather(home_hidden, 'dp', axis=1, tiled=True)  8.16 us
    ppermute x2, waiting for transfers between devices, gather_dp(): partner = lax.ppermute(block, 'dp', perm=[(0, 1), (1, 0)])  7.28 us
    dot_general x1, matrix products, per_device(): jnp.einsum('gpi,gic->gpc', spare_pick, grouped, preferred_element_type=jn...  7.08 us
    dot_general x1, matrix products, per_device(): jnp.dot(home_hidden, down_weight[0], preferred_element_type=jnp.float32)  4.85 us
  transfers between devices with their start and end apart: 5, of which 5 were waited for; matrix products, arithmetic and copies ran while one was open for 8% of the time, Pallas kernels for 0%

profile of v6, /device:TPU:0, one launch (start us, length us, event | category | flops | bytes accessed | tf_op | source)
XLA Modules:
  0.0 238.4 jit_solution(13176321242135439198)
XLA Ops:
  6.5 3.0 %collective-permute-start = (bf16[64,2048]{1,0:T(8,128)(2,1)}, bf16[64,2048]{1,0:T(8,128)(2,1)S(1)}, u32[]{:S(2)}, u32[]{:S(2)}) collective-permute-start(bf16[64,2048]{1,0:T(8,128)(2,1)} %param.9), channel_id=1, source_target_pairs={{0,1},{1,0},{2,3},{3,2},{4,5},{5,4},{6,7},{7,6},{8,9},{9,8},{10,11... | collective-permute-start | bytes 786440 | tf_op jit(solution)/shard_map/ppermute | solution.py:46
  9.5 0.7 convert_element_type.67
  10.2 0.8 fusion.45
  11.0 0.1 copy.56
  11.1 4.9 %collective-permute-done = bf16[64,2048]{1,0:T(8,128)(2,1)S(1)} collective-permute-done((bf16[64,2048]{1,0:T(8,128)(2,1)}, bf16[64,2048]{1,0:T(8,128)(2,1)S(1)}, u32[]{:S(2)}, u32[]{:S(2)}) %collective-permute-start) | collective-permute-done | bytes 262176 | tf_op jit(solution)/shard_map/ppermute | solution.py:46
  16.0 1.0 broadcast_select_fusion.3
  17.0 0.9 fusion.25
  17.9 0.0 all-gather.3.cloned.1.call-update
  17.9 0.0 all-gather.5.cloned.1.call-start
  18.0 1.2 dynamic_slice.6
  19.3 1.2 dynamic_slice.7
  20.5 1.4 fusion.39
  22.6 1.4 compare_reduce_fusion
  24.6 71.5 %all-gather.3.cloned.1.call-done = bf16[1024,4224]{1,0:T(8,128)(2,1)} async-done(((bf16[64,4224]{1,0:T(8,128)(2,1)}), bf16[1024,4224]{1,0:T(8,128)(2,1)}) %all-gather.3.cloned.1.call-update) | async-done | bytes 8650768 | tf_op jit(solution)/shard_map/all_gather | solution.py:76
  96.2 1.8 convert_compare_fusion.1
  97.9 0.3 eq.63
  98.3 0.3 eq.72
  98.6 0.3 compare_and_fusion.1
  98.9 0.2 copy.44
  99.1 0.2 copy.45
  99.3 0.8 compare_and_fusion
  100.1 0.2 copy.49
  100.3 0.2 copy.50
  100.4 0.1 copy.46
  100.6 0.1 copy.47
  100.7 0.1 copy.51
  100.8 0.1 copy.52
  101.0 0.0 slice-start
  101.0 0.5 fusion.18
  101.5 0.5 fusion.20
  102.0 0.0 slice-start.1
  102.0 0.0 slice-start.2
  102.0 0.0 slice-start.3
  102.0 7.1 %convolution_convert_fusion = bf16[16,32,4224]{2,1,0:T(8,128)(2,1)} fusion(pred[16,64,32]{1,2,0:T(8,128)(4,1)S(1)} %fusion.20, bf16[16,64,4224]{2,1,0:T(8,128)(2,1)} %bitcast.73), kind=kOutput, calls=%fused_computation.6 | convolution fusion | flops 278986752 | bytes 13008896 | tf_op jit(solution)/shard_map/gpi,gic->gpc/dot_general | solution.py:111
  109.1 0.0 slice-done
  109.1 0.0 slice-start.4
  109.1 1.3 convolution_convert_fusion.1
  110.5 0.9 slice-done.4
  111.3 4.5 %fusion.2 = f32[512,2,512]{2,0,1:T(8,128)S(1)} fusion(bf16[4096,2,512]{2,1,0:T(2,128)(2,1)S(1)} %bitcast.88, bf16[512,4224]{1,0:T(8,128)(2,1)S(1)} %bitcast.78), kind=kOutput, calls=%fused_computation.4 | convolution fusion | flops 4294967296 | bytes 14680064 | tf_op jit(solution)/shard_map/rd,djf->rjf/dot_general | solution.py:8
  115.8 1.2 fusion.24
  117.0 5.8 %fusion.4 = f32[512,2,256]{0,2,1:T(8,128)S(1)} fusion(bf16[512,4224]{1,0:T(8,128)(2,1)} %bitcast.77, bf16[4096,2,256]{2,1,0:T(2,128)(2,1)} %bitcast.89), kind=kOutput, calls=%fused_computation.9 | convolution fusion | flops 2147483648 | bytes 9437184 | tf_op jit(solution)/shard_map/rd,djf->rjf/dot_general | solution.py:8
  122.8 0.9 fusion.27
  123.7 1.5 collective-permute-start.1
  125.1 1.1 slice_convert_fusion
  126.2 1.3 fusion.43
  127.6 0.4 reshape.57
  127.9 0.4 reshape.52
  128.3 0.0 all-gather.5.cloned.1.call-update
  128.3 0.0 reduce-scatter.2.cloned.1.call-start
  128.3 1.5 select_reduce_fusion.1
  129.9 0.2 copy.53
  130.1 2.3 collective-permute-done.1
  132.4 1.2 broadcast_select_fusion.1
  133.6 0.0 copy-done
  133.6 1.3 subtract_convert_fusion
  134.9 4.0 %fusion.5 = f32[16,64,2048]{2,1,0:T(8,128)} fusion(bf16[16,32,2048]{2,1,0:T(8,128)(2,1)S(1)} %bitcast.79, bf16[16,32,2048]{2,1,0:T(8,128)(2,1)S(1)} %bitcast.80, pred[16,64,32]{2,1,0:T(32,128)(4,1)S(1)} %copy.53), kind=kOutput, calls=%fused_computation.11 | convolution fusion | flops 276889600 | bytes 12615680 | tf_op jit(solution)/shard_map/gip,gpc->gic/dot_general | solution.py:129
  139.0 8.2 %all-gather.5.cloned.1.call-done = bf16[512,1024]{1,0:T(8,128)(2,1)} async-done(((bf16[512,512]{1,0:T(8,128)(2,1)}), bf16[512,1024]{1,0:T(8,128)(2,1)}) %all-gather.5.cloned.1.call-update) | async-done | bytes 1048592 | tf_op jit(solution)/shard_map/all_gather | solution.py:116
  147.1 4.8 %fusion.12 = bf16[512,2048]{1,0:T(8,128)(2,1)S(1)} fusion(bf16[512,1024]{1,0:T(8,128)(2,1)} %all-gather.5.cloned.1.call-done, bf16[1,1024,2048]{2,1,0:T(8,128)(2,1)} %param.15), kind=kOutput, calls=%fused_computation.19 | convolution fusion | flops 2148532224 | bytes 7340032 | tf_op jit(solution)/shard_map/dot_general | solution.py:118
  152.0 0.0 copy-start.1
  152.0 1.3 fusion.46
  153.3 2.1 copy-done.1
  155.4 3.7 %fusion.1 = bf16[1024,2048]{1,0:T(8,128)(2,1)} fusion(f32[16,64,2048]{2,1,0:T(8,128)S(1)} %copy-done.1, f32[16,64,2048]{2,1,0:T(8,128)S(1)} %fusion.46, f32[1024]{0:T(1024)S(1)} %get-tuple-element.6, f32[1024]{0:T(1024)S(1)} %get-tuple-element.5), kind=kLoop, calls=%fused_computation.2 | loop fusion | flops 8388608 | bytes 20979712 | tf_op jit(solution)/shard_map/convert_element_type | solution.py:136
  159.0 0.0 reduce-scatter.2.cloned.1.call-update
  159.0 72.8 %reduce-scatter.2.cloned.1.call-done = bf16[64,2048]{1,0:T(8,128)(2,1)} async-done(((bf16[1024,2048]{1,0:T(8,128)(2,1)}), bf16[64,2048]{1,0:T(8,128)(2,1)}) %reduce-scatter.2.cloned.1.call-update) | async-done | bytes 262160 | tf_op jit(solution)/shard_map/reduce_scatter | solution.py:136
  (8 shorter events, 0.0 us)
Async XLA Ops:
  6.5 127.1 %copy-start = (bf16[1,512,2048]{2,1,0:T(8,128)(2,1)S(1)}, bf16[1,512,2048]{2,1,0:T(8,128)(2,1)}, u32[]{:S(2)}) copy-start(bf16[1,512,2048]{2,1,0:T(8,128)(2,1)} %param.17) | copy-start | bytes 6291460
  6.5 89.6 %all-gather.3.cloned.1.call-start = ((), (), s32[]{:S(2)}) async-start(), calls=%async_computation.1 | async-start | bytes 9191424 | tf_op jit(solution)/shard_map/all_gather | solution.py:76
  6.5 9.5 %collective-permute-start = (bf16[64,2048]{1,0:T(8,128)(2,1)}, bf16[64,2048]{1,0:T(8,128)(2,1)S(1)}, u32[]{:S(2)}, u32[]{:S(2)}) collective-permute-start(bf16[64,2048]{1,0:T(8,128)(2,1)} %param.9), channel_id=1, source_target_pairs={{0,1},{1,0},{2,3},{3,2},{4,5},{5,4},{6,7},{7,6},{8,9},{9,8},{10,11... | collective-permute-start | bytes 786440 | tf_op jit(solution)/shard_map/ppermute | solution.py:46
  17.9 129.2 %all-gather.5.cloned.1.call-start = ((), (), s32[]{:S(2)}) async-start(), calls=%async_computation.2 | async-start | bytes 1572864 | tf_op jit(solution)/shard_map/all_gather | solution.py:116
  101.0 8.1 %slice-start = ((s8[8650752]{0:T(1024)(128)(4,1)}), s8[4194304]{0:T(1024)(128)(4,1)S(1)}, s32[]{:S(2)}) async-start(s8[8650752]{0:T(1024)(128)(4,1)} %bitcast.74), calls=%async_computation.4 | async-start | bytes 8388608
  102.0 7.1 %slice-start.1 = ((s8[8650752]{0:T(1024)(128)(4,1)}), s8[4194304]{0:T(1024)(128)(4,1)S(1)}, s32[]{:S(2)}) async-start(s8[8650752]{0:T(1024)(128)(4,1)} %bitcast.74), calls=%async_computation.5 | async-start | bytes 8388608
  102.0 7.1 %slice-start.2 = ((s8[8650752]{0:T(1024)(128)(4,1)}), s8[262144]{0:T(1024)(128)(4,1)S(1)}, s32[]{:S(2)}) async-start(s8[8650752]{0:T(1024)(128)(4,1)} %bitcast.74), calls=%async_computation.6 | async-start | bytes 524288
  102.0 8.4 %slice-start.3 = ((s8[8388608]{0:T(1024)(128)(4,1)}), s8[4194304]{0:T(1024)(128)(4,1)S(1)}, s32[]{:S(2)}) async-start(s8[8388608]{0:T(1024)(128)(4,1)} %bitcast.86), calls=%async_computation.7 | async-start | bytes 8388608
  109.1 2.2 slice-start.4
  123.7 8.8 %collective-permute-start.1 = (bf16[512,256]{0,1:T(8,128)(2,1)}, bf16[512,256]{0,1:T(8,128)(2,1)}, u32[]{:S(2)}, u32[]{:S(2)}) collective-permute-start(bf16[512,256]{0,1:T(8,128)(2,1)} %fusion.27), channel_id=1, source_target_pairs={{0,1},{1,0},{2,3},{3,2},{4,5},{5,4},{6,7},{7,6},{8,9},{9,8},{10,11... | collective-permute-start | bytes 786440 | tf_op jit(solution)/shard_map/ppermute | solution.py:46
  128.3 103.6 %reduce-scatter.2.cloned.1.call-start = ((), (), s32[]{:S(2)}) async-start(), calls=%async_computation.3 | async-start | bytes 4456448 | tf_op jit(solution)/shard_map/reduce_scatter | solution.py:136
  152.0 3.4 %copy-start.1 = (f32[16,64,2048]{2,1,0:T(8,128)S(1)}, f32[16,64,2048]{2,1,0:T(8,128)}, u32[]{:S(2)}) copy-start(f32[16,64,2048]{2,1,0:T(8,128)} %fusion.5) | copy-start | bytes 25165828
Sparse Core Ops, SparseCore 0:
  18.1 78.0 all-gather.2
  128.4 18.6 all-gather.4
  159.2 72.6 reduce-scatter.1

commit v7 on v6

--- a/solution.py
+++ b/solution.py
@@ -133,8 +133,14 @@
         preferred_element_type=jnp.float32,
     ).reshape(all_tokens, -1)
     partial = home_scale[:, None] * home_term + spare_scale[:, None] * spare_term
-    mixed = lax.psum_scatter(partial.astype(jnp.bfloat16), "ep", scatter_dimension=0, tiled=True)
-    return mixed.astype(jnp.bfloat16)
+    partial = partial.astype(jnp.bfloat16)
+    split = partial.shape[1] // 2
+    reduced = lax.psum_scatter(partial[:, :split], "ep", scatter_dimension=0, tiled=True)
+    moved = lax.all_to_all(
+        partial[:, split:].reshape(ep_count, group_tokens, -1), "ep", 0, 0, tiled=True
+    )
+    summed = jnp.sum(moved.astype(jnp.float32), axis=0)
+    return jnp.concatenate([reduced, summed.astype(jnp.bfloat16)], axis=1)
 
 
 def solution(mesh):

time: 239 us -> 248 us (1.038)
  starting transfers between devices: 4.53 us -> 10.2 us
    reduce_scatter x1, waiting for transfers between devices: 72.8 us -> 27.2 us  [per_device(): lax.psum_scatter(partial[:, :split], 'ep', scatter_dimension=0, tiled=True)]
    all_to_all x0 -> x1, waiting for transfers between devices: none -> 43.9 us  [per_device(): lax.all_to_all(partial[:, split:].reshape(ep_count, group_tokens, -1), 'e...]
    all_to_all x0 -> x1, starting transfers between devices: none -> 5.66 us  [per_device(): lax.all_to_all(partial[:, split:].reshape(ep_count, group_tokens, -1), 'e...]
  transfers between devices with their start and end apart: 5 -> 6, of which waited for: 5 -> 6; matrix products, arithmetic and copies ran while one was open for 8% -> 8% of each run, Pallas kernels for 0% -> 0%
where the time goes in v7:
time: 248 us
  waiting for transfers between devices  159 us (64%)
  matrix products  31.2 us (13%)
  other arithmetic  22 us (9%)
  between operations  14.8 us (6%)
  local copies, waits for them, and re-layouts  10.7 us (4%)
  starting transfers between devices  10.2 us (4%)
    all_gather x1, waiting for transfers between devices, per_device(): every_row = lax.all_gather(packed, 'ep', axis=0, tiled=True)  71.5 us
    all_to_all x1, waiting for transfers between devices, per_device(): lax.all_to_all(partial[:, split:].reshape(ep_count, group_tokens, -1), 'e...  43.9 us
    reduce_scatter x1, waiting for transfers between devices, per_device(): lax.psum_scatter(partial[:, :split], 'ep', scatter_dimension=0, tiled=True)  27.2 us
    dot_general x2, matrix products, gate_up(): jnp.einsum('rd,djf->rjf', row_block, weight, preferred_element_type=jnp.f...  10.3 us
    all_gather x1, waiting for transfers between devices, per_device(): home_hidden = lax.all_gather(home_hidden, 'dp', axis=1, tiled=True)  8.16 us
    ppermute x2, waiting for transfers between devices, gather_dp(): partner = lax.ppermute(block, 'dp', perm=[(0, 1), (1, 0)])  7.33 us
    dot_general x1, matrix products, per_device(): jnp.einsum('gpi,gic->gpc', spare_pick, grouped, preferred_element_type=jn...  7.08 us
    all_to_all x1, starting transfers between devices, per_device(): lax.all_to_all(partial[:, split:].reshape(ep_count, group_tokens, -1), 'e...  5.66 us
  transfers between devices with their start and end apart: 6, of which 6 were waited for; matrix products, arithmetic and copies ran while one was open for 8% of the time, Pallas kernels for 0%

profile of v7, /device:TPU:0, one launch (start us, length us, event | category | flops | bytes accessed | tf_op | source)
XLA Modules:
  0.0 247.8 jit_solution(8332238563004557407)
XLA Ops:
  6.5 3.0 %collective-permute-start = (bf16[64,2048]{1,0:T(8,128)(2,1)}, bf16[64,2048]{1,0:T(8,128)(2,1)S(1)}, u32[]{:S(2)}, u32[]{:S(2)}) collective-permute-start(bf16[64,2048]{1,0:T(8,128)(2,1)} %param.9), channel_id=1, source_target_pairs={{0,1},{1,0},{2,3},{3,2},{4,5},{5,4},{6,7},{7,6},{8,9},{9,8},{10,11... | collective-permute-start | bytes 786440 | tf_op jit(solution)/shard_map/ppermute | solution.py:46
  9.5 0.7 convert_element_type.69
  10.2 0.8 fusion.46
  11.0 0.1 copy.56
  11.1 4.9 %collective-permute-done = bf16[64,2048]{1,0:T(8,128)(2,1)S(1)} collective-permute-done((bf16[64,2048]{1,0:T(8,128)(2,1)}, bf16[64,2048]{1,0:T(8,128)(2,1)S(1)}, u32[]{:S(2)}, u32[]{:S(2)}) %collective-permute-start) | collective-permute-done | bytes 262176 | tf_op jit(solution)/shard_map/ppermute | solution.py:46
  16.0 1.0 broadcast_select_fusion.3
  17.0 0.9 fusion.25
  17.9 0.0 all-gather.3.cloned.1.call-update
  17.9 0.0 all-gather.5.cloned.1.call-start
  18.0 1.2 dynamic_slice.6
  19.3 1.2 dynamic_slice.7
  20.5 1.4 fusion.39
  22.6 1.4 compare_reduce_fusion
  24.6 71.5 %all-gather.3.cloned.1.call-done = bf16[1024,4224]{1,0:T(8,128)(2,1)} async-done(((bf16[64,4224]{1,0:T(8,128)(2,1)}), bf16[1024,4224]{1,0:T(8,128)(2,1)}) %all-gather.3.cloned.1.call-update) | async-done | bytes 8650768 | tf_op jit(solution)/shard_map/all_gather | solution.py:76
  96.2 1.8 convert_compare_fusion.1
  97.9 0.3 eq.63
  98.3 0.3 eq.72
  98.6 0.3 compare_and_fusion.1
  98.9 0.2 copy.44
  99.1 0.2 copy.45
  99.3 0.8 compare_and_fusion
  100.1 0.2 copy.49
  100.3 0.2 copy.50
  100.4 0.1 copy.46
  100.6 0.1 copy.47
  100.7 0.1 copy.51
  100.8 0.1 copy.52
  101.0 0.0 slice-start
  101.0 0.5 fusion.18
  101.5 0.5 fusion.20
  102.0 0.0 slice-start.3
  102.0 7.1 %convolution_convert_fusion = bf16[16,32,4224]{2,1,0:T(8,128)(2,1)} fusion(pred[16,64,32]{1,2,0:T(8,128)(4,1)S(1)} %fusion.20, bf16[16,64,4224]{2,1,0:T(8,128)(2,1)} %bitcast.74), kind=kOutput, calls=%fused_computation.6 | convolution fusion | flops 278986752 | bytes 13008896 | tf_op jit(solution)/shard_map/gpi,gic->gpc/dot_general | solution.py:111
  109.1 0.0 slice-start.4
  109.1 1.3 convolution_convert_fusion.1
  110.5 0.9 slice-done.4
  111.3 4.5 %fusion.2 = f32[512,2,512]{2,0,1:T(8,128)S(1)} fusion(bf16[4096,2,512]{2,1,0:T(2,128)(2,1)S(1)} %bitcast.90, bf16[512,4224]{1,0:T(8,128)(2,1)S(1)} %bitcast.79), kind=kOutput, calls=%fused_computation.4 | convolution fusion | flops 4294967296 | bytes 14680064 | tf_op jit(solution)/shard_map/rd,djf->rjf/dot_general | solution.py:8
  115.8 1.2 fusion.24
  117.0 5.8 %fusion.4 = f32[512,2,256]{0,2,1:T(8,128)S(1)} fusion(bf16[512,4224]{1,0:T(8,128)(2,1)} %bitcast.78, bf16[4096,2,256]{2,1,0:T(2,128)(2,1)} %bitcast.91), kind=kOutput, calls=%fused_computation.9 | convolution fusion | flops 2147483648 | bytes 9437184 | tf_op jit(solution)/shard_map/rd,djf->rjf/dot_general | solution.py:8
  122.8 0.9 fusion.27
  123.7 1.5 collective-permute-start.1
  125.1 1.1 slice_convert_fusion
  126.2 1.3 fusion.43
  127.6 0.4 reshape.60
  127.9 0.4 reshape.55
  128.3 0.0 all-gather.5.cloned.1.call-update
  128.3 1.5 select_reduce_fusion.1
  129.8 0.2 copy.53
  130.1 2.4 collective-permute-done.1
  132.4 1.2 broadcast_select_fusion.1
  133.6 1.3 subtract_convert_fusion
  134.9 4.0 %fusion.5 = f32[16,64,2048]{2,1,0:T(8,128)} fusion(bf16[16,32,2048]{2,1,0:T(8,128)(2,1)S(1)} %bitcast.81, bf16[16,32,2048]{2,1,0:T(8,128)(2,1)S(1)} %bitcast.82, pred[16,64,32]{2,1,0:T(32,128)(4,1)S(1)} %copy.53), kind=kOutput, calls=%fused_computation.11 | convolution fusion | flops 276889600 | bytes 12615680 | tf_op jit(solution)/shard_map/gip,gpc->gic/dot_general | solution.py:129
  139.0 8.2 %all-gather.5.cloned.1.call-done = bf16[512,1024]{1,0:T(8,128)(2,1)} async-done(((bf16[512,512]{1,0:T(8,128)(2,1)}), bf16[512,1024]{1,0:T(8,128)(2,1)}) %all-gather.5.cloned.1.call-update) | async-done | bytes 1048592 | tf_op jit(solution)/shard_map/all_gather | solution.py:116
  147.1 4.8 %fusion.12 = bf16[512,2048]{1,0:T(8,128)(2,1)S(1)} fusion(bf16[512,1024]{1,0:T(8,128)(2,1)} %all-gather.5.cloned.1.call-done, bf16[1,1024,2048]{2,1,0:T(8,128)(2,1)} %param.15), kind=kOutput, calls=%fused_computation.19 | convolution fusion | flops 2148532224 | bytes 7340032 | tf_op jit(solution)/shard_map/dot_general | solution.py:118
  152.0 1.3 fusion.47
  153.3 2.1 copy-done.1
  155.4 2.4 fusion.1
  157.7 2.4 fusion.45
  160.1 5.7 %all-to-all-start = ((bf16[16,64,1024]{2,1,0:T(8,128)(2,1)}), bf16[16,64,1024]{2,1,0:T(8,128)(2,1)}, u32[]{:S(2)}, u32[]{:S(2)}) async-start(bf16[16,64,1024]{2,1,0:T(8,128)(2,1)} %bitcast.80), calls=%async_computation.1 | async-start | bytes 4194304 | tf_op jit(solution)/shard_map/all_to_all | solution.py:139
  165.8 0.0 reduce-scatter.2.cloned.1.call-start
  165.8 0.7 reduce-scatter.2.cloned.1.call-update
  166.5 43.9 %all-to-all-done = bf16[16,64,1024]{2,1,0:T(8,128)(2,1)} async-done(((bf16[16,64,1024]{2,1,0:T(8,128)(2,1)}), bf16[16,64,1024]{2,1,0:T(8,128)(2,1)}, u32[]{:S(2)}, u32[]{:S(2)}) %all-to-all-start) | async-done | bytes 2097184 | tf_op jit(solution)/shard_map/all_to_all | solution.py:139
  210.5 2.0 reduce_sum.52
  212.5 27.2 %reduce-scatter.2.cloned.1.call-done = bf16[64,1024]{1,0:T(8,128)(2,1)} async-done(((bf16[1024,1024]{1,0:T(8,128)(2,1)}), bf16[64,1024]{1,0:T(8,128)(2,1)}) %reduce-scatter.2.cloned.1.call-update) | async-done | bytes 131088 | tf_op jit(solution)/shard_map/reduce_scatter | solution.py:138
  239.7 1.6 pad_maximum_fusion
  (13 shorter events, 0.0 us)
Async XLA Ops:
  6.5 127.1 %copy-start = (bf16[1,512,2048]{2,1,0:T(8,128)(2,1)S(1)}, bf16[1,512,2048]{2,1,0:T(8,128)(2,1)}, u32[]{:S(2)}) copy-start(bf16[1,512,2048]{2,1,0:T(8,128)(2,1)} %param.17) | copy-start | bytes 6291460
  6.5 89.6 %all-gather.3.cloned.1.call-start = ((), (), s32[]{:S(2)}) async-start(), calls=%async_computation.2 | async-start | bytes 9191424 | tf_op jit(solution)/shard_map/all_gather | solution.py:76
  6.5 9.5 %collective-permute-start = (bf16[64,2048]{1,0:T(8,128)(2,1)}, bf16[64,2048]{1,0:T(8,128)(2,1)S(1)}, u32[]{:S(2)}, u32[]{:S(2)}) collective-permute-start(bf16[64,2048]{1,0:T(8,128)(2,1)} %param.9), channel_id=1, source_target_pairs={{0,1},{1,0},{2,3},{3,2},{4,5},{5,4},{6,7},{7,6},{8,9},{9,8},{10,11... | collective-permute-start | bytes 786440 | tf_op jit(solution)/shard_map/ppermute | solution.py:46
  17.9 129.2 %all-gather.5.cloned.1.call-start = ((), (), s32[]{:S(2)}) async-start(), calls=%async_computation.3 | async-start | bytes 1572864 | tf_op jit(solution)/shard_map/all_gather | solution.py:116
  101.0 8.1 %slice-start = ((s8[8650752]{0:T(1024)(128)(4,1)}), s8[4194304]{0:T(1024)(128)(4,1)S(1)}, s32[]{:S(2)}) async-start(s8[8650752]{0:T(1024)(128)(4,1)} %bitcast.75), calls=%async_computation.5 | async-start | bytes 8388608
  102.0 7.1 %slice-start.1 = ((s8[8650752]{0:T(1024)(128)(4,1)}), s8[4194304]{0:T(1024)(128)(4,1)S(1)}, s32[]{:S(2)}) async-start(s8[8650752]{0:T(1024)(128)(4,1)} %bitcast.75), calls=%async_computation.6 | async-start | bytes 8388608
  102.0 7.1 %slice-start.2 = ((s8[8650752]{0:T(1024)(128)(4,1)}), s8[262144]{0:T(1024)(128)(4,1)S(1)}, s32[]{:S(2)}) async-start(s8[8650752]{0:T(1024)(128)(4,1)} %bitcast.75), calls=%async_computation.7 | async-start | bytes 524288
  102.0 8.4 %slice-start.3 = ((s8[8388608]{0:T(1024)(128)(4,1)}), s8[4194304]{0:T(1024)(128)(4,1)S(1)}, s32[]{:S(2)}) async-start(s8[8388608]{0:T(1024)(128)(4,1)} %bitcast.88), calls=%async_computation.8 | async-start | bytes 8388608
  109.1 2.2 slice-start.4
  123.7 8.8 %collective-permute-start.1 = (bf16[512,256]{0,1:T(8,128)(2,1)}, bf16[512,256]{0,1:T(8,128)(2,1)}, u32[]{:S(2)}, u32[]{:S(2)}) collective-permute-start(bf16[512,256]{0,1:T(8,128)(2,1)} %fusion.27), channel_id=1, source_target_pairs={{0,1},{1,0},{2,3},{3,2},{4,5},{5,4},{6,7},{7,6},{8,9},{9,8},{10,11... | collective-permute-start | bytes 786440 | tf_op jit(solution)/shard_map/ppermute | solution.py:46
  152.0 3.4 %copy-start.1 = (f32[16,64,2048]{2,1,0:T(8,128)S(1)}, f32[16,64,2048]{2,1,0:T(8,128)}, u32[]{:S(2)}) copy-start(f32[16,64,2048]{2,1,0:T(8,128)} %fusion.5) | copy-start | bytes 25165828
  160.1 50.3 %all-to-all-start = ((bf16[16,64,1024]{2,1,0:T(8,128)(2,1)}), bf16[16,64,1024]{2,1,0:T(8,128)(2,1)}, u32[]{:S(2)}, u32[]{:S(2)}) async-start(bf16[16,64,1024]{2,1,0:T(8,128)(2,1)} %bitcast.80), calls=%async_computation.1 | async-start | bytes 4194304 | tf_op jit(solution)/shard_map/all_to_all | solution.py:139
  165.8 73.9 %reduce-scatter.2.cloned.1.call-start = ((), (), s32[]{:S(2)}) async-start(), calls=%async_computation.4 | async-start | bytes 2228224 | tf_op jit(solution)/shard_map/reduce_scatter | solution.py:138
Sparse Core Ops, SparseCore 0:
  18.1 78.0 all-gather.2
  128.4 18.6 all-gather.4
  170.4 69.2 reduce-scatter.1

commit v8 on v6

--- a/solution.py
+++ b/solution.py
@@ -1,7 +1,7 @@
 import jax
 import jax.numpy as jnp
 from jax import lax
-from jax.sharding import PartitionSpec as P
+from jax.sharding import Mesh, PartitionSpec as P
 
 
 def gate_up(row_block, weight):
@@ -50,6 +50,23 @@
     return jnp.concatenate([low, high], axis=axis)
 
 
+def reduce_partial(partial, inner, group_tokens):
+    if inner == 2:
+        paired = partial.reshape(-1, 2, group_tokens, partial.shape[1])
+        first = lax.axis_index("core") == 0
+        keep = jnp.where(first, paired[:, 0], paired[:, 1])
+        send = jnp.where(first, paired[:, 1], paired[:, 0])
+        partial = (keep + lax.ppermute(send, "core", perm=[(0, 1), (1, 0)])).reshape(
+            -1, partial.shape[1]
+        )
+        axes = "chip"
+    else:
+        axes = ("chip", "core")
+    return lax.psum_scatter(
+        partial.astype(jnp.bfloat16), axes, scatter_dimension=0, tiled=True
+    ).astype(jnp.bfloat16)
+
+
 def per_device(
     tokens,
     expert_ids,
@@ -61,8 +78,9 @@
     spare_gate_up,
     spare_down,
 ):
-    ep_count = lax.axis_size("ep")
-    me = lax.axis_index("ep")
+    inner = lax.axis_size("core")
+    ep_count = lax.axis_size("chip") * inner
+    me = lax.axis_index("chip") * inner + lax.axis_index("core")
     group_tokens = tokens.shape[0]
     top_count = expert_ids.shape[1]
     spares = placement.shape[0]
@@ -73,7 +91,7 @@
     d_model = tokens.shape[1] * lax.axis_size("dp")
     whole_rows = gather_dp(tokens, 1)
     packed = jnp.concatenate([whole_rows, side_columns(expert_ids, gate_logits)], axis=1)
-    every_row = lax.all_gather(packed, "ep", axis=0, tiled=True)
+    every_row = lax.all_gather(packed, ("chip", "core"), axis=0, tiled=True)
     all_tokens = every_row.shape[0]
     ids = every_row[:, d_model : d_model + top_count].astype(jnp.int32)
     parts = every_row[:, d_model + top_count : d_model + 4 * top_count].astype(jnp.float32)
@@ -133,25 +151,30 @@
         preferred_element_type=jnp.float32,
     ).reshape(all_tokens, -1)
     partial = home_scale[:, None] * home_term + spare_scale[:, None] * spare_term
-    mixed = lax.psum_scatter(partial.astype(jnp.bfloat16), "ep", scatter_dimension=0, tiled=True)
-    return mixed.astype(jnp.bfloat16)
+    return reduce_partial(partial, inner, group_tokens)
 
 
 def solution(mesh):
+    ep_count = mesh.shape["ep"]
+    inner = 2 if ep_count % 2 == 0 else 1
+    view = Mesh(
+        mesh.devices.reshape(ep_count // inner, inner, mesh.shape["dp"]), ("chip", "core", "dp")
+    )
+    ep = ("chip", "core")
     return jax.shard_map(
         per_device,
-        mesh=mesh,
+        mesh=view,
         in_specs=(
-            P("ep", "dp"),
-            P("ep", None),
-            P("ep", None),
+            P(ep, "dp"),
+            P(ep, None),
+            P(ep, None),
             P(),
             P(),
-            P("ep", None, None, "dp"),
-            P("ep", None, "dp"),
-            P("ep", None, None, "dp"),
-            P("ep", None, "dp"),
+            P(ep, None, None, "dp"),
+            P(ep, None, "dp"),
+            P(ep, None, None, "dp"),
+            P(ep, None, "dp"),
         ),
-        out_specs=P("ep", "dp"),
+        out_specs=P(ep, "dp"),
         check_vma=False,
     )

time: 239 us -> 243 us (1.017)
  other arithmetic: 19.7 us -> 23.3 us
    ppermute x0 -> x1, waiting for transfers between devices: none -> 7.15 us  [reduce_partial(): lax.ppermute(send, 'core', perm=[(0, 1), (1, 0)])]
    reduce_scatter x1, waiting for transfers between devices: 72.8 us -> 68.4 us  [reduce_partial(): lax.psum_scatter(partial.astype(jnp.bfloat16), axes, scatter_dimension=0,...]
    add x0 -> x1, other arithmetic: none -> 4.06 us  [per_device(): home_scale[:, None] * home_term + spare_scale[:, None] * spare_term]
  transfers between devices with their start and end apart: 5 -> 6, of which waited for: 5 -> 6; matrix products, arithmetic and copies ran while one was open for 8% -> 8% of each run, Pallas kernels for 0% -> 0%
where the time goes in v8:
time: 243 us
  waiting for transfers between devices  162 us (67%)
  matrix products  31.3 us (13%)
  other arithmetic  23.3 us (10%)
  between operations  14.7 us (6%)
  local copies, waits for them, and re-layouts  6.51 us (3%)
  starting transfers between devices  4.6 us (2%)
    all_gather x1, waiting for transfers between devices, per_device(): every_row = lax.all_gather(packed, ('chip', 'core'), axis=0, tiled=True)  71.6 us
    reduce_scatter x1, waiting for transfers between devices, reduce_partial(): lax.psum_scatter(partial.astype(jnp.bfloat16), axes, scatter_dimension=0,...  68.4 us
    dot_general x2, matrix products, gate_up(): jnp.einsum('rd,djf->rjf', row_block, weight, preferred_element_type=jnp.f...  10.3 us
    all_gather x1, waiting for transfers between devices, per_device(): home_hidden = lax.all_gather(home_hidden, 'dp', axis=1, tiled=True)  8.17 us
    ppermute x1, waiting for transfers between devices, reduce_partial(): lax.ppermute(send, 'core', perm=[(0, 1), (1, 0)])  7.15 us
    ppermute x2, waiting for transfers between devices, gather_dp(): partner = lax.ppermute(block, 'dp', perm=[(0, 1), (1, 0)])  7.13 us
    dot_general x1, matrix products, per_device(): jnp.einsum('gpi,gic->gpc', spare_pick, grouped, preferred_element_type=jn...  7.08 us
  transfers between devices with their start and end apart: 6, of which 6 were waited for; matrix products, arithmetic and copies ran while one was open for 8% of the time, Pallas kernels for 0%

profile of v8, /device:TPU:0, one launch (start us, length us, event | category | flops | bytes accessed | tf_op | source)
XLA Modules:
  0.0 242.8 jit_solution(5638599318291738438)
XLA Ops:
  6.5 3.0 %collective-permute-start = (bf16[64,2048]{1,0:T(8,128)(2,1)}, bf16[64,2048]{1,0:T(8,128)(2,1)S(1)}, u32[]{:S(2)}, u32[]{:S(2)}) collective-permute-start(bf16[64,2048]{1,0:T(8,128)(2,1)} %param.9), channel_id=1, source_target_pairs={{0,1},{1,0},{2,3},{3,2},{4,5},{5,4},{6,7},{7,6},{8,9},{9,8},{10,11... | collective-permute-start | bytes 786440 | tf_op jit(solution)/shard_map/ppermute | solution.py:46
  9.5 0.7 convert_element_type.70
  10.2 0.8 fusion.46
  11.0 0.1 copy.73
  11.1 4.9 %collective-permute-done = bf16[64,2048]{1,0:T(8,128)(2,1)S(1)} collective-permute-done((bf16[64,2048]{1,0:T(8,128)(2,1)}, bf16[64,2048]{1,0:T(8,128)(2,1)S(1)}, u32[]{:S(2)}, u32[]{:S(2)}) %collective-permute-start) | collective-permute-done | bytes 262176 | tf_op jit(solution)/shard_map/ppermute | solution.py:46
  16.0 1.0 broadcast_select_fusion.3
  17.0 0.9 fusion.26
  17.9 0.0 all-gather.3.cloned.1.call-update
  17.9 0.0 all-gather.5.cloned.1.call-start
  18.0 1.2 dynamic_slice.6
  19.3 1.3 dynamic_slice.7
  20.6 1.4 fusion.40
  22.6 1.4 compare_reduce_fusion
  24.6 71.6 %all-gather.3.cloned.1.call-done = bf16[1024,4224]{1,0:T(8,128)(2,1)} async-done(((bf16[64,4224]{1,0:T(8,128)(2,1)}), bf16[1024,4224]{1,0:T(8,128)(2,1)}) %all-gather.3.cloned.1.call-update) | async-done | bytes 8650768 | tf_op jit(solution)/shard_map/all_gather | solution.py:94
  96.2 1.8 convert_compare_fusion.1
  97.9 0.3 eq.67
  98.3 0.3 eq.76
  98.6 0.3 compare_and_fusion.1
  98.9 0.2 copy.56
  99.1 0.2 copy.57
  99.3 0.9 compare_and_fusion
  100.2 0.2 copy.61
  100.4 0.2 copy.62
  100.5 0.1 copy.58
  100.7 0.1 copy.59
  100.8 0.1 copy.63
  101.0 0.1 copy.64
  101.1 0.0 slice-start
  101.1 0.5 fusion.19
  101.6 0.5 fusion.21
  102.1 0.0 slice-start.3
  102.1 7.1 %convolution_convert_fusion = bf16[16,32,4224]{2,1,0:T(8,128)(2,1)} fusion(pred[16,64,32]{1,2,0:T(8,128)(4,1)S(1)} %fusion.21, bf16[16,64,4224]{2,1,0:T(8,128)(2,1)} %bitcast.88), kind=kOutput, calls=%fused_computation.3 | convolution fusion | flops 278986752 | bytes 13008896 | tf_op jit(solution)/shard_map/gpi,gic->gpc/dot_general | solution.py:129
  109.2 0.0 slice-start.4
  109.3 1.3 convolution_convert_fusion.1
  110.6 0.9 slice-done.4
  111.4 4.5 %fusion = f32[512,2,512]{2,0,1:T(8,128)S(1)} fusion(bf16[4096,2,512]{2,1,0:T(2,128)(2,1)S(1)} %bitcast.106, bf16[512,4224]{1,0:T(8,128)(2,1)S(1)} %bitcast.95), kind=kOutput, calls=%fused_computation | convolution fusion | flops 4294967296 | bytes 14680064 | tf_op jit(solution)/shard_map/rd,djf->rjf/dot_general | solution.py:8
  115.9 1.2 fusion.25
  117.1 5.8 %fusion.2 = f32[512,2,256]{0,2,1:T(8,128)S(1)} fusion(bf16[512,4224]{1,0:T(8,128)(2,1)} %bitcast.94, bf16[4096,2,256]{2,1,0:T(2,128)(2,1)} %bitcast.107), kind=kOutput, calls=%fused_computation.6 | convolution fusion | flops 2147483648 | bytes 9437184 | tf_op jit(solution)/shard_map/rd,djf->rjf/dot_general | solution.py:8
  122.9 0.9 fusion.28
  123.8 1.5 collective-permute-start.1
  125.2 1.1 slice_convert_fusion
  126.3 1.3 fusion.44
  127.7 0.4 reshape.76
  128.0 0.4 reshape.71
  128.4 0.0 all-gather.5.cloned.1.call-update
  128.4 0.0 reduce-scatter.2.cloned.1.call-start
  128.5 1.5 select_reduce_fusion.1
  130.0 0.2 copy.65
  130.2 0.1 mul.48
  130.3 0.1 mul.53
  130.4 2.2 collective-permute-done.1
  132.6 1.2 broadcast_select_fusion.1
  133.8 1.3 subtract_convert_fusion
  135.0 4.0 %fusion.3 = f32[16,64,2048]{2,1,0:T(8,128)} fusion(bf16[16,32,2048]{2,1,0:T(8,128)(2,1)S(1)} %bitcast.97, bf16[16,32,2048]{2,1,0:T(8,128)(2,1)S(1)} %bitcast.98, pred[16,64,32]{2,1,0:T(32,128)(4,1)S(1)} %copy.65), kind=kOutput, calls=%fused_computation.8 | convolution fusion | flops 276889600 | bytes 12615680 | tf_op jit(solution)/shard_map/gip,gpc->gic/dot_general | solution.py:147
  139.1 8.2 %all-gather.5.cloned.1.call-done = bf16[512,1024]{1,0:T(8,128)(2,1)} async-done(((bf16[512,512]{1,0:T(8,128)(2,1)}), bf16[512,1024]{1,0:T(8,128)(2,1)}) %all-gather.5.cloned.1.call-update) | async-done | bytes 1048592 | tf_op jit(solution)/shard_map/all_gather | solution.py:134
  147.2 4.8 %fusion.13 = bf16[512,2048]{1,0:T(8,128)(2,1)S(1)} fusion(bf16[512,1024]{1,0:T(8,128)(2,1)} %all-gather.5.cloned.1.call-done, bf16[1,1024,2048]{2,1,0:T(8,128)(2,1)} %param.15), kind=kOutput, calls=%fused_computation.21 | convolution fusion | flops 2148532224 | bytes 7340032 | tf_op jit(solution)/shard_map/dot_general | solution.py:136
  152.1 1.3 fusion.47
  153.4 4.1 %multiply_add_fusion = f32[8,2,64,2048]{3,2,1,0:T(8,128)S(1)} fusion(f32[8,2,64,2048]{3,2,1,0:T(8,128)} %bitcast.93, f32[8,2,64,2048]{3,2,1,0:T(8,128)S(1)} %bitcast.92, f32[8,2,64]{2,1,0:T(2,128)S(1)} %mul.53, f32[8,2,64]{2,1,0:T(2,128)S(1)} %mul.48), kind=kLoop, calls=%fused_computation.2 | loop fusion | flops 6291456 | bytes 25174016 | tf_op jit(solution)/shard_map/add | solution.py:153
  157.4 0.8 select_bitcast_fusion
  158.2 0.1 collective-permute-start.2
  158.3 7.1 %collective-permute-done.2 = f32[8,64,2048]{2,1,0:T(8,128)S(1)} collective-permute-done((f32[8,64,2048]{2,1,0:T(8,128)S(1)}, f32[8,64,2048]{2,1,0:T(8,128)S(1)}, u32[]{:S(2)}, u32[]{:S(2)}) %collective-permute-start.2) | collective-permute-done | bytes 4194336 | tf_op jit(solution)/shard_map/ppermute | solution.py:59
  165.4 2.5 %fusion.9 = bf16[8,64,2048]{2,1,0:T(8,128)(2,1)} fusion(f32[8,64,2048]{2,1,0:T(8,128)S(1)} %collective-permute-done.2, f32[8,2,64,2048]{3,2,1,0:T(8,128)S(1)} %multiply_add_fusion, pred[]{:T(512)S(6)} %eq.63), kind=kLoop, calls=%fused_computation.15 | loop fusion | flops 3145728 | bytes 14680065 | tf_op jit(solution)/shard_map/convert_element_type | solution.py:66
  167.9 0.0 reduce-scatter.2.cloned.1.call-update
  167.9 68.4 %reduce-scatter.2.cloned.1.call-done = bf16[64,2048]{1,0:T(8,128)(2,1)} async-done(((bf16[512,2048]{1,0:T(8,128)(2,1)}), bf16[64,2048]{1,0:T(8,128)(2,1)}) %reduce-scatter.2.cloned.1.call-update) | async-done | bytes 262160 | tf_op jit(solution)/shard_map/reduce_scatter | solution.py:65
  (14 shorter events, 0.0 us)
Async XLA Ops:
  6.5 127.2 %copy-start = (bf16[1,512,2048]{2,1,0:T(8,128)(2,1)S(1)}, bf16[1,512,2048]{2,1,0:T(8,128)(2,1)}, u32[]{:S(2)}) copy-start(bf16[1,512,2048]{2,1,0:T(8,128)(2,1)} %param.17) | copy-start | bytes 6291460
  6.5 89.6 %all-gather.3.cloned.1.call-start = ((), (), s32[]{:S(2)}) async-start(), calls=%async_computation.1 | async-start | bytes 9191424 | tf_op jit(solution)/shard_map/all_gather | solution.py:94
  6.5 9.5 %collective-permute-start = (bf16[64,2048]{1,0:T(8,128)(2,1)}, bf16[64,2048]{1,0:T(8,128)(2,1)S(1)}, u32[]{:S(2)}, u32[]{:S(2)}) collective-permute-start(bf16[64,2048]{1,0:T(8,128)(2,1)} %param.9), channel_id=1, source_target_pairs={{0,1},{1,0},{2,3},{3,2},{4,5},{5,4},{6,7},{7,6},{8,9},{9,8},{10,11... | collective-permute-start | bytes 786440 | tf_op jit(solution)/shard_map/ppermute | solution.py:46
  17.9 129.3 %all-gather.5.cloned.1.call-start = ((), (), s32[]{:S(2)}) async-start(), calls=%async_computation.2 | async-start | bytes 1572864 | tf_op jit(solution)/shard_map/all_gather | solution.py:134
  101.1 8.1 %slice-start = ((s8[8650752]{0:T(1024)(128)(4,1)}), s8[4194304]{0:T(1024)(128)(4,1)S(1)}, s32[]{:S(2)}) async-start(s8[8650752]{0:T(1024)(128)(4,1)} %bitcast.89), calls=%async_computation.4 | async-start | bytes 8388608
  102.1 7.1 %slice-start.1 = ((s8[8650752]{0:T(1024)(128)(4,1)}), s8[4194304]{0:T(1024)(128)(4,1)S(1)}, s32[]{:S(2)}) async-start(s8[8650752]{0:T(1024)(128)(4,1)} %bitcast.89), calls=%async_computation.5 | async-start | bytes 8388608
  102.1 7.1 %slice-start.2 = ((s8[8650752]{0:T(1024)(128)(4,1)}), s8[262144]{0:T(1024)(128)(4,1)S(1)}, s32[]{:S(2)}) async-start(s8[8650752]{0:T(1024)(128)(4,1)} %bitcast.89), calls=%async_computation.6 | async-start | bytes 524288
  102.1 8.4 %slice-start.3 = ((s8[8388608]{0:T(1024)(128)(4,1)}), s8[4194304]{0:T(1024)(128)(4,1)S(1)}, s32[]{:S(2)}) async-start(s8[8388608]{0:T(1024)(128)(4,1)} %bitcast.104), calls=%async_computation.7 | async-start | bytes 8388608
  109.2 2.2 slice-start.4
  123.8 8.8 %collective-permute-start.1 = (bf16[512,256]{0,1:T(8,128)(2,1)}, bf16[512,256]{0,1:T(8,128)(2,1)}, u32[]{:S(2)}, u32[]{:S(2)}) collective-permute-start(bf16[512,256]{0,1:T(8,128)(2,1)} %fusion.28), channel_id=1, source_target_pairs={{0,1},{1,0},{2,3},{3,2},{4,5},{5,4},{6,7},{7,6},{8,9},{9,8},{10,11... | collective-permute-start | bytes 786440 | tf_op jit(solution)/shard_map/ppermute | solution.py:46
  128.4 107.9 %reduce-scatter.2.cloned.1.call-start = ((), (), s32[]{:S(2)}) async-start(), calls=%async_computation.3 | async-start | bytes 2359296 | tf_op jit(solution)/shard_map/reduce_scatter | solution.py:65
  158.2 7.2 %collective-permute-start.2 = (f32[8,64,2048]{2,1,0:T(8,128)S(1)}, f32[8,64,2048]{2,1,0:T(8,128)S(1)}, u32[]{:S(2)}, u32[]{:S(2)}) collective-permute-start(f32[8,64,2048]{2,1,0:T(8,128)S(1)} %select_bitcast_fusion), channel_id=1, source_target_pairs={{0,2},{2,0},{1,3},{3,1},{4,6},{6,4},{5,7},{7,5},{8,10},{10,8},{9,1... | collective-permute-start | bytes 12582920 | tf_op jit(solution)/shard_map/ppermute | solution.py:59
  165.4 70.8 %copy-start.1 = (bf16[1,512,2048]{2,1,0:T(8,128)(2,1)S(1)}, bf16[1,512,2048]{2,1,0:T(8,128)(2,1)}, u32[]{:S(2)}) copy-start(bf16[1,512,2048]{2,1,0:T(8,128)(2,1)} %param.17) | copy-start | bytes 6291460
Sparse Core Ops, SparseCore 0:
  18.1 78.0 all-gather.2
  128.5 18.6 all-gather.4
  168.1 68.1 reduce-scatter.1

commit v9 on v6

--- a/solution.py
+++ b/solution.py
@@ -113,7 +113,7 @@
     ).astype(jnp.bfloat16).reshape(slot_rows, -1)
     home_hidden = gate_up(home_rows[:, :d_model], gate_up_weight[0])
     spare_hidden = gate_up(spare_rows[:, :d_model], spare_gate_up[0])
-    home_hidden = lax.all_gather(home_hidden, "dp", axis=1, tiled=True)
+    home_hidden = gather_dp(home_hidden, 1)
     spare_hidden = gather_dp(spare_hidden, 1)
     home_out = jnp.dot(home_hidden, down_weight[0], preferred_element_type=jnp.float32)
     home_out = home_out.astype(jnp.bfloat16).reshape(ep_count, capacity, -1)

time: 239 us -> 229 us (0.958)
  matrix products: 31.2 us -> 25.9 us
  waiting for transfers between devices: 160 us -> 155 us
    all_gather x1 -> x0, waiting for transfers between devices: 8.16 us -> none  [per_device(): home_hidden = lax.all_gather(home_hidden, 'dp', axis=1, tiled=True)]
    ppermute x2 -> x3, waiting for transfers between devices: 7.28 us -> 12.7 us  [gather_dp(): partner = lax.ppermute(block, 'dp', perm=[(0, 1), (1, 0)])]
    reduce_scatter x1, waiting for transfers between devices: 72.8 us -> 69.9 us  [per_device(): lax.psum_scatter(partial.astype(jnp.bfloat16), 'ep', scatter_dimension=0,...]
    dot_general x1, matrix products: 4.02 us -> 1.57 us  [per_device(): jnp.einsum('gip,gpc->gic', jnp.concatenate([spare_take, spare_take], axis...]
    dot_general x1, matrix products: 4.85 us -> 2.45 us  [per_device(): jnp.dot(home_hidden, down_weight[0], preferred_element_type=jnp.float32)]
    ppermute x2 -> x3, starting transfers between devices: 4.45 us -> 5.04 us  [gather_dp(): partner = lax.ppermute(block, 'dp', perm=[(0, 1), (1, 0)])]
  transfers between devices with their start and end apart: 5 -> 5, of which waited for: 5 -> 4; matrix products, arithmetic and copies ran while one was open for 8% -> 12% of each run, Pallas kernels for 0% -> 0%
where the time goes in v9:
time: 229 us
  waiting for transfers between devices  155 us (68%)
  matrix products  25.9 us (11%)
  other arithmetic  20.5 us (9%)
  between operations  14.9 us (7%)
  local copies, waits for them, and re-layouts  7.67 us (3%)
  starting transfers between devices  5.09 us (2%)
    all_gather x1, waiting for transfers between devices, per_device(): every_row = lax.all_gather(packed, 'ep', axis=0, tiled=True)  71.9 us
    reduce_scatter x1, waiting for transfers between devices, per_device(): lax.psum_scatter(partial.astype(jnp.bfloat16), 'ep', scatter_dimension=0,...  69.9 us
    ppermute x3, waiting for transfers between devices, gather_dp(): partner = lax.ppermute(block, 'dp', perm=[(0, 1), (1, 0)])  12.7 us
    dot_general x2, matrix products, gate_up(): jnp.einsum('rd,djf->rjf', row_block, weight, preferred_element_type=jnp.f...  11.8 us
    ppermute x3, starting transfers between devices, gather_dp(): partner = lax.ppermute(block, 'dp', perm=[(0, 1), (1, 0)])  5.04 us
    dot_general x1, matrix products, per_device(): jnp.einsum('gpi,gic->gpc', spare_pick, grouped, preferred_element_type=jn...  5.04 us
  transfers between devices with their start and end apart: 5, of which 4 were waited for; matrix products, arithmetic and copies ran while one was open for 12% of the time, Pallas kernels for 0%

profile of v9, /device:TPU:0, one launch (start us, length us, event | category | flops | bytes accessed | tf_op | source)
XLA Modules:
  0.0 228.6 jit_solution(7721407174150498209)
XLA Ops:
  6.5 0.0 copy-start
  6.5 3.0 %collective-permute-start = (bf16[64,2048]{1,0:T(8,128)(2,1)}, bf16[64,2048]{1,0:T(8,128)(2,1)S(1)}, u32[]{:S(2)}, u32[]{:S(2)}) collective-permute-start(bf16[64,2048]{1,0:T(8,128)(2,1)} %param.9), channel_id=1, source_target_pairs={{0,1},{1,0},{2,3},{3,2},{4,5},{5,4},{6,7},{7,6},{8,9},{9,8},{10,11... | collective-permute-start | bytes 786440 | tf_op jit(solution)/shard_map/ppermute | solution.py:46
  9.5 0.7 convert_element_type.67
  10.2 0.8 fusion.49
  11.0 0.1 copy.56
  11.1 4.9 %collective-permute-done = bf16[64,2048]{1,0:T(8,128)(2,1)S(1)} collective-permute-done((bf16[64,2048]{1,0:T(8,128)(2,1)}, bf16[64,2048]{1,0:T(8,128)(2,1)S(1)}, u32[]{:S(2)}, u32[]{:S(2)}) %collective-permute-start) | collective-permute-done | bytes 262176 | tf_op jit(solution)/shard_map/ppermute | solution.py:46
  16.0 1.0 broadcast_select_fusion.5
  17.0 0.9 fusion.28
  17.9 0.0 all-gather.2.cloned.1.call-update
  17.9 0.0 reduce-scatter.2.cloned.1.call-start
  18.0 1.2 dynamic_slice.6
  19.3 1.2 dynamic_slice.7
  20.5 1.3 fusion.42
  22.4 1.3 compare_reduce_fusion
  24.3 71.9 %all-gather.2.cloned.1.call-done = bf16[1024,4224]{1,0:T(8,128)(2,1)} async-done(((bf16[64,4224]{1,0:T(8,128)(2,1)}), bf16[1024,4224]{1,0:T(8,128)(2,1)}) %all-gather.2.cloned.1.call-update) | async-done | bytes 8650768 | tf_op jit(solution)/shard_map/all_gather | solution.py:76
  96.2 1.8 convert_compare_fusion.1
  97.9 0.3 eq.64
  98.3 0.3 eq.73
  98.7 0.3 compare_and_fusion.1
  98.9 0.2 copy.44
  99.1 0.2 copy.45
  99.3 0.9 compare_and_fusion
  100.1 0.2 copy.49
  100.3 0.2 copy.50
  100.5 0.1 copy.46
  100.6 0.1 copy.47
  100.8 0.1 copy.51
  100.9 0.1 copy.52
  101.0 0.0 slice-start
  101.0 0.5 fusion.18
  101.5 0.5 fusion.20
  102.0 0.0 slice-start.1
  102.1 0.0 slice-start.2
  102.1 5.0 %convolution_convert_fusion = bf16[16,32,4224]{2,1,0:T(8,128)(2,1)S(1)} fusion(pred[16,64,32]{1,2,0:T(8,128)(4,1)S(1)} %fusion.20, bf16[16,64,4224]{2,1,0:T(8,128)(2,1)} %bitcast.76), kind=kOutput, calls=%fused_computation.6 | convolution fusion | flops 278986752 | bytes 13008896 | tf_op jit(solution)/shard_map/gpi,gic->gpc/dot_general | solution.py:111
  107.1 0.1 slice-done.1
  107.2 0.0 slice-done.2
  107.2 1.3 convolution_convert_fusion.1
  108.5 0.9 copy-done.4
  109.4 2.4 %fusion.4 = f32[512,2,256]{0,2,1:T(8,128)S(1)} fusion(bf16[512,4224]{1,0:T(8,128)(2,1)S(1)} %bitcast.81, bf16[4096,2,256]{2,1,0:T(2,128)(2,1)S(1)} %bitcast.90), kind=kOutput, calls=%fused_computation.9 | convolution fusion | flops 2147483648 | bytes 9437184 | tf_op jit(solution)/shard_map/rd,djf->rjf/dot_general | solution.py:8
  111.8 0.9 fusion.30
  112.7 1.5 collective-permute-start.2
  114.1 9.5 %fusion.2 = f32[512,2,512]{0,2,1:T(8,128)} fusion(bf16[4096,2,512]{2,1,0:T(2,128)(2,1)} %bitcast.89, bf16[512,4224]{1,0:T(8,128)(2,1)S(1)} %bitcast.80), kind=kOutput, calls=%fused_computation.4 | convolution fusion | flops 4294967296 | bytes 14680064 | tf_op jit(solution)/shard_map/rd,djf->rjf/dot_general | solution.py:8
  123.6 2.7 %fusion.24 = bf16[512,512]{0,1:T(8,128)(2,1)} fusion(f32[512,2,512]{0,2,1:T(8,128)} %fusion.2), kind=kLoop, calls=%fused_computation.35 | loop fusion | flops 1572864 | bytes 2621440 | tf_op jit(solution)/shard_map/convert_element_type | solution.py:9
  126.3 0.1 slice_convert_fusion
  126.4 1.2 fusion.47
  127.6 1.0 reshape.57
  128.6 1.0 reshape.52
  129.6 0.2 copy.53
  129.8 0.6 collective-permute-start.1
  130.4 1.6 select_reduce_fusion.1
  132.0 0.0 collective-permute-done.2
  132.0 1.2 broadcast_select_fusion.3
  133.2 1.3 subtract_convert_fusion
  134.5 0.0 copy-start.5
  134.6 1.6 fusion.5
  136.1 7.7 %collective-permute-done.1 = bf16[512,512]{0,1:T(8,128)(2,1)S(1)} collective-permute-done((bf16[512,512]{0,1:T(8,128)(2,1)}, bf16[512,512]{0,1:T(8,128)(2,1)S(1)}, u32[]{:S(2)}, u32[]{:S(2)}) %collective-permute-start.1) | collective-permute-done | bytes 524320 | tf_op jit(solution)/shard_map/ppermute | solution.py:46
  143.9 0.0 copy-done.1
  143.9 0.5 broadcast_select_fusion.1
  144.4 0.0 copy-done.5
  144.4 2.4 %fusion.12 = bf16[512,2048]{1,0:T(8,128)(2,1)S(1)} fusion(bf16[1,1024,2048]{2,1,0:T(8,128)(2,1)S(1)} %copy-done.5, bf16[512,512]{0,1:T(8,128)(2,1)S(1)} %get-tuple-element.14, bf16[512,512]{0,1:T(8,128)(2,1)S(1)} %get-tuple-element.13), kind=kOutput, calls=%fused_computation.19 | convolution fusion | flops 2150629376 | bytes 7340032 | tf_op jit(solution)/shard_map/dot_general | solution.py:118
  146.9 1.3 fusion.50
  148.2 3.7 %fusion.1 = bf16[1024,2048]{1,0:T(8,128)(2,1)} fusion(f32[16,64,2048]{2,1,0:T(8,128)S(1)} %fusion.5, f32[16,64,2048]{2,1,0:T(8,128)S(1)} %fusion.50, f32[1024]{0:T(1024)S(1)} %get-tuple-element.6, f32[1024]{0:T(1024)S(1)} %get-tuple-element.5), kind=kLoop, calls=%fused_computation.2 | loop fusion | flops 8388608 | bytes 20979712 | tf_op jit(solution)/shard_map/convert_element_type | solution.py:136
  151.8 0.0 reduce-scatter.2.cloned.1.call-update
  151.9 69.9 %reduce-scatter.2.cloned.1.call-done = bf16[64,2048]{1,0:T(8,128)(2,1)} async-done(((bf16[1024,2048]{1,0:T(8,128)(2,1)}), bf16[64,2048]{1,0:T(8,128)(2,1)}) %reduce-scatter.2.cloned.1.call-update) | async-done | bytes 262160 | tf_op jit(solution)/shard_map/reduce_scatter | solution.py:136
  (11 shorter events, 0.0 us)
Async XLA Ops:
  6.5 126.7 %copy-start = (bf16[1,512,2048]{2,1,0:T(8,128)(2,1)S(1)}, bf16[1,512,2048]{2,1,0:T(8,128)(2,1)}, u32[]{:S(2)}) copy-start(bf16[1,512,2048]{2,1,0:T(8,128)(2,1)} %param.17) | copy-start | bytes 6291460
  6.5 89.6 %all-gather.2.cloned.1.call-start = ((), (), s32[]{:S(2)}) async-start(), calls=%async_computation.1 | async-start | bytes 9191424 | tf_op jit(solution)/shard_map/all_gather | solution.py:76
  6.5 9.5 %collective-permute-start = (bf16[64,2048]{1,0:T(8,128)(2,1)}, bf16[64,2048]{1,0:T(8,128)(2,1)S(1)}, u32[]{:S(2)}, u32[]{:S(2)}) collective-permute-start(bf16[64,2048]{1,0:T(8,128)(2,1)} %param.9), channel_id=1, source_target_pairs={{0,1},{1,0},{2,3},{3,2},{4,5},{5,4},{6,7},{7,6},{8,9},{9,8},{10,11... | collective-permute-start | bytes 786440 | tf_op jit(solution)/shard_map/ppermute | solution.py:46
  17.9 203.9 %reduce-scatter.2.cloned.1.call-start = ((), (), s32[]{:S(2)}) async-start(), calls=%async_computation.2 | async-start | bytes 4456448 | tf_op jit(solution)/shard_map/reduce_scatter | solution.py:136
  101.0 6.1 %slice-start = ((s8[8650752]{0:T(1024)(128)(4,1)}), s8[4194304]{0:T(1024)(128)(4,1)S(1)}, s32[]{:S(2)}) async-start(s8[8650752]{0:T(1024)(128)(4,1)} %bitcast.77), calls=%async_computation.3 | async-start | bytes 8388608
  102.0 5.1 %copy-start.2 = (pred[16,64,32]{1,2,0:T(8,128)(4,1)}, pred[16,64,32]{1,2,0:T(8,128)(4,1)S(1)}, u32[]{:S(2)}) copy-start(pred[16,64,32]{1,2,0:T(8,128)(4,1)S(1)} %fusion.20) | copy-start | bytes 98308
  102.0 5.2 %slice-start.1 = ((s8[8650752]{0:T(1024)(128)(4,1)}), s8[4194304]{0:T(1024)(128)(4,1)S(1)}, s32[]{:S(2)}) async-start(s8[8650752]{0:T(1024)(128)(4,1)} %bitcast.77), calls=%async_computation.4 | async-start | bytes 8388608
  102.1 5.2 %slice-start.2 = ((s8[8650752]{0:T(1024)(128)(4,1)}), s8[262144]{0:T(1024)(128)(4,1)S(1)}, s32[]{:S(2)}) async-start(s8[8650752]{0:T(1024)(128)(4,1)} %bitcast.77), calls=%async_computation.5 | async-start | bytes 524288
  107.2 2.2 copy-start.4
  112.7 19.4 %collective-permute-start.2 = (bf16[512,256]{0,1:T(8,128)(2,1)}, bf16[512,256]{0,1:T(8,128)(2,1)}, u32[]{:S(2)}, u32[]{:S(2)}) collective-permute-start(bf16[512,256]{0,1:T(8,128)(2,1)} %fusion.30), channel_id=1, source_target_pairs={{0,1},{1,0},{2,3},{3,2},{4,5},{5,4},{6,7},{7,6},{8,9},{9,8},{10,11... | collective-permute-start | bytes 786440 | tf_op jit(solution)/shard_map/ppermute | solution.py:46
  123.6 6.0 %copy-start.3 = (pred[16,64,32]{1,2,0:T(8,128)(4,1)S(1)}, pred[16,64,32]{1,2,0:T(8,128)(4,1)}, u32[]{:S(2)}) copy-start(pred[16,64,32]{1,2,0:T(8,128)(4,1)} %copy-done.2) | copy-start | bytes 98308
  129.8 14.1 %collective-permute-start.1 = (bf16[512,512]{0,1:T(8,128)(2,1)}, bf16[512,512]{0,1:T(8,128)(2,1)S(1)}, u32[]{:S(2)}, u32[]{:S(2)}) collective-permute-start(bf16[512,512]{0,1:T(8,128)(2,1)} %fusion.24), channel_id=1, source_target_pairs={{0,1},{1,0},{2,3},{3,2},{4,5},{5,4},{6,7},{7,6},{8,9},{9,8},{10,11... | collective-permute-start | bytes 1572872 | tf_op jit(solution)/shard_map/ppermute | solution.py:46
  134.5 9.3 %copy-start.1 = (f32[512,2,512]{0,2,1:T(8,128)S(1)}, f32[512,2,512]{0,2,1:T(8,128)}, u32[]{:S(2)}) copy-start(f32[512,2,512]{0,2,1:T(8,128)} %fusion.2) | copy-start | bytes 6291460
  134.5 9.8 %copy-start.5 = (bf16[1,1024,2048]{2,1,0:T(8,128)(2,1)S(1)}, bf16[1,1024,2048]{2,1,0:T(8,128)(2,1)}, u32[]{:S(2)}) copy-start(bf16[1,1024,2048]{2,1,0:T(8,128)(2,1)} %param.15) | copy-start | bytes 12582916
Sparse Core Ops, SparseCore 0:
  18.1 78.0 all-gather.1
  152.0 69.7 reduce-scatter.1

commit v10 on v9

--- a/solution.py
+++ b/solution.py
@@ -112,9 +112,9 @@
         "gpi,gic->gpc", spare_pick, grouped, preferred_element_type=jnp.float32
     ).astype(jnp.bfloat16).reshape(slot_rows, -1)
     home_hidden = gate_up(home_rows[:, :d_model], gate_up_weight[0])
-    spare_hidden = gate_up(spare_rows[:, :d_model], spare_gate_up[0])
+    home_hidden, spare_rows = lax.optimization_barrier((home_hidden, spare_rows))
     home_hidden = gather_dp(home_hidden, 1)
-    spare_hidden = gather_dp(spare_hidden, 1)
+    spare_hidden = gather_dp(gate_up(spare_rows[:, :d_model], spare_gate_up[0]), 1)
     home_out = jnp.dot(home_hidden, down_weight[0], preferred_element_type=jnp.float32)
     home_out = home_out.astype(jnp.bfloat16).reshape(ep_count, capacity, -1)
     spare_out = jnp.dot(spare_hidden, spare_down[0], preferred_element_type=jnp.float32)

time: 229 us -> 226 us (0.987)
  transfers between devices with their start and end apart: 5 -> 5, of which waited for: 4 -> 5; matrix products, arithmetic and copies ran while one was open for 12% -> 6% of each run, Pallas kernels for 0% -> 0%
where the time goes in v10:
time: 226 us; the launch traced here: 225 us
  waiting for transfers between devices  157 us (69%)
  matrix products  23.8 us (11%)
  other arithmetic  18.5 us (8%)
  between operations  15.1 us (7%)
  local copies, waits for them, and re-layouts  5.53 us (2%)
  starting transfers between devices  5.1 us (2%)
    all_gather x1, waiting for transfers between devices, per_device(): every_row = lax.all_gather(packed, 'ep', axis=0, tiled=True)  71.5 us
    reduce_scatter x1, waiting for transfers between devices, per_device(): lax.psum_scatter(partial.astype(jnp.bfloat16), 'ep', scatter_dimension=0,...  70.7 us
    ppermute x3, waiting for transfers between devices, gather_dp(): partner = lax.ppermute(block, 'dp', perm=[(0, 1), (1, 0)])  14.9 us
    dot_general x2, matrix products, gate_up(): jnp.einsum('rd,djf->rjf', row_block, weight, preferred_element_type=jnp.f...  9.81 us
    ppermute x3, starting transfers between devices, gather_dp(): partner = lax.ppermute(block, 'dp', perm=[(0, 1), (1, 0)])  5.06 us
    dot_general x1, matrix products, per_device(): jnp.einsum('gpi,gic->gpc', spare_pick, grouped, preferred_element_type=jn...  5.03 us
  transfers between devices with their start and end apart: 5, of which 5 were waited for; matrix products, arithmetic and copies ran while one was open for 6% of the time, Pallas kernels for 0%

profile of v10, /device:TPU:0, one launch (start us, length us, event | category | flops | bytes accessed | tf_op | source)
XLA Modules:
  0.0 225.2 jit_solution(4207617745241658118)
XLA Ops:
  6.5 0.0 copy-start
  6.5 0.0 all-gather.2.cloned.1.call-start
  6.5 3.0 %collective-permute-start = (bf16[64,2048]{1,0:T(8,128)(2,1)}, bf16[64,2048]{1,0:T(8,128)(2,1)S(1)}, u32[]{:S(2)}, u32[]{:S(2)}) collective-permute-start(bf16[64,2048]{1,0:T(8,128)(2,1)} %param.9), channel_id=1, source_target_pairs={{0,1},{1,0},{2,3},{3,2},{4,5},{5,4},{6,7},{7,6},{8,9},{9,8},{10,11... | collective-permute-start | bytes 786440 | tf_op jit(solution)/shard_map/ppermute | solution.py:46
  9.5 0.7 convert_element_type.67
  10.2 0.8 fusion.51
  11.0 0.1 copy.56
  11.1 4.9 %collective-permute-done = bf16[64,2048]{1,0:T(8,128)(2,1)S(1)} collective-permute-done((bf16[64,2048]{1,0:T(8,128)(2,1)}, bf16[64,2048]{1,0:T(8,128)(2,1)S(1)}, u32[]{:S(2)}, u32[]{:S(2)}) %collective-permute-start) | collective-permute-done | bytes 262176 | tf_op jit(solution)/shard_map/ppermute | solution.py:46
  16.0 1.0 broadcast_select_fusion.5
  17.0 0.9 fusion.30
  17.9 0.0 all-gather.2.cloned.1.call-update
  17.9 0.0 reduce-scatter.2.cloned.1.call-start
  18.0 1.2 dynamic_slice.6
  19.3 1.3 dynamic_slice.7
  20.5 1.4 fusion.44
  22.6 1.4 compare_reduce_fusion
  24.6 71.5 %all-gather.2.cloned.1.call-done = bf16[1024,4224]{1,0:T(8,128)(2,1)} async-done(((bf16[64,4224]{1,0:T(8,128)(2,1)}), bf16[1024,4224]{1,0:T(8,128)(2,1)}) %all-gather.2.cloned.1.call-update) | async-done | bytes 8650768 | tf_op jit(solution)/shard_map/all_gather | solution.py:76
  96.2 1.8 convert_compare_fusion
  97.9 0.3 eq.73
  98.3 0.3 eq.64
  98.7 0.9 compare_and_fusion
  99.5 0.2 copy.49
  99.7 0.2 copy.50
  99.9 0.3 compare_and_fusion.1
  100.1 0.2 copy.44
  100.3 0.2 copy.45
  100.5 0.1 copy.51
  100.6 0.1 copy.52
  100.7 0.1 copy.46
  100.9 0.1 copy.47
  101.0 0.0 slice-start
  101.0 0.5 fusion.22
  101.5 0.5 fusion.20
  102.0 0.0 slice-start.1
  102.0 0.0 slice-start.2
  102.1 5.0 %convolution_convert_fusion = bf16[16,32,4224]{2,1,0:T(8,128)(2,1)S(1)} fusion(pred[16,64,32]{1,2,0:T(8,128)(4,1)S(1)} %fusion.22, bf16[16,64,4224]{2,1,0:T(8,128)(2,1)} %bitcast.72), kind=kOutput, calls=%fused_computation.6 | convolution fusion | flops 278986752 | bytes 13008896 | tf_op jit(solution)/shard_map/gpi,gic->gpc/dot_general | solution.py:111
  107.1 0.0 slice-done
  107.1 0.1 slice-done.1
  107.2 1.3 convolution_convert_fusion.1
  108.5 0.0 copy-start.2
  108.5 7.4 %fusion.2 = f32[512,2,512]{2,0,1:T(8,128)S(1)} fusion(bf16[4096,2,512]{2,1,0:T(2,128)(2,1)} %bitcast.85, bf16[512,4224]{1,0:T(8,128)(2,1)S(1)} %bitcast.77), kind=kOutput, calls=%fused_computation.4 | convolution fusion | flops 4294967296 | bytes 14680064 | tf_op jit(solution)/shard_map/rd,djf->rjf/dot_general | solution.py:8
  116.0 1.1 fusion.26
  117.1 0.0 copy-done.2
  117.1 2.4 %fusion.8 = f32[512,2,256]{0,2,1:T(8,128)S(1)} fusion(bf16[4096,2,256]{2,1,0:T(2,128)(2,1)S(1)} %bitcast.86, bf16[512,4224]{1,0:T(8,128)(2,1)S(1)} %bitcast.76), kind=kOutput, calls=%fused_computation.13 | convolution fusion | flops 2147483648 | bytes 9437184 | tf_op jit(solution)/shard_map/rd,djf->rjf/dot_general | solution.py:8
  119.5 0.9 fusion.32
  120.3 1.5 collective-permute-start.2
  121.8 0.1 slice_convert_fusion
  121.9 1.1 fusion.49
  123.1 0.4 reshape.52
  123.4 0.4 reshape.58
  123.8 0.2 copy.53
  124.0 0.6 collective-permute-start.1
  124.6 1.5 select_reduce_fusion.1
  126.2 3.6 %collective-permute-done.2 = bf16[512,256]{0,1:T(8,128)(2,1)} collective-permute-done((bf16[512,256]{0,1:T(8,128)(2,1)}, bf16[512,256]{0,1:T(8,128)(2,1)}, u32[]{:S(2)}, u32[]{:S(2)}) %collective-permute-start.2) | collective-permute-done | bytes 262176 | tf_op jit(solution)/shard_map/ppermute | solution.py:46
  129.8 1.2 broadcast_select_fusion.3
  130.9 1.3 subtract_convert_fusion
  132.3 0.0 copy-start.3
  132.3 1.6 fusion.4
  133.8 6.4 %collective-permute-done.1 = bf16[512,512]{1,0:T(8,128)(2,1)S(1)} collective-permute-done((bf16[512,512]{1,0:T(8,128)(2,1)}, bf16[512,512]{1,0:T(8,128)(2,1)S(1)}, u32[]{:S(2)}, u32[]{:S(2)}) %collective-permute-start.1) | collective-permute-done | bytes 524320 | tf_op jit(solution)/shard_map/ppermute | solution.py:46
  140.2 0.1 broadcast_select_fusion.1
  140.3 2.3 %fusion.14 = bf16[512,2048]{1,0:T(8,128)(2,1)S(1)} fusion(bf16[1,1024,2048]{2,1,0:T(8,128)(2,1)S(1)} %copy-done.3, bf16[512,512]{1,0:T(8,128)(2,1)S(1)} %get-tuple-element.18, bf16[512,512]{1,0:T(8,128)(2,1)S(1)} %get-tuple-element.17), kind=kOutput, calls=%fused_computation.20 | convolution fusion | flops 2150629376 | bytes 7340032 | tf_op jit(solution)/shard_map/dot_general | solution.py:118
  142.7 1.3 fusion.52
  144.0 3.7 %fusion.1 = bf16[1024,2048]{1,0:T(8,128)(2,1)} fusion(f32[16,64,2048]{2,1,0:T(8,128)S(1)} %fusion.4, f32[16,64,2048]{2,1,0:T(8,128)S(1)} %fusion.52, f32[1024]{0:T(1024)S(1)} %get-tuple-element.10, f32[1024]{0:T(1024)S(1)} %get-tuple-element.9), kind=kLoop, calls=%fused_computation.2 | loop fusion | flops 8388608 | bytes 20979712 | tf_op jit(solution)/shard_map/convert_element_type | solution.py:136
  147.6 0.0 reduce-scatter.2.cloned.1.call-update
  147.7 70.7 %reduce-scatter.2.cloned.1.call-done = bf16[64,2048]{1,0:T(8,128)(2,1)} async-done(((bf16[1024,2048]{1,0:T(8,128)(2,1)}), bf16[64,2048]{1,0:T(8,128)(2,1)}) %reduce-scatter.2.cloned.1.call-update) | async-done | bytes 262160 | tf_op jit(solution)/shard_map/reduce_scatter | solution.py:136
  (7 shorter events, 0.0 us)
Async XLA Ops:
  6.5 124.4 %copy-start = (bf16[1,512,2048]{2,1,0:T(8,128)(2,1)S(1)}, bf16[1,512,2048]{2,1,0:T(8,128)(2,1)}, u32[]{:S(2)}) copy-start(bf16[1,512,2048]{2,1,0:T(8,128)(2,1)} %param.17) | copy-start | bytes 6291460
  6.5 89.6 %all-gather.2.cloned.1.call-start = ((), (), s32[]{:S(2)}) async-start(), calls=%async_computation.1 | async-start | bytes 9191424 | tf_op jit(solution)/shard_map/all_gather | solution.py:76
  6.5 9.5 %collective-permute-start = (bf16[64,2048]{1,0:T(8,128)(2,1)}, bf16[64,2048]{1,0:T(8,128)(2,1)S(1)}, u32[]{:S(2)}, u32[]{:S(2)}) collective-permute-start(bf16[64,2048]{1,0:T(8,128)(2,1)} %param.9), channel_id=1, source_target_pairs={{0,1},{1,0},{2,3},{3,2},{4,5},{5,4},{6,7},{7,6},{8,9},{9,8},{10,11... | collective-permute-start | bytes 786440 | tf_op jit(solution)/shard_map/ppermute | solution.py:46
  17.9 200.4 %reduce-scatter.2.cloned.1.call-start = ((), (), s32[]{:S(2)}) async-start(), calls=%async_computation.2 | async-start | bytes 4456448 | tf_op jit(solution)/shard_map/reduce_scatter | solution.py:136
  101.0 6.1 %slice-start = ((s8[8650752]{0:T(1024)(128)(4,1)}), s8[4194304]{0:T(1024)(128)(4,1)S(1)}, s32[]{:S(2)}) async-start(s8[8650752]{0:T(1024)(128)(4,1)} %bitcast.73), calls=%async_computation.3 | async-start | bytes 8388608
  102.0 5.2 %slice-start.1 = ((s8[8650752]{0:T(1024)(128)(4,1)}), s8[4194304]{0:T(1024)(128)(4,1)S(1)}, s32[]{:S(2)}) async-start(s8[8650752]{0:T(1024)(128)(4,1)} %bitcast.73), calls=%async_computation.4 | async-start | bytes 8388608
  102.0 5.2 %slice-start.2 = ((s8[8650752]{0:T(1024)(128)(4,1)}), s8[262144]{0:T(1024)(128)(4,1)S(1)}, s32[]{:S(2)}) async-start(s8[8650752]{0:T(1024)(128)(4,1)} %bitcast.73), calls=%async_computation.5 | async-start | bytes 524288
  108.5 8.6 %copy-start.2 = (bf16[1,4096,2,256]{3,2,1,0:T(2,128)(2,1)S(1)}, bf16[1,4096,2,256]{3,2,1,0:T(2,128)(2,1)}, u32[]{:S(2)}) copy-start(bf16[1,4096,2,256]{3,2,1,0:T(2,128)(2,1)} %param.16) | copy-start | bytes 12582916
  120.3 9.5 %collective-permute-start.2 = (bf16[512,256]{0,1:T(8,128)(2,1)}, bf16[512,256]{0,1:T(8,128)(2,1)}, u32[]{:S(2)}, u32[]{:S(2)}) collective-permute-start(bf16[512,256]{0,1:T(8,128)(2,1)} %fusion.32), channel_id=1, source_target_pairs={{0,1},{1,0},{2,3},{3,2},{4,5},{5,4},{6,7},{7,6},{8,9},{9,8},{10,11... | collective-permute-start | bytes 786440 | tf_op jit(solution)/shard_map/ppermute | solution.py:46
  124.0 16.2 %collective-permute-start.1 = (bf16[512,512]{1,0:T(8,128)(2,1)}, bf16[512,512]{1,0:T(8,128)(2,1)S(1)}, u32[]{:S(2)}, u32[]{:S(2)}) collective-permute-start(bf16[512,512]{1,0:T(8,128)(2,1)} %fusion.26), channel_id=1, source_target_pairs={{0,1},{1,0},{2,3},{3,2},{4,5},{5,4},{6,7},{7,6},{8,9},{9,8},{10,11... | collective-permute-start | bytes 1572872 | tf_op jit(solution)/shard_map/ppermute | solution.py:46
  132.3 8.0 %copy-start.1 = (bf16[512,512]{1,0:T(8,128)(2,1)S(1)}, bf16[512,512]{1,0:T(8,128)(2,1)}, u32[]{:S(2)}) copy-start(bf16[512,512]{1,0:T(8,128)(2,1)} %fusion.26) | copy-start | bytes 1572868
  132.3 8.0 %copy-start.3 = (bf16[1,1024,2048]{2,1,0:T(8,128)(2,1)S(1)}, bf16[1,1024,2048]{2,1,0:T(8,128)(2,1)}, u32[]{:S(2)}) copy-start(bf16[1,1024,2048]{2,1,0:T(8,128)(2,1)} %param.15) | copy-start | bytes 12582916
Sparse Core Ops, SparseCore 0:
  18.1 78.0 all-gather.1
  147.8 70.5 reduce-scatter.1

commit v11 on v10

--- a/solution.py
+++ b/solution.py
@@ -105,12 +105,14 @@
 
     grouped = every_row.reshape(ep_count, group_tokens, -1)
     slot_rows = ep_count * capacity
-    home_rows = jnp.einsum(
-        "gpi,gic->gpc", home_pick, grouped, preferred_element_type=jnp.float32
-    ).astype(jnp.bfloat16).reshape(slot_rows, -1)
-    spare_rows = jnp.einsum(
-        "gpi,gic->gpc", spare_pick, grouped, preferred_element_type=jnp.float32
-    ).astype(jnp.bfloat16).reshape(slot_rows, -1)
+    rows = jnp.einsum(
+        "gpi,gic->gpc",
+        jnp.concatenate([home_pick, spare_pick], axis=1),
+        grouped,
+        preferred_element_type=jnp.float32,
+    ).astype(jnp.bfloat16)
+    home_rows = rows[:, :capacity].reshape(slot_rows, -1)
+    spare_rows = rows[:, capacity:].reshape(slot_rows, -1)
     home_hidden = gate_up(home_rows[:, :d_model], gate_up_weight[0])
     home_hidden, spare_rows = lax.optimization_barrier((home_hidden, spare_rows))
     home_hidden = gather_dp(home_hidden, 1)

time: 226 us -> 226 us (level)
    dot_general x2 -> x1, matrix products: 6.33 us -> 5.83 us  [per_device(): jnp.einsum('gpi,gic->gpc', jnp.concatenate([home_pick, spare_pick], axis=...]
  transfers between devices with their start and end apart: 5 -> 5, of which waited for: 5 -> 5; matrix products, arithmetic and copies ran while one was open for 6% -> 7% of each run, Pallas kernels for 0% -> 0%
where the time goes in v11:
time: 226 us; the launch traced here: 225 us
  waiting for transfers between devices  157 us (69%)
  matrix products  23.2 us (10%)
  other arithmetic  19.4 us (9%)
  between operations  14.8 us (7%)
  local copies, waits for them, and re-layouts  6.28 us (3%)
  starting transfers between devices  5.1 us (2%)
    all_gather x1, waiting for transfers between devices, per_device(): every_row = lax.all_gather(packed, 'ep', axis=0, tiled=True)  71.8 us
    reduce_scatter x1, waiting for transfers between devices, per_device(): lax.psum_scatter(partial.astype(jnp.bfloat16), 'ep', scatter_dimension=0,...  70.7 us
    ppermute x3, waiting for transfers between devices, gather_dp(): partner = lax.ppermute(block, 'dp', perm=[(0, 1), (1, 0)])  14 us
    dot_general x2, matrix products, gate_up(): jnp.einsum('rd,djf->rjf', row_block, weight, preferred_element_type=jnp.f...  9.62 us
    dot_general x1, matrix products, per_device(): jnp.einsum('gpi,gic->gpc', jnp.concatenate([home_pick, spare_pick], axis=...  5.83 us
    ppermute x3, starting transfers between devices, gather_dp(): partner = lax.ppermute(block, 'dp', perm=[(0, 1), (1, 0)])  5.06 us
  transfers between devices with their start and end apart: 5, of which 5 were waited for; matrix products, arithmetic and copies ran while one was open for 7% of the time, Pallas kernels for 0%

profile of v11, /device:TPU:0, one launch (start us, length us, event | category | flops | bytes accessed | tf_op | source)
XLA Modules:
  0.0 225.3 jit_solution(6869626213176107499)
XLA Ops:
  6.5 0.0 copy-start
  6.5 0.0 all-gather.2.cloned.1.call-start
  6.5 3.0 %collective-permute-start = (bf16[64,2048]{1,0:T(8,128)(2,1)}, bf16[64,2048]{1,0:T(8,128)(2,1)S(1)}, u32[]{:S(2)}, u32[]{:S(2)}) collective-permute-start(bf16[64,2048]{1,0:T(8,128)(2,1)} %param.9), channel_id=1, source_target_pairs={{0,1},{1,0},{2,3},{3,2},{4,5},{5,4},{6,7},{7,6},{8,9},{9,8},{10,11... | collective-permute-start | bytes 786440 | tf_op jit(solution)/shard_map/ppermute | solution.py:46
  9.5 0.7 convert_element_type.70
  10.2 0.8 fusion.56
  11.0 0.1 copy.56
  11.1 4.9 %collective-permute-done = bf16[64,2048]{1,0:T(8,128)(2,1)S(1)} collective-permute-done((bf16[64,2048]{1,0:T(8,128)(2,1)}, bf16[64,2048]{1,0:T(8,128)(2,1)S(1)}, u32[]{:S(2)}, u32[]{:S(2)}) %collective-permute-start) | collective-permute-done | bytes 262176 | tf_op jit(solution)/shard_map/ppermute | solution.py:46
  16.0 1.0 broadcast_select_fusion.5
  17.0 0.9 fusion.30
  17.9 0.0 all-gather.2.cloned.1.call-update
  17.9 0.0 reduce-scatter.2.cloned.1.call-start
  18.0 1.2 dynamic_slice.6
  19.2 1.3 dynamic_slice.7
  20.5 1.3 fusion.47
  22.4 1.3 compare_reduce_fusion
  24.3 71.8 %all-gather.2.cloned.1.call-done = bf16[1024,4224]{1,0:T(8,128)(2,1)} async-done(((bf16[64,4224]{1,0:T(8,128)(2,1)}), bf16[1024,4224]{1,0:T(8,128)(2,1)}) %all-gather.2.cloned.1.call-update) | async-done | bytes 8650768 | tf_op jit(solution)/shard_map/all_gather | solution.py:76
  96.1 1.8 convert_compare_fusion.1
  97.9 0.3 eq.64
  98.3 0.3 eq.73
  98.6 0.3 compare_and_fusion.1
  98.9 0.2 copy.44
  99.1 0.2 copy.45
  99.2 0.9 compare_and_fusion
  100.2 0.2 copy.48
  100.4 0.2 copy.49
  100.5 0.1 copy.46
  100.7 0.1 copy.47
  100.8 0.1 copy.50
  100.9 0.1 copy.51
  101.1 0.5 fusion.20
  101.6 0.5 fusion.22
  102.1 5.8 %convolution_convert_fusion = bf16[16,64,4224]{2,1,0:T(8,128)(2,1)S(1)} fusion(bf16[16,64,4224]{2,1,0:T(8,128)(2,1)} %bitcast.71, pred[16,32,64]{2,1,0:T(8,128)(4,1)S(1)} %bitcast.80, pred[16,32,64]{2,1,0:T(8,128)(4,1)S(1)} %bitcast.79), kind=kOutput, calls=%fused_computation | convolution fusion | flops 558039040 | bytes 17367040 | tf_op jit(solution)/shard_map/gpi,gic->gpc/dot_general | solution.py:108
  107.9 0.8 fusion.55
  108.7 0.0 copy-start.2
  108.8 7.3 %fusion.2 = f32[512,2,512]{2,0,1:T(8,128)S(1)} fusion(bf16[4096,2,512]{2,1,0:T(2,128)(2,1)} %bitcast.83, bf16[512,4224]{1,0:T(8,128)(2,1)S(1)} %bitcast.73), kind=kOutput, calls=%fused_computation.5 | convolution fusion | flops 4294967296 | bytes 14680064 | tf_op jit(solution)/shard_map/rd,djf->rjf/dot_general | solution.py:8
  116.0 1.2 fusion.26
  117.2 0.0 copy-done.2
  117.2 2.4 %fusion.8 = f32[512,2,256]{0,2,1:T(8,128)S(1)} fusion(bf16[4096,2,256]{2,1,0:T(2,128)(2,1)S(1)} %bitcast.84, bf16[512,4224]{1,0:T(8,128)(2,1)S(1)} %bitcast.72), kind=kOutput, calls=%fused_computation.12 | convolution fusion | flops 2147483648 | bytes 9437184 | tf_op jit(solution)/shard_map/rd,djf->rjf/dot_general | solution.py:8
  119.6 0.9 fusion.32
  120.4 1.5 collective-permute-start.2
  121.9 1.1 slice_convert_fusion
  123.0 1.1 fusion.53
  124.1 0.4 reshape.58
  124.5 0.4 reshape.52
  124.8 0.2 copy.53
  125.1 0.6 collective-permute-start.1
  125.7 1.5 select_reduce_fusion.1
  127.2 2.6 %collective-permute-done.2 = bf16[512,256]{0,1:T(8,128)(2,1)} collective-permute-done((bf16[512,256]{0,1:T(8,128)(2,1)}, bf16[512,256]{0,1:T(8,128)(2,1)}, u32[]{:S(2)}, u32[]{:S(2)}) %collective-permute-start.2) | collective-permute-done | bytes 262176 | tf_op jit(solution)/shard_map/ppermute | solution.py:46
  129.9 1.2 broadcast_select_fusion.3
  131.0 0.0 copy-done
  131.0 1.3 subtract_convert_fusion
  132.4 0.0 copy-start.1
  132.4 0.0 copy-start.3
  132.4 1.6 fusion.4
  133.9 6.4 %collective-permute-done.1 = bf16[512,512]{1,0:T(8,128)(2,1)S(1)} collective-permute-done((bf16[512,512]{1,0:T(8,128)(2,1)}, bf16[512,512]{1,0:T(8,128)(2,1)S(1)}, u32[]{:S(2)}, u32[]{:S(2)}) %collective-permute-start.1) | collective-permute-done | bytes 524320 | tf_op jit(solution)/shard_map/ppermute | solution.py:46
  140.3 0.0 copy-done.1
  140.3 0.1 broadcast_select_fusion.1
  140.4 0.0 copy-done.3
  140.4 2.3 %fusion.14 = bf16[512,2048]{1,0:T(8,128)(2,1)S(1)} fusion(bf16[1,1024,2048]{2,1,0:T(8,128)(2,1)S(1)} %copy-done.3, bf16[512,512]{1,0:T(8,128)(2,1)S(1)} %get-tuple-element.20, bf16[512,512]{1,0:T(8,128)(2,1)S(1)} %get-tuple-element.19), kind=kOutput, calls=%fused_computation.19 | convolution fusion | flops 2150629376 | bytes 7340032 | tf_op jit(solution)/shard_map/dot_general | solution.py:120
  142.8 1.3 fusion.57
  144.1 3.7 %fusion.1 = bf16[1024,2048]{1,0:T(8,128)(2,1)} fusion(f32[16,64,2048]{2,1,0:T(8,128)S(1)} %fusion.4, f32[16,64,2048]{2,1,0:T(8,128)S(1)} %fusion.57, f32[1024]{0:T(1024)S(1)} %get-tuple-element.10, f32[1024]{0:T(1024)S(1)} %get-tuple-element.9), kind=kLoop, calls=%fused_computation.3 | loop fusion | flops 8388608 | bytes 20979712 | tf_op jit(solution)/shard_map/convert_element_type | solution.py:138
  147.7 0.0 reduce-scatter.2.cloned.1.call-update
  147.8 70.7 %reduce-scatter.2.cloned.1.call-done = bf16[64,2048]{1,0:T(8,128)(2,1)} async-done(((bf16[1024,2048]{1,0:T(8,128)(2,1)}), bf16[64,2048]{1,0:T(8,128)(2,1)}) %reduce-scatter.2.cloned.1.call-update) | async-done | bytes 262160 | tf_op jit(solution)/shard_map/reduce_scatter | solution.py:138
  (1 shorter events, 0.0 us)
Async XLA Ops:
  6.5 124.5 %copy-start = (bf16[1,512,2048]{2,1,0:T(8,128)(2,1)S(1)}, bf16[1,512,2048]{2,1,0:T(8,128)(2,1)}, u32[]{:S(2)}) copy-start(bf16[1,512,2048]{2,1,0:T(8,128)(2,1)} %param.17) | copy-start | bytes 6291460
  6.5 89.6 %all-gather.2.cloned.1.call-start = ((), (), s32[]{:S(2)}) async-start(), calls=%async_computation.1 | async-start | bytes 9191424 | tf_op jit(solution)/shard_map/all_gather | solution.py:76
  6.5 9.5 %collective-permute-start = (bf16[64,2048]{1,0:T(8,128)(2,1)}, bf16[64,2048]{1,0:T(8,128)(2,1)S(1)}, u32[]{:S(2)}, u32[]{:S(2)}) collective-permute-start(bf16[64,2048]{1,0:T(8,128)(2,1)} %param.9), channel_id=1, source_target_pairs={{0,1},{1,0},{2,3},{3,2},{4,5},{5,4},{6,7},{7,6},{8,9},{9,8},{10,11... | collective-permute-start | bytes 786440 | tf_op jit(solution)/shard_map/ppermute | solution.py:46
  17.9 200.5 %reduce-scatter.2.cloned.1.call-start = ((), (), s32[]{:S(2)}) async-start(), calls=%async_computation.2 | async-start | bytes 4456448 | tf_op jit(solution)/shard_map/reduce_scatter | solution.py:138
  108.7 8.4 %copy-start.2 = (bf16[1,4096,2,256]{3,2,1,0:T(2,128)(2,1)S(1)}, bf16[1,4096,2,256]{3,2,1,0:T(2,128)(2,1)}, u32[]{:S(2)}) copy-start(bf16[1,4096,2,256]{3,2,1,0:T(2,128)(2,1)} %param.16) | copy-start | bytes 12582916
  120.4 9.4 %collective-permute-start.2 = (bf16[512,256]{0,1:T(8,128)(2,1)}, bf16[512,256]{0,1:T(8,128)(2,1)}, u32[]{:S(2)}, u32[]{:S(2)}) collective-permute-start(bf16[512,256]{0,1:T(8,128)(2,1)} %fusion.32), channel_id=1, source_target_pairs={{0,1},{1,0},{2,3},{3,2},{4,5},{5,4},{6,7},{7,6},{8,9},{9,8},{10,11... | collective-permute-start | bytes 786440 | tf_op jit(solution)/shard_map/ppermute | solution.py:46
  125.1 15.3 %collective-permute-start.1 = (bf16[512,512]{1,0:T(8,128)(2,1)}, bf16[512,512]{1,0:T(8,128)(2,1)S(1)}, u32[]{:S(2)}, u32[]{:S(2)}) collective-permute-start(bf16[512,512]{1,0:T(8,128)(2,1)} %fusion.26), channel_id=1, source_target_pairs={{0,1},{1,0},{2,3},{3,2},{4,5},{5,4},{6,7},{7,6},{8,9},{9,8},{10,11... | collective-permute-start | bytes 1572872 | tf_op jit(solution)/shard_map/ppermute | solution.py:46
  132.4 8.0 %copy-start.1 = (bf16[512,512]{1,0:T(8,128)(2,1)S(1)}, bf16[512,512]{1,0:T(8,128)(2,1)}, u32[]{:S(2)}) copy-start(bf16[512,512]{1,0:T(8,128)(2,1)} %fusion.26) | copy-start | bytes 1572868
  132.4 8.0 %copy-start.3 = (bf16[1,1024,2048]{2,1,0:T(8,128)(2,1)S(1)}, bf16[1,1024,2048]{2,1,0:T(8,128)(2,1)}, u32[]{:S(2)}) copy-start(bf16[1,1024,2048]{2,1,0:T(8,128)(2,1)} %param.15) | copy-start | bytes 12582916
Sparse Core Ops, SparseCore 0:
  18.0 78.0 all-gather.1
  147.9 70.5 reduce-scatter.1

commit v12 on v11

--- a/solution.py
+++ b/solution.py
@@ -5,8 +5,11 @@
 
 
 def gate_up(row_block, weight):
-    gate_both = jnp.einsum("rd,djf->rjf", row_block, weight, preferred_element_type=jnp.float32)
-    return (jax.nn.silu(gate_both[:, 0, :]) * gate_both[:, 1, :]).astype(jnp.bfloat16)
+    units = weight.shape[2]
+    gate_both = jnp.dot(
+        row_block, weight.reshape(weight.shape[0], 2 * units), preferred_element_type=jnp.float32
+    )
+    return (jax.nn.silu(gate_both[:, :units]) * gate_both[:, units:]).astype(jnp.bfloat16)
 
 
 def slot_tables(ids, target, low, limit, capacity, top_count, gate_weight):

time: 226 us -> 226 us (level)
  local copies, waits for them, and re-layouts: 6.28 us -> 19.1 us
  waiting for transfers between devices: 157 us -> 149 us
  other arithmetic: 19.4 us -> 14.1 us
    unnamed x9 -> x15, local copies, waits for them, and re-layouts: 0.12 us -> 13.1 us
    all_gather x1, waiting for transfers between devices: 71.8 us -> 60.4 us  [per_device(): every_row = lax.all_gather(packed, 'ep', axis=0, tiled=True)]
    ppermute x3, waiting for transfers between devices: 14 us -> 17.9 us  [gather_dp(): partner = lax.ppermute(block, 'dp', perm=[(0, 1), (1, 0)])]
  transfers between devices with their start and end apart: 5 -> 5, of which waited for: 5 -> 4; matrix products, arithmetic and copies ran while one was open for 7% -> 11% of each run, Pallas kernels for 0% -> 0%
where the time goes in v12:
time: 226 us; the launch traced here: 225 us
  waiting for transfers between devices  149 us (66%)
  matrix products  22.8 us (10%)
  local copies, waits for them, and re-layouts  19.1 us (8%)
  between operations  15.1 us (7%)
  other arithmetic  14.1 us (6%)
  starting transfers between devices  5.17 us (2%)
    reduce_scatter x1, waiting for transfers between devices, per_device(): lax.psum_scatter(partial.astype(jnp.bfloat16), 'ep', scatter_dimension=0,...  70.8 us
    all_gather x1, waiting for transfers between devices, per_device(): every_row = lax.all_gather(packed, 'ep', axis=0, tiled=True)  60.4 us
    ppermute x3, waiting for transfers between devices, gather_dp(): partner = lax.ppermute(block, 'dp', perm=[(0, 1), (1, 0)])  17.9 us
    unnamed x15, local copies, waits for them, and re-layouts  13.1 us
    dot_general x2, matrix products, gate_up(): jnp.dot(row_block, weight.reshape(weight.shape[0], 2 * units), preferred_...  9.43 us
    dot_general x1, matrix products, per_device(): jnp.einsum('gpi,gic->gpc', jnp.concatenate([home_pick, spare_pick], axis=...  5.83 us
    ppermute x3, starting transfers between devices, gather_dp(): partner = lax.ppermute(block, 'dp', perm=[(0, 1), (1, 0)])  5.12 us
  transfers between devices with their start and end apart: 5, of which 4 were waited for; matrix products, arithmetic and copies ran while one was open for 11% of the time, Pallas kernels for 0%

profile of v12, /device:TPU:0, one launch (start us, length us, event | category | flops | bytes accessed | tf_op | source)
XLA Modules:
  0.0 225.5 jit_solution(7387468166079147018)
XLA Ops:
  6.5 0.0 copy-start
  6.5 0.0 all-gather.2.cloned.1.call-start
  6.5 3.0 %collective-permute-start = (bf16[64,2048]{1,0:T(8,128)(2,1)}, bf16[64,2048]{1,0:T(8,128)(2,1)S(1)}, u32[]{:S(2)}, u32[]{:S(2)}) collective-permute-start(bf16[64,2048]{1,0:T(8,128)(2,1)} %param.9), channel_id=1, source_target_pairs={{0,1},{1,0},{2,3},{3,2},{4,5},{5,4},{6,7},{7,6},{8,9},{9,8},{10,11... | collective-permute-start | bytes 786440 | tf_op jit(solution)/shard_map/ppermute | solution.py:49
  9.5 0.7 convert_element_type.70
  10.2 0.8 fusion.52
  11.0 0.1 copy.48
  11.1 4.9 %collective-permute-done = bf16[64,2048]{1,0:T(8,128)(2,1)S(1)} collective-permute-done((bf16[64,2048]{1,0:T(8,128)(2,1)}, bf16[64,2048]{1,0:T(8,128)(2,1)S(1)}, u32[]{:S(2)}, u32[]{:S(2)}) %collective-permute-start) | collective-permute-done | bytes 262176 | tf_op jit(solution)/shard_map/ppermute | solution.py:49
  16.0 1.0 broadcast_select_fusion.5
  17.0 0.8 fusion.27
  17.9 0.0 all-gather.2.cloned.1.call-update
  17.9 0.0 reduce-scatter.2.cloned.1.call-start
  17.9 1.2 dynamic_slice.6
  19.2 1.2 dynamic_slice.7
  20.4 9.5 %copy.49 = bf16[512,8,2,512]{3,1,2,0:T(8,128)(2,1)} copy(bf16[512,8,2,512]{3,2,1,0:T(2,128)(2,1)} %bitcast.48) | data formatting | bytes 16777216
  29.9 0.0 copy-done.1
  29.9 2.9 %copy.50 = bf16[512,8,2,256]{3,1,2,0:T(8,128)(2,1)} copy(bf16[512,8,2,256]{3,2,1,0:T(2,128)(2,1)S(1)} %bitcast.52) | data formatting | bytes 8388608
  32.8 0.0 copy-done.3
  32.8 0.0 copy-done.4
  32.8 0.7 fusion.43
  34.2 0.7 compare_reduce_fusion
  35.7 60.4 %all-gather.2.cloned.1.call-done = bf16[1024,4224]{1,0:T(8,128)(2,1)} async-done(((bf16[64,4224]{1,0:T(8,128)(2,1)}), bf16[1024,4224]{1,0:T(8,128)(2,1)}) %all-gather.2.cloned.1.call-update) | async-done | bytes 8650768 | tf_op jit(solution)/shard_map/all_gather | solution.py:79
  96.1 1.8 convert_compare_fusion.1
  97.9 0.3 eq.73
  98.2 0.8 compare_and_fusion
  99.0 0.2 copy.42
  99.2 0.4 reshape.58
  99.6 0.3 eq.64
  99.9 0.3 compare_and_fusion.1
  100.2 0.2 copy.38
  100.4 0.4 reshape.52
  100.7 0.1 copy.44
  100.9 0.1 copy.45
  101.0 0.2 copy.43
  101.2 0.1 copy.40
  101.3 0.1 copy.41
  101.5 0.2 copy.39
  101.6 0.5 fusion.20
  102.1 0.2 copy.46
  102.3 0.5 fusion.18
  102.8 5.8 %convolution_convert_fusion = bf16[16,64,4224]{2,1,0:T(8,128)(2,1)S(1)} fusion(bf16[16,64,4224]{2,1,0:T(8,128)(2,1)} %bitcast.47, pred[16,32,64]{2,1,0:T(8,128)(4,1)S(1)} %bitcast.60, pred[16,32,64]{2,1,0:T(8,128)(4,1)S(1)} %bitcast.59), kind=kOutput, calls=%fused_computation | convolution fusion | flops 558039040 | bytes 17367040 | tf_op jit(solution)/shard_map/gpi,gic->gpc/dot_general | solution.py:111
  108.7 0.8 fusion.51
  109.5 7.1 %fusion.2 = f32[512,1024]{1,0:T(8,128)S(1)} fusion(bf16[4096,1024]{1,0:T(8,128)(2,1)} %bitcast.49, bf16[512,4224]{1,0:T(8,128)(2,1)S(1)} %bitcast.51), kind=kOutput, calls=%fused_computation.5 | convolution fusion | flops 4294967296 | bytes 14680064 | tf_op jit(solution)/shard_map/dot_general | solution.py:9
  116.6 0.3 fusion.23
  116.9 1.5 collective-permute-start.1
  118.5 2.4 %fusion.10 = f32[512,512]{0,1:T(8,128)S(1)} fusion(bf16[4096,512]{1,0:T(8,128)(2,1)S(1)} %bitcast.53, bf16[512,4224]{1,0:T(8,128)(2,1)S(1)} %bitcast.50), kind=kOutput, calls=%fused_computation.14 | convolution fusion | flops 2147483648 | bytes 9437184 | tf_op jit(solution)/shard_map/dot_general | solution.py:9
  120.8 0.2 fusion.28
  121.0 0.6 collective-permute-start.2
  121.6 1.1 slice_convert_fusion
  122.7 0.5 fusion.49
  123.2 0.5 select_reduce_fusion.1
  123.7 12.9 %collective-permute-done.2 = bf16[512,256]{0,1:T(8,128)(2,1)S(1)} collective-permute-done((bf16[512,256]{0,1:T(8,128)(2,1)S(1)}, bf16[512,256]{0,1:T(8,128)(2,1)S(1)}, u32[]{:S(2)}, u32[]{:S(2)}) %collective-permute-start.2) | collective-permute-done | bytes 262176 | tf_op jit(solution)/shard_map/ppermute | solution.py:49
  136.7 0.2 broadcast_select_fusion.3
  136.9 0.0 copy-done
  136.9 1.3 subtract_convert_fusion
  138.2 0.0 copy-start.5
  138.3 1.6 fusion.4
  139.8 0.0 collective-permute-done.1
  139.8 0.1 broadcast_select_fusion.1
  139.9 0.5 copy-done.5
  140.4 2.3 %fusion.12 = bf16[512,2048]{1,0:T(8,128)(2,1)S(1)} fusion(bf16[1,1024,2048]{2,1,0:T(8,128)(2,1)S(1)} %copy-done.5, bf16[512,512]{1,0:T(8,128)(2,1)S(1)} %get-tuple-element.20, bf16[512,512]{1,0:T(8,128)(2,1)S(1)} %get-tuple-element.19), kind=kOutput, calls=%fused_computation.16 | convolution fusion | flops 2150629376 | bytes 7340032 | tf_op jit(solution)/shard_map/dot_general | solution.py:123
  142.8 1.3 fusion.53
  144.1 3.7 %fusion.1 = bf16[1024,2048]{1,0:T(8,128)(2,1)} fusion(f32[16,64,2048]{2,1,0:T(8,128)S(1)} %fusion.4, f32[16,64,2048]{2,1,0:T(8,128)S(1)} %fusion.53, f32[1024]{0:T(1024)S(1)} %get-tuple-element.10, f32[1024]{0:T(1024)S(1)} %get-tuple-element.9), kind=kLoop, calls=%fused_computation.3 | loop fusion | flops 8388608 | bytes 20979712 | tf_op jit(solution)/shard_map/convert_element_type | solution.py:141
  147.8 0.0 reduce-scatter.2.cloned.1.call-update
  147.8 70.8 %reduce-scatter.2.cloned.1.call-done = bf16[64,2048]{1,0:T(8,128)(2,1)} async-done(((bf16[1024,2048]{1,0:T(8,128)(2,1)}), bf16[64,2048]{1,0:T(8,128)(2,1)}) %reduce-scatter.2.cloned.1.call-update) | async-done | bytes 262160 | tf_op jit(solution)/shard_map/reduce_scatter | solution.py:141
  (6 shorter events, 0.0 us)
Async XLA Ops:
  6.5 130.4 %copy-start = (bf16[1,512,2048]{2,1,0:T(8,128)(2,1)S(1)}, bf16[1,512,2048]{2,1,0:T(8,128)(2,1)}, u32[]{:S(2)}) copy-start(bf16[1,512,2048]{2,1,0:T(8,128)(2,1)} %param.17) | copy-start | bytes 6291460
  6.5 89.6 %all-gather.2.cloned.1.call-start = ((), (), s32[]{:S(2)}) async-start(), calls=%async_computation.1 | async-start | bytes 9191424 | tf_op jit(solution)/shard_map/all_gather | solution.py:79
  6.5 9.5 %collective-permute-start = (bf16[64,2048]{1,0:T(8,128)(2,1)}, bf16[64,2048]{1,0:T(8,128)(2,1)S(1)}, u32[]{:S(2)}, u32[]{:S(2)}) collective-permute-start(bf16[64,2048]{1,0:T(8,128)(2,1)} %param.9), channel_id=1, source_target_pairs={{0,1},{1,0},{2,3},{3,2},{4,5},{5,4},{6,7},{7,6},{8,9},{9,8},{10,11... | collective-permute-start | bytes 786440 | tf_op jit(solution)/shard_map/ppermute | solution.py:49
  17.9 200.7 %reduce-scatter.2.cloned.1.call-start = ((), (), s32[]{:S(2)}) async-start(), calls=%async_computation.2 | async-start | bytes 4456448 | tf_op jit(solution)/shard_map/reduce_scatter | solution.py:141
  20.4 9.5 %copy-start.1 = (bf16[1,4096,2,256]{3,2,1,0:T(2,128)(2,1)S(1)}, bf16[1,4096,2,256]{3,2,1,0:T(2,128)(2,1)}, u32[]{:S(2)}) copy-start(bf16[1,4096,2,256]{3,2,1,0:T(2,128)(2,1)} %param.16) | copy-start | bytes 12582916
  29.9 2.9 %copy-start.3 = (s32[8]{0:T(128)S(1)}, s32[8]{0:T(128)}, u32[]{:S(2)}) copy-start(s32[8]{0:T(128)} %param.13) | copy-start | bytes 100
  29.9 2.9 %copy-start.4 = (s32[8]{0:T(128)S(1)}, s32[8]{0:T(128)}, u32[]{:S(2)}) copy-start(s32[8]{0:T(128)} %param.12) | copy-start | bytes 100
  109.5 8.9 %copy-start.2 = (bf16[512,8,2,256]{3,1,2,0:T(8,128)(2,1)S(1)}, bf16[512,8,2,256]{3,1,2,0:T(8,128)(2,1)}, u32[]{:S(2)}) copy-start(bf16[512,8,2,256]{3,1,2,0:T(8,128)(2,1)} %copy.50) | copy-start | bytes 12582916
  116.9 22.9 %collective-permute-start.1 = (bf16[512,512]{1,0:T(8,128)(2,1)S(1)}, bf16[512,512]{1,0:T(8,128)(2,1)S(1)}, u32[]{:S(2)}, u32[]{:S(2)}) collective-permute-start(bf16[512,512]{1,0:T(8,128)(2,1)S(1)} %fusion.23), channel_id=1, source_target_pairs={{0,1},{1,0},{2,3},{3,2},{4,5},{5,4},{6,7},{7,6},{8,9},{9,8},{10,11... | collective-permute-start | bytes 1572872 | tf_op jit(solution)/shard_map/ppermute | solution.py:49
  121.0 15.7 %collective-permute-start.2 = (bf16[512,256]{0,1:T(8,128)(2,1)S(1)}, bf16[512,256]{0,1:T(8,128)(2,1)S(1)}, u32[]{:S(2)}, u32[]{:S(2)}) collective-permute-start(bf16[512,256]{0,1:T(8,128)(2,1)S(1)} %fusion.28), channel_id=1, source_target_pairs={{0,1},{1,0},{2,3},{3,2},{4,5},{5,4},{6,7},{7,6},{8,9},{9,8},{10,11... | collective-permute-start | bytes 786440 | tf_op jit(solution)/shard_map/ppermute | solution.py:49
  138.2 2.2 copy-start.5
Sparse Core Ops, SparseCore 0:
  18.0 78.0 all-gather.1
  147.9 70.6 reduce-scatter.1

commit v13 on v11

--- a/solution.py
+++ b/solution.py
@@ -113,9 +113,13 @@
     ).astype(jnp.bfloat16)
     home_rows = rows[:, :capacity].reshape(slot_rows, -1)
     spare_rows = rows[:, capacity:].reshape(slot_rows, -1)
-    home_hidden = gate_up(home_rows[:, :d_model], gate_up_weight[0])
-    home_hidden, spare_rows = lax.optimization_barrier((home_hidden, spare_rows))
-    home_hidden = gather_dp(home_hidden, 1)
+    half = slot_rows // 2
+    first_hidden = gate_up(home_rows[:half, :d_model], gate_up_weight[0])
+    first_hidden, home_rows = lax.optimization_barrier((first_hidden, home_rows))
+    first_hidden = gather_dp(first_hidden, 1)
+    second_hidden = gate_up(home_rows[half:, :d_model], gate_up_weight[0])
+    second_hidden, spare_rows = lax.optimization_barrier((second_hidden, spare_rows))
+    home_hidden = jnp.concatenate([first_hidden, gather_dp(second_hidden, 1)], axis=0)
     spare_hidden = gather_dp(gate_up(spare_rows[:, :d_model], spare_gate_up[0]), 1)
     home_out = jnp.dot(home_hidden, down_weight[0], preferred_element_type=jnp.float32)
     home_out = home_out.astype(jnp.bfloat16).reshape(ep_count, capacity, -1)

time: 226 us -> 232 us (1.027)
  matrix products: 23.2 us -> 26.6 us
    ppermute x3 -> x4, starting transfers between devices: 5.06 us -> 6.46 us  [gather_dp(): partner = lax.ppermute(block, 'dp', perm=[(0, 1), (1, 0)])]
    dot_general x2 -> x3, matrix products: 9.62 us -> 10.8 us  [gate_up(): jnp.einsum('rd,djf->rjf', row_block, weight, preferred_element_type=jnp.f...]
    ppermute x3 -> x4, waiting for transfers between devices: 14 us -> 14 us  [gather_dp(): partner = lax.ppermute(block, 'dp', perm=[(0, 1), (1, 0)])]
  transfers between devices with their start and end apart: 5 -> 6, of which waited for: 5 -> 4; matrix products, arithmetic and copies ran while one was open for 7% -> 9% of each run, Pallas kernels for 0% -> 0%
where the time goes in v13:
time: 232 us
  waiting for transfers between devices  156 us (67%)
  matrix products  26.6 us (11%)
  other arithmetic  20.2 us (9%)
  between operations  14.9 us (6%)
  local copies, waits for them, and re-layouts  7.59 us (3%)
  starting transfers between devices  6.51 us (3%)
    all_gather x1, waiting for transfers between devices, per_device(): every_row = lax.all_gather(packed, 'ep', axis=0, tiled=True)  71.7 us
    reduce_scatter x1, waiting for transfers between devices, per_device(): lax.psum_scatter(partial.astype(jnp.bfloat16), 'ep', scatter_dimension=0,...  70.1 us
    ppermute x4, waiting for transfers between devices, gather_dp(): partner = lax.ppermute(block, 'dp', perm=[(0, 1), (1, 0)])  14 us
    dot_general x3, matrix products, gate_up(): jnp.einsum('rd,djf->rjf', row_block, weight, preferred_element_type=jnp.f...  10.8 us
    ppermute x4, starting transfers between devices, gather_dp(): partner = lax.ppermute(block, 'dp', perm=[(0, 1), (1, 0)])  6.46 us
    dot_general x1, matrix products, per_device(): jnp.einsum('gpi,gic->gpc', jnp.concatenate([home_pick, spare_pick], axis=...  5.84 us
  transfers between devices with their start and end apart: 6, of which 4 were waited for; matrix products, arithmetic and copies ran while one was open for 9% of the time, Pallas kernels for 0%

profile of v13, /device:TPU:0, one launch (start us, length us, event | category | flops | bytes accessed | tf_op | source)
XLA Modules:
  0.0 231.7 jit_solution(4145326013455720293)
XLA Ops:
  6.5 3.0 %collective-permute-start = (bf16[64,2048]{1,0:T(8,128)(2,1)}, bf16[64,2048]{1,0:T(8,128)(2,1)S(1)}, u32[]{:S(2)}, u32[]{:S(2)}) collective-permute-start(bf16[64,2048]{1,0:T(8,128)(2,1)} %param.9), channel_id=1, source_target_pairs={{0,1},{1,0},{2,3},{3,2},{4,5},{5,4},{6,7},{7,6},{8,9},{9,8},{10,11... | collective-permute-start | bytes 786440 | tf_op jit(solution)/shard_map/ppermute | solution.py:46
  9.5 0.7 convert_element_type.73
  10.2 0.8 fusion.66
  11.0 0.1 copy.60
  11.1 4.9 %collective-permute-done = bf16[64,2048]{1,0:T(8,128)(2,1)S(1)} collective-permute-done((bf16[64,2048]{1,0:T(8,128)(2,1)}, bf16[64,2048]{1,0:T(8,128)(2,1)S(1)}, u32[]{:S(2)}, u32[]{:S(2)}) %collective-permute-start) | collective-permute-done | bytes 262176 | tf_op jit(solution)/shard_map/ppermute | solution.py:46
  16.0 1.0 broadcast_select_fusion.7
  17.0 0.9 fusion.36
  17.9 0.0 all-gather.2.cloned.1.call-update
  17.9 0.0 reduce-scatter.2.cloned.1.call-start
  18.0 1.2 dynamic_slice.6
  19.2 1.3 dynamic_slice.7
  20.6 1.3 fusion.57
  22.5 1.3 compare_reduce_fusion
  24.5 71.7 %all-gather.2.cloned.1.call-done = bf16[1024,4224]{1,0:T(8,128)(2,1)} async-done(((bf16[64,4224]{1,0:T(8,128)(2,1)}), bf16[1024,4224]{1,0:T(8,128)(2,1)}) %all-gather.2.cloned.1.call-update) | async-done | bytes 8650768 | tf_op jit(solution)/shard_map/all_gather | solution.py:76
  96.2 1.8 convert_compare_fusion.1
  97.9 0.3 eq.65
  98.3 0.3 eq.74
  98.6 0.3 compare_and_fusion.1
  98.9 0.2 copy.47
  99.1 0.2 copy.48
  99.2 0.9 compare_and_fusion
  100.2 0.2 copy.51
  100.4 0.2 copy.52
  100.5 0.1 copy.49
  100.7 0.1 copy.50
  100.8 0.1 copy.53
  100.9 0.1 copy.54
  101.1 1.1 slice_convert_fusion
  102.2 1.8 fusion.63
  104.0 0.5 fusion.24
  104.5 0.5 fusion.26
  105.0 5.8 %convolution_convert_fusion = bf16[16,64,4224]{2,1,0:T(8,128)(2,1)S(1)} fusion(bf16[16,64,4224]{2,1,0:T(8,128)(2,1)} %bitcast.84, pred[16,32,64]{2,1,0:T(8,128)(4,1)S(1)} %bitcast.94, pred[16,32,64]{2,1,0:T(8,128)(4,1)S(1)} %bitcast.93), kind=kOutput, calls=%fused_computation | convolution fusion | flops 558039040 | bytes 17367040 | tf_op jit(solution)/shard_map/gpi,gic->gpc/dot_general | solution.py:108
  110.8 0.0 slice-start
  110.8 0.8 fusion.65
  111.7 0.0 slice-start.1
  111.7 6.1 %fusion.4 = f32[256,2,512]{2,0,1:T(8,128)S(1)} fusion(bf16[4096,2,512]{2,1,0:T(2,128)(2,1)} %bitcast.97, bf16[512,4224]{1,0:T(8,128)(2,1)S(1)} %bitcast.86), kind=kOutput, calls=%fused_computation.7 | convolution fusion | flops 2147483648 | bytes 11534336 | tf_op jit(solution)/shard_map/rd,djf->rjf/dot_general | solution.py:8
  117.8 0.2 fusion.42
  118.0 0.0 copy-start.1
  118.0 2.3 %fusion.2 = f32[256,2,512]{2,0,1:T(8,128)S(1)} fusion(bf16[4096,2,512]{2,1,0:T(2,128)(2,1)S(1)} %bitcast.100, bf16[512,4224]{1,0:T(8,128)(2,1)S(1)} %bitcast.87), kind=kOutput, calls=%fused_computation.5 | convolution fusion | flops 2147483648 | bytes 11534336 | tf_op jit(solution)/shard_map/rd,djf->rjf/dot_general | solution.py:8
  120.3 0.8 fusion.40
  121.2 1.5 collective-permute-start.2
  122.7 0.0 copy-done.1
  122.7 2.4 %fusion.10 = f32[512,2,256]{0,2,1:T(8,128)S(1)} fusion(bf16[4096,2,256]{2,1,0:T(2,128)(2,1)S(1)} %bitcast.101, bf16[512,4224]{1,0:T(8,128)(2,1)S(1)} %bitcast.85), kind=kOutput, calls=%fused_computation.13 | convolution fusion | flops 2147483648 | bytes 9437184 | tf_op jit(solution)/shard_map/rd,djf->rjf/dot_general | solution.py:8
  125.0 0.9 fusion.38
  125.9 1.0 reshape.58
  126.9 1.0 reshape.52
  127.9 0.6 collective-permute-start.3
  128.5 1.5 collective-permute-start.1
  129.9 1.6 select_reduce_fusion.1
  131.6 0.2 copy.57
  131.8 0.0 collective-permute-done.2
  131.8 1.1 broadcast_select_fusion.3
  132.9 9.1 %collective-permute-done.1 = bf16[256,512]{1,0:T(8,128)(2,1)S(1)} collective-permute-done((bf16[256,512]{1,0:T(8,128)(2,1)S(1)}, bf16[256,512]{1,0:T(8,128)(2,1)S(1)}, u32[]{:S(2)}, u32[]{:S(2)}) %collective-permute-start.1) | collective-permute-done | bytes 262176 | tf_op jit(solution)/shard_map/ppermute | solution.py:46
  141.9 0.1 broadcast_select_fusion.5
  142.0 4.6 %fusion.16 = bf16[512,2048]{1,0:T(8,128)(2,1)S(1)} fusion(bf16[1,1024,2048]{2,1,0:T(8,128)(2,1)} %param.15, bf16[256,512]{1,0:T(8,128)(2,1)S(1)} %get-tuple-element.26, bf16[256,512]{1,0:T(8,128)(2,1)S(1)} %get-tuple-element.25, bf16[256,512]{1,0:T(8,128)(2,1)S(1)} %get-tuple-element.24, bf16[256,512]{1,0:T(8,128)(2,1)S(1)} %get-tuple-element.23), kind=kOutput, calls=%fused_computation.20 | convolution fusion | flops 2152726528 | bytes 7340032 | tf_op jit(solution)/shard_map/dot_general | solution.py:124
  146.6 1.3 fusion.67
  147.9 0.0 collective-permute-done.3
  147.9 0.2 broadcast_select_fusion.1
  148.2 0.0 copy-done
  148.2 1.3 subtract_convert_fusion
  149.5 1.6 fusion.6
  151.0 3.7 %fusion.1 = bf16[1024,2048]{1,0:T(8,128)(2,1)} fusion(f32[16,64,2048]{2,1,0:T(8,128)S(1)} %fusion.6, f32[16,64,2048]{2,1,0:T(8,128)S(1)} %fusion.67, f32[1024]{0:T(1024)S(1)} %get-tuple-element.14, f32[1024]{0:T(1024)S(1)} %get-tuple-element.13), kind=kLoop, calls=%fused_computation.3 | loop fusion | flops 8388608 | bytes 20979712 | tf_op jit(solution)/shard_map/convert_element_type | solution.py:142
  154.7 0.0 reduce-scatter.2.cloned.1.call-update
  154.8 70.1 %reduce-scatter.2.cloned.1.call-done = bf16[64,2048]{1,0:T(8,128)(2,1)} async-done(((bf16[1024,2048]{1,0:T(8,128)(2,1)}), bf16[64,2048]{1,0:T(8,128)(2,1)}) %reduce-scatter.2.cloned.1.call-update) | async-done | bytes 262160 | tf_op jit(solution)/shard_map/reduce_scatter | solution.py:142
  (6 shorter events, 0.0 us)
Async XLA Ops:
  6.5 141.6 %copy-start = (bf16[1,512,2048]{2,1,0:T(8,128)(2,1)S(1)}, bf16[1,512,2048]{2,1,0:T(8,128)(2,1)}, u32[]{:S(2)}) copy-start(bf16[1,512,2048]{2,1,0:T(8,128)(2,1)} %param.17) | copy-start | bytes 6291460
  6.5 89.6 %all-gather.2.cloned.1.call-start = ((), (), s32[]{:S(2)}) async-start(), calls=%async_computation.1 | async-start | bytes 9191424 | tf_op jit(solution)/shard_map/all_gather | solution.py:76
  6.5 9.5 %collective-permute-start = (bf16[64,2048]{1,0:T(8,128)(2,1)}, bf16[64,2048]{1,0:T(8,128)(2,1)S(1)}, u32[]{:S(2)}, u32[]{:S(2)}) collective-permute-start(bf16[64,2048]{1,0:T(8,128)(2,1)} %param.9), channel_id=1, source_target_pairs={{0,1},{1,0},{2,3},{3,2},{4,5},{5,4},{6,7},{7,6},{8,9},{9,8},{10,11... | collective-permute-start | bytes 786440 | tf_op jit(solution)/shard_map/ppermute | solution.py:46
  17.9 207.0 %reduce-scatter.2.cloned.1.call-start = ((), (), s32[]{:S(2)}) async-start(), calls=%async_computation.2 | async-start | bytes 4456448 | tf_op jit(solution)/shard_map/reduce_scatter | solution.py:142
  110.8 7.1 %slice-start = ((s8[8388608]{0:T(1024)(128)(4,1)}), s8[4194304]{0:T(1024)(128)(4,1)S(1)}, s32[]{:S(2)}) async-start(s8[8388608]{0:T(1024)(128)(4,1)} %bitcast.98), calls=%async_computation.3 | async-start | bytes 8388608
  111.7 6.3 %slice-start.1 = ((s8[8388608]{0:T(1024)(128)(4,1)}), s8[4194304]{0:T(1024)(128)(4,1)S(1)}, s32[]{:S(2)}) async-start(s8[8388608]{0:T(1024)(128)(4,1)} %bitcast.98), calls=%async_computation.4 | async-start | bytes 8388608
  118.0 4.7 %copy-start.1 = (bf16[1,4096,2,256]{3,2,1,0:T(2,128)(2,1)S(1)}, bf16[1,4096,2,256]{3,2,1,0:T(2,128)(2,1)}, u32[]{:S(2)}) copy-start(bf16[1,4096,2,256]{3,2,1,0:T(2,128)(2,1)} %param.16) | copy-start | bytes 12582916
  121.2 10.6 %collective-permute-start.2 = (bf16[256,512]{1,0:T(8,128)(2,1)}, bf16[256,512]{1,0:T(8,128)(2,1)}, u32[]{:S(2)}, u32[]{:S(2)}) collective-permute-start(bf16[256,512]{1,0:T(8,128)(2,1)} %fusion.40), channel_id=1, source_target_pairs={{0,1},{1,0},{2,3},{3,2},{4,5},{5,4},{6,7},{7,6},{8,9},{9,8},{10,11... | collective-permute-start | bytes 786440 | tf_op jit(solution)/shard_map/ppermute | solution.py:46
  127.9 20.0 %collective-permute-start.3 = (bf16[512,256]{0,1:T(8,128)(2,1)}, bf16[512,256]{0,1:T(8,128)(2,1)S(1)}, u32[]{:S(2)}, u32[]{:S(2)}) collective-permute-start(bf16[512,256]{0,1:T(8,128)(2,1)} %fusion.38), channel_id=1, source_target_pairs={{0,1},{1,0},{2,3},{3,2},{4,5},{5,4},{6,7},{7,6},{8,9},{9,8},{10,11... | collective-permute-start | bytes 786440 | tf_op jit(solution)/shard_map/ppermute | solution.py:46
  128.5 13.5 %collective-permute-start.1 = (bf16[256,512]{1,0:T(8,128)(2,1)S(1)}, bf16[256,512]{1,0:T(8,128)(2,1)S(1)}, u32[]{:S(2)}, u32[]{:S(2)}) collective-permute-start(bf16[256,512]{1,0:T(8,128)(2,1)S(1)} %fusion.42), channel_id=1, source_target_pairs={{0,1},{1,0},{2,3},{3,2},{4,5},{5,4},{6,7},{7,6},{8,9},{9,8},{10,11... | collective-permute-start | bytes 786440 | tf_op jit(solution)/shard_map/ppermute | solution.py:46
Sparse Core Ops, SparseCore 0:
  18.1 78.0 all-gather.1
  154.9 69.9 reduce-scatter.1

commit v14 on v11

--- a/solution.py
+++ b/solution.py
@@ -48,6 +48,20 @@
     low = jnp.where(first, block, partner)
     high = jnp.where(first, partner, block)
     return jnp.concatenate([low, high], axis=axis)
+
+
+def down_dp(hidden, weight):
+    if lax.axis_size("dp") != 2:
+        gathered = lax.all_gather(hidden, "dp", axis=1, tiled=True)
+        return jnp.dot(gathered, weight, preferred_element_type=jnp.float32)
+    partner = lax.ppermute(hidden, "dp", perm=[(0, 1), (1, 0)])
+    blocks = weight.reshape(2, hidden.shape[1], weight.shape[1])
+    first = lax.axis_index("dp") == 0
+    own = jnp.where(first, blocks[0], blocks[1])
+    other = jnp.where(first, blocks[1], blocks[0])
+    return jnp.dot(hidden, own, preferred_element_type=jnp.float32) + jnp.dot(
+        partner, other, preferred_element_type=jnp.float32
+    )
 
 
 def per_device(
@@ -115,11 +129,9 @@
     spare_rows = rows[:, capacity:].reshape(slot_rows, -1)
     home_hidden = gate_up(home_rows[:, :d_model], gate_up_weight[0])
     home_hidden, spare_rows = lax.optimization_barrier((home_hidden, spare_rows))
-    home_hidden = gather_dp(home_hidden, 1)
-    spare_hidden = gather_dp(gate_up(spare_rows[:, :d_model], spare_gate_up[0]), 1)
-    home_out = jnp.dot(home_hidden, down_weight[0], preferred_element_type=jnp.float32)
+    home_out = down_dp(home_hidden, down_weight[0])
     home_out = home_out.astype(jnp.bfloat16).reshape(ep_count, capacity, -1)
-    spare_out = jnp.dot(spare_hidden, spare_down[0], preferred_element_type=jnp.float32)
+    spare_out = down_dp(gate_up(spare_rows[:, :d_model], spare_gate_up[0]), spare_down[0])
     spare_high = spare_out.astype(jnp.bfloat16)
     spare_low = (spare_out - spare_high.astype(jnp.float32)).astype(jnp.bfloat16)
     spare_high = spare_high.reshape(ep_count, capacity, -1)

time: 226 us -> 225 us (level)
  matrix products: 23.2 us -> 30.8 us
  waiting for transfers between devices: 157 us -> 150 us
  other arithmetic: 19.4 us -> 16.6 us
    ppermute x3 -> x1, waiting for transfers between devices: 14 us -> 4.95 us  [gather_dp(): partner = lax.ppermute(block, 'dp', perm=[(0, 1), (1, 0)])]
    dot_general x2 -> x4, matrix products: 3.64 us -> 11.4 us  [the longest x2 6.95 us: down_dp(): jnp.dot(hidden, own, preferred_element_type=jnp.float32)]
    ppermute x0 -> x2, waiting for transfers between devices: none -> 3.24 us  [down_dp(): partner = lax.ppermute(hidden, 'dp', perm=[(0, 1), (1, 0)])]
    ppermute x3 -> x1, starting transfers between devices: 5.06 us -> 2.97 us  [gather_dp(): partner = lax.ppermute(block, 'dp', perm=[(0, 1), (1, 0)])]
  transfers between devices with their start and end apart: 5 -> 5, of which waited for: 5 -> 4; matrix products, arithmetic and copies ran while one was open for 7% -> 10% of each run, Pallas kernels for 0% -> 0%
where the time goes in v14:
time: 225 us; the launch traced here: 224 us
  waiting for transfers between devices  150 us (67%)
  matrix products  30.8 us (14%)
  other arithmetic  16.6 us (7%)
  between operations  15.1 us (7%)
  local copies, waits for them, and re-layouts  6.24 us (3%)
  starting transfers between devices  5.04 us (2%)
    all_gather x1, waiting for transfers between devices, per_device(): every_row = lax.all_gather(packed, 'ep', axis=0, tiled=True)  71.5 us
    reduce_scatter x1, waiting for transfers between devices, per_device(): lax.psum_scatter(partial.astype(jnp.bfloat16), 'ep', scatter_dimension=0,...  70.7 us
    dot_general x2, matrix products, gate_up(): jnp.einsum('rd,djf->rjf', row_block, weight, preferred_element_type=jnp.f...  9.58 us
    dot_general x2, matrix products, down_dp(): jnp.dot(hidden, own, preferred_element_type=jnp.float32)  6.95 us
    dot_general x1, matrix products, per_device(): jnp.einsum('gpi,gic->gpc', jnp.concatenate([home_pick, spare_pick], axis=...  5.83 us
    ppermute x1, waiting for transfers between devices, gather_dp(): partner = lax.ppermute(block, 'dp', perm=[(0, 1), (1, 0)])  4.95 us
  transfers between devices with their start and end apart: 5, of which 4 were waited for; matrix products, arithmetic and copies ran while one was open for 10% of the time, Pallas kernels for 0%

profile of v14, /device:TPU:0, one launch (start us, length us, event | category | flops | bytes accessed | tf_op | source)
XLA Modules:
  0.0 224.1 jit_solution(15065613179835285331)
XLA Ops:
  6.5 0.0 all-gather.2.cloned.1.call-start
  6.5 3.0 %collective-permute-start = (bf16[64,2048]{1,0:T(8,128)(2,1)}, bf16[64,2048]{1,0:T(8,128)(2,1)S(1)}, u32[]{:S(2)}, u32[]{:S(2)}) collective-permute-start(bf16[64,2048]{1,0:T(8,128)(2,1)} %param.9), channel_id=1, source_target_pairs={{0,1},{1,0},{2,3},{3,2},{4,5},{5,4},{6,7},{7,6},{8,9},{9,8},{10,11... | collective-permute-start | bytes 786440 | tf_op jit(solution)/shard_map/ppermute | solution.py:46
  9.5 0.7 convert_element_type.75
  10.2 0.8 fusion.67
  11.0 0.1 copy.56
  11.1 4.9 %collective-permute-done = bf16[64,2048]{1,0:T(8,128)(2,1)S(1)} collective-permute-done((bf16[64,2048]{1,0:T(8,128)(2,1)}, bf16[64,2048]{1,0:T(8,128)(2,1)S(1)}, u32[]{:S(2)}, u32[]{:S(2)}) %collective-permute-start) | collective-permute-done | bytes 262176 | tf_op jit(solution)/shard_map/ppermute | solution.py:46
  16.0 1.0 broadcast_select_fusion.1
  17.0 0.9 fusion.42
  17.9 0.0 all-gather.2.cloned.1.call-update
  17.9 0.0 reduce-scatter.2.cloned.1.call-start
  18.0 1.2 dynamic_slice.6
  19.2 1.3 dynamic_slice.7
  20.5 1.4 fusion.59
  22.6 1.4 compare_reduce_fusion
  24.6 71.5 %all-gather.2.cloned.1.call-done = bf16[1024,4224]{1,0:T(8,128)(2,1)} async-done(((bf16[64,4224]{1,0:T(8,128)(2,1)}), bf16[1024,4224]{1,0:T(8,128)(2,1)}) %all-gather.2.cloned.1.call-update) | async-done | bytes 8650768 | tf_op jit(solution)/shard_map/all_gather | solution.py:90
  96.1 1.8 convert_compare_fusion.1
  97.9 0.3 eq.64
  98.3 0.3 eq.73
  98.6 0.3 compare_and_fusion.1
  98.9 0.2 copy.44
  99.1 0.2 copy.45
  99.2 0.9 compare_and_fusion
  100.1 0.2 copy.48
  100.3 0.2 copy.49
  100.4 0.1 copy.46
  100.6 0.1 copy.47
  100.7 0.1 copy.50
  100.8 0.1 copy.51
  101.0 0.5 fusion.18
  101.5 0.5 fusion.20
  102.0 5.8 %convolution_convert_fusion = bf16[16,64,4224]{2,1,0:T(8,128)(2,1)S(1)} fusion(bf16[16,64,4224]{2,1,0:T(8,128)(2,1)} %bitcast.84, pred[16,32,64]{2,1,0:T(8,128)(4,1)S(1)} %bitcast.93, pred[16,32,64]{2,1,0:T(8,128)(4,1)S(1)} %bitcast.92), kind=kOutput, calls=%fused_computation | convolution fusion | flops 558039040 | bytes 17367040 | tf_op jit(solution)/shard_map/gpi,gic->gpc/dot_general | solution.py:122
  107.8 0.8 fusion.66
  108.6 0.0 copy-start.4
  108.7 7.3 %fusion.2 = f32[512,2,512]{2,0,1:T(8,128)S(1)} fusion(bf16[4096,2,512]{2,1,0:T(2,128)(2,1)} %bitcast.96, bf16[512,4224]{1,0:T(8,128)(2,1)S(1)} %bitcast.89), kind=kOutput, calls=%fused_computation.5 | convolution fusion | flops 4294967296 | bytes 14680064 | tf_op jit(solution)/shard_map/rd,djf->rjf/dot_general | solution.py:8
  115.9 1.1 fusion.30
  117.0 0.0 copy-done.4
  117.0 0.0 copy-start.1
  117.0 2.3 %fusion.8 = f32[512,2,256]{2,0,1:T(8,128)S(1)} fusion(bf16[4096,2,256]{2,1,0:T(2,128)(2,1)S(1)} %bitcast.97, bf16[512,4224]{1,0:T(8,128)(2,1)S(1)} %bitcast.88), kind=kOutput, calls=%fused_computation.12 | convolution fusion | flops 2147483648 | bytes 9437184 | tf_op jit(solution)/shard_map/rd,djf->rjf/dot_general | solution.py:8
  119.4 0.9 fusion.47
  120.2 1.5 collective-permute-start.2
  121.7 0.5 collective-permute-start.1
  122.3 0.0 copy-done.1
  122.3 2.7 %fusion.32 = f32[512,2048]{1,0:T(8,128)} fusion(pred[]{:T(512)S(6)} %eq.61, bf16[1,512,2048]{2,1,0:T(8,128)(2,1)S(1)} %copy-done.1, f32[512,2,256]{2,0,1:T(8,128)S(1)} %fusion.8), kind=kOutput, calls=%fused_computation.46 | convolution fusion | flops 538181632 | bytes 7340033 | tf_op jit(solution)/shard_map/dot_general | solution.py:62
  124.9 0.0 copy-done.2
  124.9 4.3 %fusion.13 = f32[512,2048]{1,0:T(8,128)} fusion(bf16[512,512]{1,0:T(8,128)(2,1)} %fusion.30, pred[]{:T(512)S(6)} %eq.61, bf16[1,1024,2048]{2,1,0:T(8,128)(2,1)S(1)} %copy-done.2), kind=kOutput, calls=%fused_computation.20 | convolution fusion | flops 1074790400 | bytes 8912897 | tf_op jit(solution)/shard_map/dot_general | solution.py:62
  129.2 1.1 slice_convert_fusion
  130.3 0.5 fusion.64
  130.8 0.4 reshape.74
  131.2 0.4 reshape.68
  131.5 0.2 copy.53
  131.7 0.5 select_reduce_fusion.1
  132.3 0.0 collective-permute-done.2
  132.3 3.0 %subtract_convert_fusion = (bf16[512,2048]{1,0:T(8,128)(2,1)S(1)}, bf16[512,2048]{1,0:T(8,128)(2,1)S(1)}) fusion(f32[512,2048]{1,0:T(8,128)} %fusion.32, bf16[512,256]{1,0:T(8,128)(2,1)} %collective-permute-done.2, pred[]{:T(512)S(6)} %eq.61, bf16[1,512,2048]{2,1,0:T(8,128)(2,1)S(1)} %copy-done.1), kind=kOutput, calls=%fused_computation.15 | convolution fusion | flops 542638080 | bytes 10747905 | tf_op jit(solution)/shard_map/dot_general | solution.py:62
  135.3 0.0 copy-start
  135.3 0.0 copy-start.3
  135.3 1.6 fusion.4
  136.9 3.2 %collective-permute-done.1 = bf16[512,512]{1,0:T(8,128)(2,1)S(1)} collective-permute-done((bf16[512,512]{1,0:T(8,128)(2,1)}, bf16[512,512]{1,0:T(8,128)(2,1)S(1)}, u32[]{:S(2)}, u32[]{:S(2)}) %collective-permute-start.1) | collective-permute-done | bytes 524320 | tf_op jit(solution)/shard_map/ppermute | solution.py:57
  140.1 0.0 copy-done
  140.1 0.0 copy-done.3
  140.1 1.4 add_convert_fusion
  141.6 1.3 fusion.68
  142.9 3.7 %fusion.1 = bf16[1024,2048]{1,0:T(8,128)(2,1)} fusion(f32[16,64,2048]{2,1,0:T(8,128)S(1)} %fusion.4, f32[16,64,2048]{2,1,0:T(8,128)S(1)} %fusion.68, f32[1024]{0:T(1024)S(1)} %get-tuple-element.10, f32[1024]{0:T(1024)S(1)} %get-tuple-element.9), kind=kLoop, calls=%fused_computation.3 | loop fusion | flops 8388608 | bytes 20979712 | tf_op jit(solution)/shard_map/convert_element_type | solution.py:150
  146.5 0.0 reduce-scatter.2.cloned.1.call-update
  146.5 70.7 %reduce-scatter.2.cloned.1.call-done = bf16[64,2048]{1,0:T(8,128)(2,1)} async-done(((bf16[1024,2048]{1,0:T(8,128)(2,1)}), bf16[64,2048]{1,0:T(8,128)(2,1)}) %reduce-scatter.2.cloned.1.call-update) | async-done | bytes 262160 | tf_op jit(solution)/shard_map/reduce_scatter | solution.py:150
  (2 shorter events, 0.0 us)
Async XLA Ops:
  6.5 89.6 %all-gather.2.cloned.1.call-start = ((), (), s32[]{:S(2)}) async-start(), calls=%async_computation.1 | async-start | bytes 9191424 | tf_op jit(solution)/shard_map/all_gather | solution.py:90
  6.5 9.5 %collective-permute-start = (bf16[64,2048]{1,0:T(8,128)(2,1)}, bf16[64,2048]{1,0:T(8,128)(2,1)S(1)}, u32[]{:S(2)}, u32[]{:S(2)}) collective-permute-start(bf16[64,2048]{1,0:T(8,128)(2,1)} %param.9), channel_id=1, source_target_pairs={{0,1},{1,0},{2,3},{3,2},{4,5},{5,4},{6,7},{7,6},{8,9},{9,8},{10,11... | collective-permute-start | bytes 786440 | tf_op jit(solution)/shard_map/ppermute | solution.py:46
  17.9 199.3 %reduce-scatter.2.cloned.1.call-start = ((), (), s32[]{:S(2)}) async-start(), calls=%async_computation.2 | async-start | bytes 4456448 | tf_op jit(solution)/shard_map/reduce_scatter | solution.py:150
  108.6 8.4 %copy-start.4 = (bf16[1,4096,2,256]{3,2,1,0:T(2,128)(2,1)S(1)}, bf16[1,4096,2,256]{3,2,1,0:T(2,128)(2,1)}, u32[]{:S(2)}) copy-start(bf16[1,4096,2,256]{3,2,1,0:T(2,128)(2,1)} %param.16) | copy-start | bytes 12582916
  117.0 5.2 %copy-start.1 = (bf16[1,512,2048]{2,1,0:T(8,128)(2,1)S(1)}, bf16[1,512,2048]{2,1,0:T(8,128)(2,1)}, u32[]{:S(2)}) copy-start(bf16[1,512,2048]{2,1,0:T(8,128)(2,1)} %param.17) | copy-start | bytes 6291460
  120.2 4.7 %copy-start.2 = (bf16[1,1024,2048]{2,1,0:T(8,128)(2,1)S(1)}, bf16[1,1024,2048]{2,1,0:T(8,128)(2,1)}, u32[]{:S(2)}) copy-start(bf16[1,1024,2048]{2,1,0:T(8,128)(2,1)} %param.15) | copy-start | bytes 12582916
  120.2 12.0 %collective-permute-start.2 = (bf16[512,256]{1,0:T(8,128)(2,1)}, bf16[512,256]{1,0:T(8,128)(2,1)}, u32[]{:S(2)}, u32[]{:S(2)}) collective-permute-start(bf16[512,256]{1,0:T(8,128)(2,1)} %fusion.47), channel_id=1, source_target_pairs={{0,1},{1,0},{2,3},{3,2},{4,5},{5,4},{6,7},{7,6},{8,9},{9,8},{10,11... | collective-permute-start | bytes 786440 | tf_op jit(solution)/shard_map/ppermute | solution.py:57
  121.7 18.4 %collective-permute-start.1 = (bf16[512,512]{1,0:T(8,128)(2,1)}, bf16[512,512]{1,0:T(8,128)(2,1)S(1)}, u32[]{:S(2)}, u32[]{:S(2)}) collective-permute-start(bf16[512,512]{1,0:T(8,128)(2,1)} %fusion.30), channel_id=1, source_target_pairs={{0,1},{1,0},{2,3},{3,2},{4,5},{5,4},{6,7},{7,6},{8,9},{9,8},{10,11... | collective-permute-start | bytes 1572872 | tf_op jit(solution)/shard_map/ppermute | solution.py:57
  135.3 4.8 %copy-start = (f32[512,2048]{1,0:T(8,128)S(1)}, f32[512,2048]{1,0:T(8,128)}, u32[]{:S(2)}) copy-start(f32[512,2048]{1,0:T(8,128)} %fusion.13) | copy-start | bytes 12582916
  135.3 4.8 %copy-start.3 = (bf16[1,1024,2048]{2,1,0:T(8,128)(2,1)S(1)}, bf16[1,1024,2048]{2,1,0:T(8,128)(2,1)}, u32[]{:S(2)}) copy-start(bf16[1,1024,2048]{2,1,0:T(8,128)(2,1)} %param.15) | copy-start | bytes 12582916
Sparse Core Ops, SparseCore 0:
  18.0 78.0 all-gather.1
  146.7 70.5 reduce-scatter.1

commit v15 on v14

--- a/solution.py
+++ b/solution.py
@@ -140,11 +140,9 @@
     home_term = jnp.einsum(
         "gip,gpc->gic", home_take, home_out, preferred_element_type=jnp.float32
     ).reshape(all_tokens, -1)
-    spare_term = jnp.einsum(
-        "gip,gpc->gic",
-        jnp.concatenate([spare_take, spare_take], axis=2),
-        jnp.concatenate([spare_high, spare_low], axis=1),
-        preferred_element_type=jnp.float32,
+    spare_term = (
+        jnp.einsum("gip,gpc->gic", spare_take, spare_high, preferred_element_type=jnp.float32)
+        + jnp.einsum("gip,gpc->gic", spare_take, spare_low, preferred_element_type=jnp.float32)
     ).reshape(all_tokens, -1)
     partial = home_scale[:, None] * home_term + spare_scale[:, None] * spare_term
     mixed = lax.psum_scatter(partial.astype(jnp.bfloat16), "ep", scatter_dimension=0, tiled=True)

time: 225 us -> 225 us (level)
  no operation moved by 1% of the time
where the time goes in v15:
time: 225 us; the launch traced here: 224 us
  waiting for transfers between devices  150 us (67%)
  matrix products  32.1 us (14%)
  other arithmetic  16.6 us (7%)
  between operations  15.1 us (7%)
  local copies, waits for them, and re-layouts  5.84 us (3%)
  starting transfers between devices  5.04 us (2%)
    all_gather x1, waiting for transfers between devices, per_device(): every_row = lax.all_gather(packed, 'ep', axis=0, tiled=True)  71.5 us
    reduce_scatter x1, waiting for transfers between devices, per_device(): lax.psum_scatter(partial.astype(jnp.bfloat16), 'ep', scatter_dimension=0,...  71 us
    dot_general x2, matrix products, gate_up(): jnp.einsum('rd,djf->rjf', row_block, weight, preferred_element_type=jnp.f...  9.76 us
    dot_general x2, matrix products, down_dp(): jnp.dot(hidden, own, preferred_element_type=jnp.float32)  6.95 us
    dot_general x1, matrix products, per_device(): jnp.einsum('gpi,gic->gpc', jnp.concatenate([home_pick, spare_pick], axis=...  5.83 us
    ppermute x1, waiting for transfers between devices, gather_dp(): partner = lax.ppermute(block, 'dp', perm=[(0, 1), (1, 0)])  4.95 us
  transfers between devices with their start and end apart: 5, of which 4 were waited for; matrix products, arithmetic and copies ran while one was open for 10% of the time, Pallas kernels for 0%

profile of v15, /device:TPU:0, one launch (start us, length us, event | category | flops | bytes accessed | tf_op | source)
XLA Modules:
  0.0 224.4 jit_solution(18311208258573623660)
XLA Ops:
  6.5 0.0 all-gather.2.cloned.1.call-start
  6.5 3.0 %collective-permute-start = (bf16[64,2048]{1,0:T(8,128)(2,1)}, bf16[64,2048]{1,0:T(8,128)(2,1)S(1)}, u32[]{:S(2)}, u32[]{:S(2)}) collective-permute-start(bf16[64,2048]{1,0:T(8,128)(2,1)} %param.9), channel_id=1, source_target_pairs={{0,1},{1,0},{2,3},{3,2},{4,5},{5,4},{6,7},{7,6},{8,9},{9,8},{10,11... | collective-permute-start | bytes 786440 | tf_op jit(solution)/shard_map/ppermute | solution.py:46
  9.5 0.7 convert_element_type.75
  10.2 0.8 fusion.58
  11.0 0.1 copy.50
  11.1 4.9 %collective-permute-done = bf16[64,2048]{1,0:T(8,128)(2,1)S(1)} collective-permute-done((bf16[64,2048]{1,0:T(8,128)(2,1)}, bf16[64,2048]{1,0:T(8,128)(2,1)S(1)}, u32[]{:S(2)}, u32[]{:S(2)}) %collective-permute-start) | collective-permute-done | bytes 262176 | tf_op jit(solution)/shard_map/ppermute | solution.py:46
  16.0 1.0 broadcast_select_fusion.1
  17.0 0.9 fusion.38
  17.9 0.0 all-gather.2.cloned.1.call-update
  17.9 0.0 reduce-scatter.2.cloned.1.call-start
  18.0 1.2 dynamic_slice.6
  19.2 1.3 dynamic_slice.7
  20.5 1.4 fusion.52
  22.6 1.4 compare_reduce_fusion
  24.6 71.5 %all-gather.2.cloned.1.call-done = bf16[1024,4224]{1,0:T(8,128)(2,1)} async-done(((bf16[64,4224]{1,0:T(8,128)(2,1)}), bf16[1024,4224]{1,0:T(8,128)(2,1)}) %all-gather.2.cloned.1.call-update) | async-done | bytes 8650768 | tf_op jit(solution)/shard_map/all_gather | solution.py:90
  96.1 1.8 convert_compare_fusion.1
  97.9 0.3 eq.64
  98.3 0.3 eq.73
  98.6 0.3 compare_and_fusion.1
  98.9 0.2 copy.40
  99.1 0.2 copy.41
  99.2 0.9 compare_and_fusion
  100.1 0.2 copy.44
  100.3 0.2 copy.45
  100.4 0.1 copy.42
  100.6 0.1 copy.43
  100.7 0.1 copy.46
  100.8 0.1 copy.47
  101.0 0.5 fusion.14
  101.5 0.5 fusion.16
  102.0 5.8 %convolution_convert_fusion = bf16[16,64,4224]{2,1,0:T(8,128)(2,1)S(1)} fusion(bf16[16,64,4224]{2,1,0:T(8,128)(2,1)} %bitcast.88, pred[16,32,64]{2,1,0:T(8,128)(4,1)S(1)} %bitcast.94, pred[16,32,64]{2,1,0:T(8,128)(4,1)S(1)} %bitcast.97), kind=kOutput, calls=%fused_computation | convolution fusion | flops 558039040 | bytes 17367040 | tf_op jit(solution)/shard_map/gpi,gic->gpc/dot_general | solution.py:122
  107.8 0.6 fusion.57
  108.5 0.0 copy-start.4
  108.5 7.4 %fusion.2 = f32[512,2,512]{2,0,1:T(8,128)S(1)} fusion(bf16[4096,2,512]{2,1,0:T(2,128)(2,1)} %bitcast.100, bf16[512,4224]{1,0:T(8,128)(2,1)S(1)} %bitcast.93), kind=kOutput, calls=%fused_computation.5 | convolution fusion | flops 4294967296 | bytes 14680064 | tf_op jit(solution)/shard_map/rd,djf->rjf/dot_general | solution.py:8
  115.9 1.1 fusion.26
  117.0 0.0 copy-done.4
  117.0 0.0 copy-start.1
  117.0 2.3 %fusion.4 = f32[512,2,256]{2,0,1:T(8,128)S(1)} fusion(bf16[4096,2,256]{2,1,0:T(2,128)(2,1)S(1)} %bitcast.101, bf16[512,4224]{1,0:T(8,128)(2,1)S(1)} %bitcast.92), kind=kOutput, calls=%fused_computation.9 | convolution fusion | flops 2147483648 | bytes 9437184 | tf_op jit(solution)/shard_map/rd,djf->rjf/dot_general | solution.py:8
  119.4 0.9 fusion.43
  120.2 1.5 collective-permute-start.2
  121.7 0.6 collective-permute-start.1
  122.3 0.0 copy-done.1
  122.3 2.7 %fusion.28 = f32[512,2048]{1,0:T(8,128)} fusion(pred[]{:T(512)S(6)} %eq.61, bf16[1,512,2048]{2,1,0:T(8,128)(2,1)S(1)} %copy-done.1, f32[512,2,256]{2,0,1:T(8,128)S(1)} %fusion.4), kind=kOutput, calls=%fused_computation.43 | convolution fusion | flops 538181632 | bytes 7340033 | tf_op jit(solution)/shard_map/dot_general | solution.py:62
  124.9 0.0 copy-done.2
  124.9 4.3 %fusion.9 = f32[512,2048]{1,0:T(8,128)} fusion(bf16[512,512]{1,0:T(8,128)(2,1)} %fusion.26, pred[]{:T(512)S(6)} %eq.61, bf16[1,1024,2048]{2,1,0:T(8,128)(2,1)S(1)} %copy-done.2), kind=kOutput, calls=%fused_computation.17 | convolution fusion | flops 1074790400 | bytes 8912897 | tf_op jit(solution)/shard_map/dot_general | solution.py:62
  129.2 1.1 slice_convert_fusion
  130.3 0.5 fusion.55
  130.8 0.4 reshape.74
  131.2 0.4 reshape.68
  131.5 0.5 select_reduce_fusion.1
  132.1 0.0 collective-permute-done.2
  132.1 3.0 %subtract_convert_fusion = (bf16[512,2048]{1,0:T(8,128)(2,1)S(1)}, bf16[512,2048]{1,0:T(8,128)(2,1)S(1)}) fusion(f32[512,2048]{1,0:T(8,128)} %fusion.28, bf16[512,256]{1,0:T(8,128)(2,1)} %collective-permute-done.2, pred[]{:T(512)S(6)} %eq.61, bf16[1,512,2048]{2,1,0:T(8,128)(2,1)S(1)} %copy-done.1), kind=kOutput, calls=%fused_computation.12 | convolution fusion | flops 542638080 | bytes 10747905 | tf_op jit(solution)/shard_map/dot_general | solution.py:62
  135.1 1.3 fusion.60
  136.4 0.0 copy-start
  136.4 0.0 copy-start.3
  136.4 1.4 convolution_add_fusion
  137.8 2.3 %collective-permute-done.1 = bf16[512,512]{1,0:T(8,128)(2,1)S(1)} collective-permute-done((bf16[512,512]{1,0:T(8,128)(2,1)}, bf16[512,512]{1,0:T(8,128)(2,1)S(1)}, u32[]{:S(2)}, u32[]{:S(2)}) %collective-permute-start.1) | collective-permute-done | bytes 524320 | tf_op jit(solution)/shard_map/ppermute | solution.py:57
  140.1 0.0 copy-done
  140.1 0.0 copy-done.3
  140.2 1.4 add_convert_fusion
  141.6 1.3 fusion.59
  142.9 3.7 %fusion.1 = bf16[1024,2048]{1,0:T(8,128)(2,1)} fusion(f32[16,64,2048]{2,1,0:T(8,128)S(1)} %convolution_add_fusion, f32[16,64,2048]{2,1,0:T(8,128)S(1)} %fusion.59, f32[1024]{0:T(1024)S(1)} %get-tuple-element.10, f32[1024]{0:T(1024)S(1)} %get-tuple-element.9), kind=kLoop, calls=%fused_computation.3 | loop fusion | flops 8388608 | bytes 20979712 | tf_op jit(solution)/shard_map/convert_element_type | solution.py:148
  146.5 0.0 reduce-scatter.2.cloned.1.call-update
  146.6 71.0 %reduce-scatter.2.cloned.1.call-done = bf16[64,2048]{1,0:T(8,128)(2,1)} async-done(((bf16[1024,2048]{1,0:T(8,128)(2,1)}), bf16[64,2048]{1,0:T(8,128)(2,1)}) %reduce-scatter.2.cloned.1.call-update) | async-done | bytes 262160 | tf_op jit(solution)/shard_map/reduce_scatter | solution.py:148
  (2 shorter events, 0.0 us)
Async XLA Ops:
  6.5 89.6 %all-gather.2.cloned.1.call-start = ((), (), s32[]{:S(2)}) async-start(), calls=%async_computation.1 | async-start | bytes 9191424 | tf_op jit(solution)/shard_map/all_gather | solution.py:90
  6.5 9.5 %collective-permute-start = (bf16[64,2048]{1,0:T(8,128)(2,1)}, bf16[64,2048]{1,0:T(8,128)(2,1)S(1)}, u32[]{:S(2)}, u32[]{:S(2)}) collective-permute-start(bf16[64,2048]{1,0:T(8,128)(2,1)} %param.9), channel_id=1, source_target_pairs={{0,1},{1,0},{2,3},{3,2},{4,5},{5,4},{6,7},{7,6},{8,9},{9,8},{10,11... | collective-permute-start | bytes 786440 | tf_op jit(solution)/shard_map/ppermute | solution.py:46
  17.9 199.7 %reduce-scatter.2.cloned.1.call-start = ((), (), s32[]{:S(2)}) async-start(), calls=%async_computation.2 | async-start | bytes 4456448 | tf_op jit(solution)/shard_map/reduce_scatter | solution.py:148
  108.5 8.6 %copy-start.4 = (bf16[1,4096,2,256]{3,2,1,0:T(2,128)(2,1)S(1)}, bf16[1,4096,2,256]{3,2,1,0:T(2,128)(2,1)}, u32[]{:S(2)}) copy-start(bf16[1,4096,2,256]{3,2,1,0:T(2,128)(2,1)} %param.16) | copy-start | bytes 12582916
  117.0 5.2 %copy-start.1 = (bf16[1,512,2048]{2,1,0:T(8,128)(2,1)S(1)}, bf16[1,512,2048]{2,1,0:T(8,128)(2,1)}, u32[]{:S(2)}) copy-start(bf16[1,512,2048]{2,1,0:T(8,128)(2,1)} %param.17) | copy-start | bytes 6291460
  120.2 4.7 %copy-start.2 = (bf16[1,1024,2048]{2,1,0:T(8,128)(2,1)S(1)}, bf16[1,1024,2048]{2,1,0:T(8,128)(2,1)}, u32[]{:S(2)}) copy-start(bf16[1,1024,2048]{2,1,0:T(8,128)(2,1)} %param.15) | copy-start | bytes 12582916
  120.2 11.8 %collective-permute-start.2 = (bf16[512,256]{1,0:T(8,128)(2,1)}, bf16[512,256]{1,0:T(8,128)(2,1)}, u32[]{:S(2)}, u32[]{:S(2)}) collective-permute-start(bf16[512,256]{1,0:T(8,128)(2,1)} %fusion.43), channel_id=1, source_target_pairs={{0,1},{1,0},{2,3},{3,2},{4,5},{5,4},{6,7},{7,6},{8,9},{9,8},{10,11... | collective-permute-start | bytes 786440 | tf_op jit(solution)/shard_map/ppermute | solution.py:57
  121.7 18.4 %collective-permute-start.1 = (bf16[512,512]{1,0:T(8,128)(2,1)}, bf16[512,512]{1,0:T(8,128)(2,1)S(1)}, u32[]{:S(2)}, u32[]{:S(2)}) collective-permute-start(bf16[512,512]{1,0:T(8,128)(2,1)} %fusion.26), channel_id=1, source_target_pairs={{0,1},{1,0},{2,3},{3,2},{4,5},{5,4},{6,7},{7,6},{8,9},{9,8},{10,11... | collective-permute-start | bytes 1572872 | tf_op jit(solution)/shard_map/ppermute | solution.py:57
  136.4 3.8 %copy-start = (f32[512,2048]{1,0:T(8,128)S(1)}, f32[512,2048]{1,0:T(8,128)}, u32[]{:S(2)}) copy-start(f32[512,2048]{1,0:T(8,128)} %fusion.9) | copy-start | bytes 12582916
  136.4 3.7 %copy-start.3 = (bf16[1,1024,2048]{2,1,0:T(8,128)(2,1)S(1)}, bf16[1,1024,2048]{2,1,0:T(8,128)(2,1)}, u32[]{:S(2)}) copy-start(bf16[1,1024,2048]{2,1,0:T(8,128)(2,1)} %param.15) | copy-start | bytes 12582916
Sparse Core Ops, SparseCore 0:
  18.0 78.0 all-gather.1
  146.7 70.8 reduce-scatter.1
